TPU v7x, 32 devices: a whole 2x2x4 slice. The times are simulated.
32 devices in a mesh: dom: 8 (over z, core), cls: 4 (over y, x).
Axes of the slice: x: 2, y: 2, z: 4, core: 2. Of those that a mesh axis runs over, the one named last changes fastest.
Arguments:
- particles: bfloat16 [8192, 9216], P('dom'), may hold values from -6 to 6
- defocus: float32 [8192], P('dom'), may hold values from 0.5 to 2
- inv_noise: float32 [4608], replicated, may hold values from 0.25 to 4
- references: bfloat16 [96, 8, 9216], P(('cls', 'dom')), may hold values from -0.125 to 0.125
- part_class: int32 [8192], P('dom'), may hold values from 0 to 95, as said below
- part_rot: int32 [8192], P('dom'), may hold values from 0 to 7
- counts: int32 [96], replicated, may hold values from 0 to 399
Outputs:
- best_score: float32 [8192], P('dom')
- class_images: float32 [96, 8, 9216], P(('cls', 'dom'))
Inputs may be any that keep to these rules, and one draw needn't show every extreme that they name: `part_class`: block o of classes is o * 3 to o * 3 + 2. In each aligned block of 1024 particles at most 96 have their class in any one block of classes; in every draw one block of classes receives exactly 96 from every block of particles.
All inputs are finite; a program needn't handle non-finite values.
Results may differ from a plain program's by a relative error of at most 0.0044.
Values may be sent and summed in bfloat16 or wider, within the bound.
No kernel may reach another device: no remote copies, remote signals or barrier semaphores. Data moves between devices by JAX's collectives and lax.ppermute only.
A program may use at most 192 MiB of HBM per device.

v0:
```python
import jax
import jax.numpy as jnp
from jax import lax
from jax.sharding import PartitionSpec as P


def frequencies(pixels):
    positions = jnp.arange(pixels, dtype=jnp.int32)
    row_offset = (positions // 64 - pixels // 128).astype(jnp.float32)
    column = (positions % 64).astype(jnp.float32)
    return (row_offset * row_offset + column * column) / 4096.0


def contrast(defocus, inv_noise):
    phase_shift = 12.0 * defocus[:, None] * frequencies(inv_noise.shape[0])[None, :]
    return -0.995 * jnp.sin(phase_shift) - 0.1 * jnp.cos(phase_shift)


def power_spectrum(images, pixels):
    real_part = images[..., :pixels].astype(jnp.float32)
    imag_part = images[..., pixels:].astype(jnp.float32)
    return (real_part * real_part + imag_part * imag_part).astype(jnp.bfloat16)


def on_device(particles, defocus, inv_noise, references, part_class, part_rot, counts):
    local_rows = particles.shape[0]
    pixels = inv_noise.shape[0]
    owned = references.shape[0]
    rotations = references.shape[1]
    dom_size = lax.axis_size("dom")
    cls_size = lax.axis_size("cls")
    cls_index = lax.axis_index("cls")
    contrast_rows = contrast(defocus, inv_noise)
    factor = inv_noise[None, :] * contrast_rows
    weighted = (particles.astype(jnp.float32) * jnp.concatenate([factor, factor], axis=1)).astype(
        jnp.bfloat16
    )
    power_weight = (factor * contrast_rows).astype(jnp.bfloat16)
    class_total = counts.shape[0]
    log_prior = jnp.log(
        (counts + 1).astype(jnp.float32) / (jnp.sum(counts) + class_total).astype(jnp.float32)
    )
    block_first = cls_index * (dom_size * owned)
    images = lax.all_gather(references, "dom", axis=0, tiled=True)
    power = power_spectrum(images, pixels)
    held = images.shape[0]
    flat_images = images.reshape(held * rotations, 2 * pixels)
    flat_power = power.reshape(held * rotations, pixels)
    cross_term = lax.dot_general(
        flat_images, weighted, (((1,), (1,)), ((), ())), preferred_element_type=jnp.float32
    )
    power_term = lax.dot_general(
        flat_power, power_weight, (((1,), (1,)), ((), ())), preferred_element_type=jnp.float32
    )
    class_prior = lax.dynamic_slice_in_dim(log_prior, block_first, held)
    score = cross_term - 0.5 * power_term + jnp.repeat(class_prior, rotations)[:, None]
    local_best = jnp.max(score, axis=0)
    best_score = lax.pmax(local_best, "cls")
    capacity = max(2, 3 * local_rows // (dom_size * cls_size))
    owner_ids = part_class // owned
    target = owner_ids % dom_size
    is_mine = owner_ids // dom_size == cls_index
    pose_code = part_class % owned * rotations + part_rot + 1
    dest_hits = (
        (target[:, None] == jnp.arange(dom_size, dtype=jnp.int32)[None, :]) & is_mine[:, None]
    ).astype(jnp.int32)
    earlier = jnp.cumsum(dest_hits, axis=0) - dest_hits
    rank_within = jnp.sum(earlier * dest_hits, axis=1)
    slot_count = dom_size * capacity
    slot_of = jnp.where(is_mine, target * capacity + rank_within, slot_count)
    source_row = (
        jnp.full((slot_count + 1,), local_rows, jnp.int32)
        .at[slot_of]
        .set(jnp.arange(local_rows, dtype=jnp.int32))[:slot_count]
    )
    filled = source_row < local_rows
    safe_row = jnp.minimum(source_row, local_rows - 1)
    empty_value = jnp.zeros((), jnp.bfloat16)
    send_weighted = jnp.where(filled[:, None], jnp.take(weighted, safe_row, axis=0), empty_value)
    send_code = jnp.where(filled, jnp.take(pose_code, safe_row), 0).astype(jnp.bfloat16)
    pose_ids = jnp.arange(owned * rotations, dtype=jnp.int32) + 1
    send_power = jnp.where(filled[:, None], jnp.take(power_weight, safe_row, axis=0), empty_value)
    payload = jnp.concatenate([send_weighted, send_power], axis=1).reshape(
        dom_size, capacity, 3 * pixels
    )
    arrived, arrived_code = (
        lax.all_to_all(payload, "dom", split_axis=0, concat_axis=0, tiled=True),
        lax.all_to_all(
            send_code.reshape(dom_size, capacity), "dom", split_axis=0, concat_axis=0, tiled=True
        ),
    )
    arrived = arrived.reshape(slot_count, 3 * pixels)
    codes = arrived_code.reshape(slot_count).astype(jnp.int32)
    selector = (pose_ids[:, None] == codes[None, :]).astype(jnp.bfloat16)
    sums = jnp.dot(selector, arrived, preferred_element_type=jnp.float32)
    numerator = sums[:, : 2 * pixels]
    denominator = sums[:, 2 * pixels :]
    images = numerator / (jnp.concatenate([denominator, denominator], axis=1) + 1.0)
    return (best_score, images.reshape(owned, rotations, 2 * pixels))


def solution(mesh):
    placed = (P("dom", None), P("dom"), P(), P(("cls", "dom"), None, None), P("dom"), P("dom"), P())
    return jax.shard_map(
        on_device,
        mesh=mesh,
        in_specs=placed,
        out_specs=(P("dom"), P(("cls", "dom"), None, None)),
        check_vma=False,
    )
```

profile of v0, /device:TPU:0, one launch (start us, length us, event | category | flops | bytes accessed | tf_op | source)
XLA Modules:
  0.0 712.4 jit_solution(14085966261514725436)
XLA Ops:
  7.2 0.7 fusion.68
  7.9 0.7 fusion.55
  8.6 0.7 fusion.58
  9.3 2.3 reduce-window.6
  12.2 0.7 compare_select_fusion.3
  12.9 4.3 scatter_custom_fusion
  17.3 3.2 gather_fusion
  21.3 6.3 all-to-all-start
  28.5 72.0 %fusion.6 = (bf16[1024,4608]{1,0:T(8,128)(2,1)}, f32[1024,4608]{1,0:T(8,128)}) fusion(f32[4608]{0:T(1024)S(1)} %fusion.51, f32[1024]{0:T(1024)S(1)} %broadcast_multiply_fusion, f32[4608]{0:T(1024)} %param.9), kind=kLoop, calls=%fused_computation.14 | loop fusion | flops 33030144 | bytes 28352512 | tf_op jit(solution)/shard_map/convert_element_type | solution.py:38
  100.5 18.4 %gather_fusion.2 = bf16[768,4608]{1,0:T(8,128)(2,1)} fusion(bf16[1024,4608]{1,0:T(8,128)(2,1)} %get-tuple-element.2, s32[1024]{0:T(1024)S(1)} %pad_clamp_fusion), kind=kCustom, calls=%fused_computation.2 | custom fusion | bytes 14158848 | tf_op jit(solution)/shard_map/jit(_take)/gather | solution.py:82
  118.8 25.5 %fusion = bf16[1024,9216]{1,0:T(8,128)(2,1)} fusion(f32[1024,4608]{1,0:T(8,128)} %get-tuple-element.3, bf16[1024,9216]{1,0:T(8,128)(2,1)} %param.7), kind=kLoop, calls=%fused_computation.5 | loop fusion | flops 37748736 | bytes 56623104 | tf_op jit(solution)/shard_map/convert_element_type | solution.py:35
  144.3 33.5 %gather_fusion.1 = bf16[768,9216]{1,0:T(8,128)(2,1)} fusion(bf16[1024,9216]{1,0:T(8,128)(2,1)} %fusion, s32[1024]{0:T(1024)S(1)} %pad_clamp_fusion), kind=kCustom, calls=%fused_computation.1 | custom fusion | bytes 28314624 | tf_op jit(solution)/shard_map/jit(_take)/gather | solution.py:79
  177.8 3.9 select_select_fusion.1
  181.7 7.1 select_select_fusion
  188.8 12.7 %pad_maximum_fusion = bf16[8,96,13824]{2,1,0:T(8,128)(2,1)} fusion(bf16[8,96,4608]{2,1,0:T(8,128)(2,1)S(1)} %select_select_fusion.1, bf16[8,96,9216]{2,1,0:T(8,128)(2,1)S(1)} %select_select_fusion), kind=kLoop, calls=%fused_computation.8 | loop fusion | flops 42467328 | bytes 42467328 | tf_op jit(solution)/shard_map/concatenate | solution.py:83
  201.5 6.3 all-to-all-start.1
  210.2 72.9 %all-gather.2.cloned.1.call-done = bf16[24,8,9216]{2,1,0:T(8,128)(2,1)} async-done(((bf16[3,8,9216]{2,1,0:T(8,128)(2,1)}), bf16[24,8,9216]{2,1,0:T(8,128)(2,1)}) %all-gather.2.cloned.1.call-update) | async-done | bytes 3538960 | tf_op jit(solution)/shard_map/all_gather | solution.py:44
  283.0 2.8 fusion.75
  285.9 71.8 %fusion.14 = f32[192,1024]{1,0:T(8,128)S(1)} fusion(f32[4608]{0:T(1024)S(1)} %fusion.51, f32[1024]{0:T(1024)S(1)} %broadcast_multiply_fusion, f32[4608]{0:T(1024)S(1)} %copy-done.1, bf16[192,4608]{1,0:T(8,128)(2,1)S(1)} %fusion.75), kind=kOutput, calls=%fused_computation.24 | convolution fusion | flops 1845166080 | bytes 2596864 | tf_op jit(solution)/shard_map/dot_general | solution.py:52
  357.7 6.3 fusion.26
  364.0 10.4 %pmax.7 = f32[1024]{0:T(1024)} all-reduce(f32[1024]{0:T(1024)S(1)} %fusion.26), channel_id=1, replica_groups=mesh['dom'=8,'cls'=4] {'cls'}, use_global_device_ids=true, to_apply=%region_2.3 | all-reduce | flops 1024 | bytes 8192 | tf_op jit(solution)/shard_map/pmax | solution.py:58
  374.5 320.9 %all-to-all-done.1 = bf16[8,96,13824]{2,1,0:T(8,128)(2,1)} async-done(((bf16[8,96,13824]{2,1,0:T(8,128)(2,1)}), bf16[8,96,13824]{2,1,0:T(8,128)(2,1)}, u32[]{:S(2)}, u32[]{:S(2)}) %all-to-all-start.1) | async-done | bytes 21233696 | tf_op jit(solution)/shard_map/all_to_all | solution.py:87
  695.4 8.6 %fusion.31 = f32[24,13824]{1,0:T(8,128)S(1)} fusion(bf16[768,13824]{1,0:T(8,128)(2,1)} %bitcast.8, s32[768]{0:T(1024)S(1)} %reshape.180, s32[24]{0:T(128)S(1)} %iota_add_fusion), kind=kOutput, calls=%fused_computation.32 | convolution fusion | flops 509626368 | bytes 22563936 | tf_op jit(solution)/shard_map/dot_general | solution.py:95
  704.0 1.1 fusion.29
  (48 shorter events, 4.1 us)
Async XLA Ops:
  21.3 180.2 %all-to-all-start = ((bf16[8,1,96]{2,1,0:T(2,128)(2,1)}), bf16[8,1,96]{2,1,0:T(2,128)(2,1)S(1)}, u32[]{:S(2)}, u32[]{:S(2)}) async-start(bf16[8,1,96]{2,1,0:T(2,128)(2,1)} %copy.9), calls=%async_computation | async-start | bytes 8192 | tf_op jit(solution)/shard_map/all_to_all | solution.py:88
  201.5 7.0 copy-start.2
  201.5 84.3 %copy-start.1 = (f32[4608]{0:T(1024)S(1)}, f32[4608]{0:T(1024)}, u32[]{:S(2)}) copy-start(f32[4608]{0:T(1024)} %param.9) | copy-start | bytes 55300
  201.5 493.9 %all-to-all-start.1 = ((bf16[8,96,13824]{2,1,0:T(8,128)(2,1)}), bf16[8,96,13824]{2,1,0:T(8,128)(2,1)}, u32[]{:S(2)}, u32[]{:S(2)}) async-start(bf16[8,96,13824]{2,1,0:T(8,128)(2,1)} %pad_maximum_fusion), calls=%async_computation.1 | async-start | bytes 42467328 | tf_op jit(solution)/shard_map/all_to_all | solution.py:87
  207.8 75.3 %all-gather.2.cloned.1.call-start = ((), (), s32[]{:S(2)}) async-start(), calls=%async_computation.2 | async-start | bytes 3981312 | tf_op jit(solution)/shard_map/all_gather | solution.py:44
  283.0 74.6 %slice-start = ((s8[18874368]{0:T(1024)(128)(4,1)}), s8[4194304]{0:T(1024)(128)(4,1)S(1)}, s32[]{:S(2)}) async-start(s8[18874368]{0:T(1024)(128)(4,1)} %bitcast.59), calls=%async_computation.3 | async-start | bytes 8388608
  285.8 71.8 %slice-start.1 = ((s8[18874368]{0:T(1024)(128)(4,1)}), s8[4194304]{0:T(1024)(128)(4,1)S(1)}, s32[]{:S(2)}) async-start(s8[18874368]{0:T(1024)(128)(4,1)} %bitcast.59), calls=%async_computation.4 | async-start | bytes 8388608
  285.9 71.8 %slice-start.2 = ((s8[18874368]{0:T(1024)(128)(4,1)}), s8[4194304]{0:T(1024)(128)(4,1)S(1)}, s32[]{:S(2)}) async-start(s8[18874368]{0:T(1024)(128)(4,1)} %bitcast.59), calls=%async_computation.5 | async-start | bytes 8388608
  285.9 71.8 %slice-start.3 = ((s8[18874368]{0:T(1024)(128)(4,1)}), s8[4194304]{0:T(1024)(128)(4,1)S(1)}, s32[]{:S(2)}) async-start(s8[18874368]{0:T(1024)(128)(4,1)} %bitcast.59), calls=%async_computation.6 | async-start | bytes 8388608
  285.9 71.8 %slice-start.4 = ((s8[18874368]{0:T(1024)(128)(4,1)}), s8[2097152]{0:T(1024)(128)(4,1)S(1)}, s32[]{:S(2)}) async-start(s8[18874368]{0:T(1024)(128)(4,1)} %bitcast.59), calls=%async_computation.7 | async-start | bytes 4194304
  285.9 71.8 %copy-start = (bf16[24,8,9216]{2,1,0:T(8,128)(2,1)S(1)}, bf16[24,8,9216]{2,1,0:T(8,128)(2,1)}, u32[]{:S(2)}) copy-start(bf16[24,8,9216]{2,1,0:T(8,128)(2,1)} %all-gather.2.cloned.1.call-done) | copy-start | bytes 10616836
Sparse Core Ops, SparseCore 0:
  210.3 72.7 all-gather.1
where the time goes:
time: 722 us; the launch traced here: 712 us
  waiting for transfers between devices  394 us (55%)
  other arithmetic  132 us (18%)
  matrix products  86.7 us (12%)
  local copies, waits for them, and re-layouts  61 us (8%)
  between operations  15.4 us (2%)
  starting transfers between devices  12.6 us (2%)
  blocking collectives  10.4 us (1%)
    all_to_all x1, waiting for transfers between devices, on_device(): lax.all_to_all(payload, 'dom', split_axis=0, concat_axis=0, tiled=True)  321 us
    all_gather x1, waiting for transfers between devices, on_device(): images = lax.all_gather(references, 'dom', axis=0, tiled=True)  72.9 us
    convert_element_type x1, other arithmetic, on_device(): power_weight = (factor * contrast_rows).astype(jnp.bfloat16)  72 us
    dot_general x1, matrix products, on_device(): lax.dot_general(flat_power, power_weight, (((1,), (1,)), ((), ())), prefe...  71.8 us
    gather x1, local copies, waits for them, and re-layouts, on_device(): jnp.take(weighted, safe_row, axis=0)  33.5 us
    convert_element_type x1, other arithmetic, on_device(): (particles.astype(jnp.float32) * jnp.concatenate([factor, factor], axis=1...  25.5 us
    gather x1, local copies, waits for them, and re-layouts, on_device(): jnp.take(power_weight, safe_row, axis=0)  18.4 us
  transfers between devices with their start and end apart: 3, of which 2 were waited for; matrix products, arithmetic and copies ran while one was open for 36% of the time, Pallas kernels for 0%

commit v1 on v0

v1 whole, which is shorter than its diff:
```python
import math

import jax
import jax.numpy as jnp
from jax import lax
from jax.experimental import pallas as pl
from jax.sharding import PartitionSpec as P

AMPLITUDE = math.hypot(0.995, 0.1)
PHASE = math.atan2(0.1, 0.995)
ROW_BLOCK = 64


def frequencies(pixels):
    positions = jnp.arange(pixels, dtype=jnp.int32)
    row_offset = (positions // 64 - pixels // 128).astype(jnp.float32)
    column = (positions % 64).astype(jnp.float32)
    return (row_offset * row_offset + column * column) / 4096.0


def weights_kernel(defocus_ref, freq_ref, noise_ref, particles_ref, out_ref):
    pixels = freq_ref.shape[1]
    phase_shift = (12.0 * defocus_ref[...]) * freq_ref[...]
    contrast_rows = -AMPLITUDE * jnp.sin(phase_shift + PHASE)
    factor = noise_ref[...] * contrast_rows
    real_part = particles_ref[:, :pixels].astype(jnp.float32)
    imag_part = particles_ref[:, pixels:].astype(jnp.float32)
    out_ref[:, :pixels] = (real_part * factor).astype(jnp.bfloat16)
    out_ref[:, pixels : 2 * pixels] = (imag_part * factor).astype(jnp.bfloat16)
    out_ref[:, 2 * pixels :] = (factor * contrast_rows).astype(jnp.bfloat16)


def weighted_rows(particles, defocus, inv_noise):
    rows = particles.shape[0]
    pixels = inv_noise.shape[0]
    block = min(ROW_BLOCK, rows)
    return pl.pallas_call(
        weights_kernel,
        grid=(rows // block,),
        in_specs=[
            pl.BlockSpec((block, 1), lambda i: (i, 0)),
            pl.BlockSpec((1, pixels), lambda i: (0, 0)),
            pl.BlockSpec((1, pixels), lambda i: (0, 0)),
            pl.BlockSpec((block, 2 * pixels), lambda i: (i, 0)),
        ],
        out_specs=pl.BlockSpec((block, 3 * pixels), lambda i: (i, 0)),
        out_shape=jax.ShapeDtypeStruct((rows, 3 * pixels), jnp.bfloat16),
    )(defocus[:, None], frequencies(pixels)[None, :], inv_noise[None, :], particles)


def on_device(particles, defocus, inv_noise, references, part_class, part_rot, counts):
    pixels = inv_noise.shape[0]
    owned = references.shape[0]
    rotations = references.shape[1]
    dom_size = lax.axis_size("dom")
    cls_index = lax.axis_index("cls")
    block_classes = dom_size * owned
    block_first = cls_index * block_classes

    images = lax.all_gather(references, "dom", axis=0, tiled=True)
    flat_images = images.reshape(block_classes * rotations, 2 * pixels)
    real_part = flat_images[:, :pixels].astype(jnp.float32)
    imag_part = flat_images[:, pixels:].astype(jnp.float32)
    power = (real_part * real_part + imag_part * imag_part).astype(jnp.bfloat16)
    templates = jnp.concatenate([flat_images, power * jnp.bfloat16(-0.5)], axis=1)

    payload = weighted_rows(particles, defocus, inv_noise)

    class_total = counts.shape[0]
    log_prior = jnp.log(
        (counts + 1).astype(jnp.float32) / (jnp.sum(counts) + class_total).astype(jnp.float32)
    )
    class_prior = lax.dynamic_slice_in_dim(log_prior, block_first, block_classes)
    score = lax.dot_general(
        payload, templates, (((1,), (1,)), ((), ())), preferred_element_type=jnp.float32
    )
    score = score + jnp.repeat(class_prior, rotations)[None, :]
    best_score = lax.pmax(jnp.max(score, axis=1), "cls")

    local_class = part_class - block_first
    in_block = (local_class >= 0) & (local_class < block_classes)
    pose = jnp.where(in_block, local_class * rotations + part_rot, -1)
    poses = jnp.arange(block_classes * rotations, dtype=jnp.int32)
    selector = (poses[:, None] == pose[None, :]).astype(jnp.bfloat16)
    partial = jnp.dot(selector, payload, preferred_element_type=jnp.float32)
    sums = lax.psum_scatter(partial, "dom", scatter_dimension=0, tiled=True)
    numerator = sums[:, : 2 * pixels]
    denominator = sums[:, 2 * pixels :]
    class_images = numerator / (jnp.concatenate([denominator, denominator], axis=1) + 1.0)
    return best_score, class_images.reshape(owned, rotations, 2 * pixels)


def solution(mesh):
    placed = (P("dom", None), P("dom"), P(), P(("cls", "dom"), None, None), P("dom"), P("dom"), P())
    return jax.shard_map(
        on_device,
        mesh=mesh,
        in_specs=placed,
        out_specs=(P("dom"), P(("cls", "dom"), None, None)),
        check_vma=False,
    )
```

time: 722 us -> 233 us (0.32); the launches traced: 712 us -> 232 us
  waiting for transfers between devices: 394 us -> 75.9 us
  other arithmetic: 132 us -> 7.67 us
  Pallas kernels: 0 us -> 82.4 us
  local copies, waits for them, and re-layouts: 61 us -> 4.98 us
  matrix products: 86.7 us -> 34.4 us
  starting transfers between devices: 12.6 us -> 0.08 us
    all_to_all x2 -> x0, waiting for transfers between devices: 321 us -> none  [the longest x1 321 us: on_device(): lax.all_to_all(payload, 'dom', split_axis=0, concat_axis=0, tiled=True)]
    convert_element_type x5 -> x0, other arithmetic: 97.5 us -> none  [the longest x1 72 us: on_device(): power_weight = (factor * contrast_rows).astype(jnp.bfloat16)]
    pallas_call x0 -> x1, Pallas kernels: none -> 82.4 us  [weighted_rows(): pl.pallas_call(weights_kernel, grid=(rows // block,), in_specs=[pl.BlockS...]
    reduce_scatter x0 -> x1, waiting for transfers between devices: none -> 75.2 us  [on_device(): sums = lax.psum_scatter(partial, 'dom', scatter_dimension=0, tiled=True)]
    all_gather x1, waiting for transfers between devices: 72.9 us -> 0.02 us  [on_device(): images = lax.all_gather(references, 'dom', axis=0, tiled=True)]
    gather x4 -> x0, local copies, waits for them, and re-layouts: 55.1 us -> none  [the longest x1 33.5 us: on_device(): jnp.take(weighted, safe_row, axis=0)]
    dot_general x3 -> x2, matrix products: 86.7 us -> 34.4 us  [the longest x1 19.8 us: on_device(): lax.dot_general(payload, templates, (((1,), (1,)), ((), ())), preferred_e...]
    concatenate x1 -> x0, other arithmetic: 12.7 us -> none  [on_device(): jnp.concatenate([send_weighted, send_power], axis=1)]
  transfers between devices with their start and end apart: 3 -> 2, of which waited for: 2 -> 1; matrix products, arithmetic and copies ran while one was open for 36% -> 19% of each run, Pallas kernels for 0% -> 35%
where the time goes in v1:
time: 233 us; the launch traced here: 232 us
  Pallas kernels  82.4 us (35%)
  waiting for transfers between devices  75.9 us (33%)
  matrix products  34.4 us (15%)
  between operations  14.7 us (6%)
  blocking collectives  12.1 us (5%)
  other arithmetic  7.67 us (3%)
  local copies, waits for them, and re-layouts  4.98 us (2%)
    pallas_call x1, Pallas kernels, weighted_rows(): pl.pallas_call(weights_kernel, grid=(rows // block,), in_specs=[pl.BlockS...  82.4 us
    reduce_scatter x1, waiting for transfers between devices, on_device(): sums = lax.psum_scatter(partial, 'dom', scatter_dimension=0, tiled=True)  75.2 us
    dot_general x1, matrix products, on_device(): lax.dot_general(payload, templates, (((1,), (1,)), ((), ())), preferred_e...  19.8 us
    dot_general x1, matrix products, on_device(): partial = jnp.dot(selector, payload, preferred_element_type=jnp.float32)  14.6 us
    pmax x1, blocking collectives, on_device(): best_score = lax.pmax(jnp.max(score, axis=1), 'cls')  12.1 us
  transfers between devices with their start and end apart: 2, of which 1 were waited for; matrix products, arithmetic and copies ran while one was open for 19% of the time, Pallas kernels for 35%

profile of v1, /device:TPU:0, one launch (start us, length us, event | category | flops | bytes accessed | tf_op | source)
XLA Modules:
  0.0 232.3 jit_solution(18168911096147298346)
XLA Ops:
  7.2 0.0 all-gather.2.cloned.1.call-start
  7.2 0.7 all-gather.2.cloned.1.call-update
  7.9 0.0 reduce-scatter.2.cloned.1.call-start
  7.9 1.3 broadcast_in_dim.17.noise_ref
  9.3 1.7 copy.10.defocus_ref
  11.0 0.7 fusion.17.freq_ref
  11.7 82.4 %shard_map.86 = bf16[1024,13824]{1,0:T(8,128)(2,1)} custom-call(f32[1024,1]{1,0:T(8,128)} %copy.10.defocus_ref, f32[1,4608]{1,0:T(1,128)} %fusion.17.freq_ref, f32[1,4608]{1,0:T(1,128)} %broadcast_in_dim.17.noise_ref, bf16[1024,9216]{1,0:T(8,128)(2,1)} %particles_ref.1), custom_call_target="tpu_custom_call" | custom-call | tf_op jit(solution)/shard_map/pallas_call | solution.py:37
  94.1 0.0 copy-done.1
  94.1 0.0 copy-done.2
  94.1 14.6 %fusion.12 = f32[192,13824]{1,0:T(8,128)} fusion(bf16[1024,13824]{1,0:T(8,128)(2,1)} %shard_map.86, s32[1024]{0:T(1024)S(1)} %add_select_fusion), kind=kOutput, calls=%fused_computation.12 | convolution fusion | flops 5436014592 | bytes 38932480 | tf_op jit(solution)/shard_map/dot_general | solution.py:85
  108.7 0.0 reduce-scatter.2.cloned.1.call-update
  108.7 0.6 copy-done.3
  109.3 0.6 reduce_sum.9
  110.6 0.1 dynamic_slice.3
  110.7 0.1 broadcast_in_dim.18
  110.8 0.1 add.82
  110.9 0.0 all-gather.2.cloned.1.call-done
  110.9 0.0 copy-start
  110.9 4.2 %fusion.4 = bf16[192,4608]{1,0:T(8,128)(2,1)} fusion(bf16[192,9216]{1,0:T(8,128)(2,1)} %bitcast.6), kind=kLoop, calls=%fused_computation.5 | loop fusion | flops 6193152 | bytes 5308416 | tf_op jit(solution)/shard_map/mul | solution.py:65
  115.1 19.8 %fusion.8 = f32[1024]{0:T(1024)S(1)} fusion(bf16[1024,13824]{1,0:T(8,128)(2,1)} %shard_map.86, bf16[192,4608]{1,0:T(8,128)(2,1)} %fusion.4, bf16[192,9216]{1,0:T(8,128)(2,1)S(1)} %bitcast.7, f32[192]{0:T(256)S(1)} %add.82), kind=kOutput, calls=%fused_computation.7 | convolution fusion | flops 5446827008 | bytes 33624832 | tf_op jit(solution)/shard_map/dot_general | solution.py:74
  134.9 12.1 %pmax.7 = f32[1024]{0:T(1024)} all-reduce(f32[1024]{0:T(1024)S(1)} %fusion.8), channel_id=1, replica_groups=mesh['dom'=8,'cls'=4] {'cls'}, use_global_device_ids=true, to_apply=%region_2.3 | all-reduce | flops 1024 | bytes 8192 | tf_op jit(solution)/shard_map/pmax | solution.py:78
  147.0 75.2 %reduce-scatter.2.cloned.1.call-done = f32[24,13824]{1,0:T(8,128)} async-done(((f32[192,13824]{1,0:T(8,128)}), f32[24,13824]{1,0:T(8,128)}) %reduce-scatter.2.cloned.1.call-update) | async-done | bytes 1327120 | tf_op jit(solution)/shard_map/reduce_scatter | solution.py:86
  222.2 1.0 slice.19
  223.2 2.2 fusion.11
  (6 shorter events, 0.0 us)
Async XLA Ops:
  7.2 103.7 %all-gather.2.cloned.1.call-start = ((), (), s32[]{:S(2)}) async-start(), calls=%async_computation.1 | async-start | bytes 3981312 | tf_op jit(solution)/shard_map/all_gather | solution.py:60
  7.9 214.3 %reduce-scatter.2.cloned.1.call-start = ((), (), s32[]{:S(2)}) async-start(), calls=%async_computation.2 | async-start | bytes 11943936 | tf_op jit(solution)/shard_map/reduce_scatter | solution.py:86
  11.6 82.4 %copy-start.1 = (s32[1024]{0:T(1024)S(1)}, s32[1024]{0:T(1024)}, u32[]{:S(2)}) copy-start(s32[1024]{0:T(1024)} %param.12) | copy-start | bytes 12292
  11.7 82.4 %copy-start.2 = (s32[1024]{0:T(1024)S(1)}, s32[1024]{0:T(1024)}, u32[]{:S(2)}) copy-start(s32[1024]{0:T(1024)} %param.11) | copy-start | bytes 12292
  108.7 0.7 copy-start.3
  110.9 4.2 %copy-start = (bf16[24,8,9216]{2,1,0:T(8,128)(2,1)S(1)}, bf16[24,8,9216]{2,1,0:T(8,128)(2,1)}, u32[]{:S(2)}) copy-start(bf16[24,8,9216]{2,1,0:T(8,128)(2,1)} %all-gather.2.cloned.1.call-done) | copy-start | bytes 10616836
Sparse Core Ops, SparseCore 0:
  9.6 44.2 all-gather.1
  108.8 113.3 reduce-scatter.1

commit v2 on v1

--- a/solution.py
+++ b/solution.py
@@ -8,44 +8,76 @@
 
 AMPLITUDE = math.hypot(0.995, 0.1)
 PHASE = math.atan2(0.1, 0.995)
-ROW_BLOCK = 64
+ROW_BLOCK = 128
 
 
-def frequencies(pixels):
-    positions = jnp.arange(pixels, dtype=jnp.int32)
-    row_offset = (positions // 64 - pixels // 128).astype(jnp.float32)
-    column = (positions % 64).astype(jnp.float32)
-    return (row_offset * row_offset + column * column) / 4096.0
+def split_pieces(values, width):
+    pieces = []
+    rest = values
+    for _ in range(3):
+        piece = lax.reduce_precision(rest, exponent_bits=8, mantissa_bits=7)
+        pieces.append(piece.astype(jnp.bfloat16))
+        rest = rest - piece
+    joined = jnp.concatenate(pieces, axis=1)
+    return jnp.pad(joined, ((0, 0), (0, width - joined.shape[1])))
 
 
-def weights_kernel(defocus_ref, freq_ref, noise_ref, particles_ref, out_ref):
-    pixels = freq_ref.shape[1]
-    phase_shift = (12.0 * defocus_ref[...]) * freq_ref[...]
-    contrast_rows = -AMPLITUDE * jnp.sin(phase_shift + PHASE)
-    factor = noise_ref[...] * contrast_rows
-    real_part = particles_ref[:, :pixels].astype(jnp.float32)
-    imag_part = particles_ref[:, pixels:].astype(jnp.float32)
-    out_ref[:, :pixels] = (real_part * factor).astype(jnp.bfloat16)
-    out_ref[:, pixels : 2 * pixels] = (imag_part * factor).astype(jnp.bfloat16)
-    out_ref[:, 2 * pixels :] = (factor * contrast_rows).astype(jnp.bfloat16)
+def contrast_tables(defocus, pixels):
+    groups = pixels // 64
+    scaled = 12.0 * defocus
+    row_offset = (jnp.arange(groups, dtype=jnp.int32) - pixels // 128).astype(jnp.float32)
+    row_angle = scaled[:, None] * (row_offset * row_offset / 4096.0)[None, :]
+    column = (jnp.arange(128, dtype=jnp.int32) % 64).astype(jnp.float32)
+    column_angle = scaled[:, None] * (column * column / 4096.0)[None, :] + PHASE
+    width = -(-3 * groups // 128) * 128
+    row_sin = split_pieces(-AMPLITUDE * jnp.sin(row_angle), width)
+    row_cos = split_pieces(-AMPLITUDE * jnp.cos(row_angle), width)
+    slot = jnp.arange(width, dtype=jnp.int32)[:, None]
+    group_of = (jnp.arange(pixels, dtype=jnp.int32) // 64)[None, :]
+    expand = ((slot < 3 * groups) & (slot % groups == group_of)).astype(jnp.bfloat16)
+    return row_sin, row_cos, expand, jnp.cos(column_angle), jnp.sin(column_angle)
+
+
+def weights_kernel(row_sin_ref, row_cos_ref, expand_ref, col_cos_ref, col_sin_ref, noise_ref, particles_ref, out_ref):
+    pixels = noise_ref.shape[1]
+    row_sin = jnp.dot(row_sin_ref[...], expand_ref[...], preferred_element_type=jnp.float32)
+    row_cos = jnp.dot(row_cos_ref[...], expand_ref[...], preferred_element_type=jnp.float32)
+    col_cos = col_cos_ref[...]
+    col_sin = col_sin_ref[...]
+    for tile in range(pixels // 128):
+        lanes = slice(tile * 128, (tile + 1) * 128)
+        contrast_rows = row_sin[:, lanes] * col_cos + row_cos[:, lanes] * col_sin
+        factor = noise_ref[:, lanes] * contrast_rows
+        real_part = particles_ref[:, lanes].astype(jnp.float32)
+        imag_part = particles_ref[:, pixels + tile * 128 : pixels + (tile + 1) * 128].astype(jnp.float32)
+        out_ref[:, lanes] = (real_part * factor).astype(jnp.bfloat16)
+        out_ref[:, pixels + tile * 128 : pixels + (tile + 1) * 128] = (imag_part * factor).astype(jnp.bfloat16)
+        out_ref[:, 2 * pixels + tile * 128 : 2 * pixels + (tile + 1) * 128] = (factor * contrast_rows).astype(
+            jnp.bfloat16
+        )
 
 
 def weighted_rows(particles, defocus, inv_noise):
     rows = particles.shape[0]
     pixels = inv_noise.shape[0]
     block = min(ROW_BLOCK, rows)
+    row_sin, row_cos, expand, col_cos, col_sin = contrast_tables(defocus, pixels)
+    width = row_sin.shape[1]
     return pl.pallas_call(
         weights_kernel,
         grid=(rows // block,),
         in_specs=[
-            pl.BlockSpec((block, 1), lambda i: (i, 0)),
-            pl.BlockSpec((1, pixels), lambda i: (0, 0)),
+            pl.BlockSpec((block, width), lambda i: (i, 0)),
+            pl.BlockSpec((block, width), lambda i: (i, 0)),
+            pl.BlockSpec((width, pixels), lambda i: (0, 0)),
+            pl.BlockSpec((block, 128), lambda i: (i, 0)),
+            pl.BlockSpec((block, 128), lambda i: (i, 0)),
             pl.BlockSpec((1, pixels), lambda i: (0, 0)),
             pl.BlockSpec((block, 2 * pixels), lambda i: (i, 0)),
         ],
         out_specs=pl.BlockSpec((block, 3 * pixels), lambda i: (i, 0)),
         out_shape=jax.ShapeDtypeStruct((rows, 3 * pixels), jnp.bfloat16),
-    )(defocus[:, None], frequencies(pixels)[None, :], inv_noise[None, :], particles)
+    )(row_sin, row_cos, expand, col_cos, col_sin, inv_noise[None, :], particles)
 
 
 def on_device(particles, defocus, inv_noise, references, part_class, part_rot, counts):

time: 233 us -> 182 us (0.78)
  Pallas kernels: 82.4 us -> 24.1 us
  other arithmetic: 7.67 us -> 17.3 us
    pallas_call x1, Pallas kernels: 82.4 us -> 24.1 us  [weighted_rows(): pl.pallas_call(weights_kernel, grid=(rows // block,), in_specs=[pl.BlockS...]
    convert_element_type x0 -> x2, other arithmetic: none -> 4.82 us  [the longest x1 2.46 us: split_pieces(): pieces.append(piece.astype(jnp.bfloat16))]
    sin x0 -> x1, other arithmetic: none -> 3.05 us  [contrast_tables(): jnp.sin(column_angle)]
  transfers between devices with their start and end apart: 2 -> 2, of which waited for: 1 -> 1; matrix products, arithmetic and copies ran while one was open for 19% -> 28% of each run, Pallas kernels for 35% -> 13%
where the time goes in v2:
time: 182 us
  waiting for transfers between devices  75.8 us (42%)
  matrix products  34.7 us (19%)
  Pallas kernels  24.1 us (13%)
  other arithmetic  17.3 us (10%)
  between operations  14.8 us (8%)
  blocking collectives  11.7 us (6%)
  local copies, waits for them, and re-layouts  3.26 us (2%)
    reduce_scatter x1, waiting for transfers between devices, on_device(): sums = lax.psum_scatter(partial, 'dom', scatter_dimension=0, tiled=True)  75.1 us
    pallas_call x1, Pallas kernels, weighted_rows(): pl.pallas_call(weights_kernel, grid=(rows // block,), in_specs=[pl.BlockS...  24.1 us
    dot_general x1, matrix products, on_device(): lax.dot_general(payload, templates, (((1,), (1,)), ((), ())), preferred_e...  19.8 us
    dot_general x1, matrix products, on_device(): partial = jnp.dot(selector, payload, preferred_element_type=jnp.float32)  14.9 us
    pmax x1, blocking collectives, on_device(): best_score = lax.pmax(jnp.max(score, axis=1), 'cls')  11.7 us
    mul x1, other arithmetic, on_device(): power * jnp.bfloat16(-0.5)  4.18 us
  transfers between devices with their start and end apart: 2, of which 1 were waited for; matrix products, arithmetic and copies ran while one was open for 28% of the time, Pallas kernels for 13%

profile of v2, /device:TPU:0, one launch (start us, length us, event | category | flops | bytes accessed | tf_op | source)
XLA Modules:
  0.0 181.8 jit_solution(16605383634392423548)
XLA Ops:
  7.2 0.0 all-gather.2.cloned.1.call-start
  7.2 0.7 all-gather.2.cloned.1.call-update
  7.9 0.0 reduce-scatter.2.cloned.1.call-start
  7.9 1.3 broadcast_in_dim.7.noise_ref
  9.3 0.7 broadcast_multiply_fusion
  10.0 2.5 %reduce-precision_convert_fusion.1 = (bf16[1024,72]{1,0:T(8,128)(2,1)S(1)}, bf16[1024,72]{1,0:T(8,128)(2,1)S(1)}, bf16[1024,72]{1,0:T(8,128)(2,1)S(1)}, bf16[102...) fusion(f32[1024]{0:T(1024)S(1)} %broadcast_multiply_fusion, ...), kind=kLoop, calls=%fused_computation.24 | loop fusion | flops 1400832 | bytes 889120 | tf_op jit(solution)/shard_map/convert_element_type | solution.py:19
  12.5 1.7 fusion.26
  14.2 3.1 %fusion.29 = (f32[1024,128]{1,0:T(8,128)}, f32[1024,128]{1,0:T(8,128)}) fusion(f32[128]{0:T(128)S(1)} %fusion.37, f32[1024]{0:T(1024)S(1)} %broadcast_multiply_fusion), kind=kLoop, calls=%fused_computation.42 | loop fusion | flops 262144 | bytes 1053184 | tf_op jit(solution)/shard_map/sin | solution.py:38
  17.2 2.4 %and_convert_fusion.expand_ref = bf16[256,4608]{1,0:T(8,128)(2,1)} fusion(s32[4608]{0:T(1024)S(1)} %add_select_fusion, s32[256]{0:T(256)S(1)} %and_select_fusion.1, pred[256]{0:T(512)(128)(4,1)S(1)} %iota_compare_fusion.3), kind=kLoop, calls=%fused_computation.4 | loop fusion | flops 3538944 | bytes 2379008 | tf_op jit(solution)/shard_map/convert_element_type | solution.py:37
  19.6 24.1 %shard_map.86 = bf16[1024,13824]{1,0:T(8,128)(2,1)} custom-call(bf16[1024,256]{1,0:T(8,128)(2,1)} %get-tuple-element.10.row_sin_ref, bf16[1024,256]{1,0:T(8,128)(2,1)} %get-tuple-element.11.row_cos_ref, bf16[256,4608]{1,0:T(8,128)(2,1)} %and_convert_fusion.expand_ref, f32[1024,128]{1,0:T(8,128)} %get-tuple-element.3.col_cos_ref, ...), custom_call_target="tpu_custom_call" | custom-call | tf_op jit(solution)/shard_map/pallas_call | solution.py:66
  43.7 14.9 %fusion.18 = f32[192,13824]{1,0:T(8,128)} fusion(bf16[1024,13824]{1,0:T(8,128)(2,1)} %shard_map.86, s32[1024]{0:T(1024)S(1)} %add_select_fusion.1), kind=kOutput, calls=%fused_computation.20 | convolution fusion | flops 5436014592 | bytes 38932480 | tf_op jit(solution)/shard_map/dot_general | solution.py:117
  58.7 0.0 reduce-scatter.2.cloned.1.call-update
  58.7 0.6 copy-done.3
  59.3 0.6 reduce_sum.9
  60.6 0.1 dynamic_slice.3
  60.7 0.1 broadcast_in_dim.8
  60.8 0.1 add.86
  60.9 0.0 all-gather.2.cloned.1.call-done
  60.9 4.2 %fusion.4 = bf16[192,4608]{1,0:T(8,128)(2,1)} fusion(bf16[192,9216]{1,0:T(8,128)(2,1)} %bitcast.5), kind=kLoop, calls=%fused_computation.6 | loop fusion | flops 6193152 | bytes 5308416 | tf_op jit(solution)/shard_map/mul | solution.py:97
  65.1 19.8 %fusion.8 = f32[1024]{0:T(1024)S(1)} fusion(bf16[1024,13824]{1,0:T(8,128)(2,1)} %shard_map.86, bf16[192,4608]{1,0:T(8,128)(2,1)} %fusion.4, bf16[192,9216]{1,0:T(8,128)(2,1)S(1)} %bitcast.6, f32[192]{0:T(256)S(1)} %add.86), kind=kOutput, calls=%fused_computation.8 | convolution fusion | flops 5446827008 | bytes 33624832 | tf_op jit(solution)/shard_map/dot_general | solution.py:106
  84.9 11.7 %pmax.7 = f32[1024]{0:T(1024)} all-reduce(f32[1024]{0:T(1024)S(1)} %fusion.8), channel_id=1, replica_groups=mesh['dom'=8,'cls'=4] {'cls'}, use_global_device_ids=true, to_apply=%region_2.3 | all-reduce | flops 1024 | bytes 8192 | tf_op jit(solution)/shard_map/pmax | solution.py:110
  96.6 75.1 %reduce-scatter.2.cloned.1.call-done = f32[24,13824]{1,0:T(8,128)} async-done(((f32[192,13824]{1,0:T(8,128)}), f32[24,13824]{1,0:T(8,128)}) %reduce-scatter.2.cloned.1.call-update) | async-done | bytes 1327120 | tf_op jit(solution)/shard_map/reduce_scatter | solution.py:118
  171.7 1.0 slice.19
  172.7 2.2 %fusion.17 = f32[3,8,9216]{2,1,0:T(8,128)} fusion(f32[24,13824]{1,0:T(8,128)} %reduce-scatter.2.cloned.1.call-done, f32[24,4608]{1,0:T(8,128)S(1)} %slice.19), kind=kLoop, calls=%fused_computation.17 | loop fusion | flops 663552 | bytes 2211840 | tf_op jit(solution)/shard_map/reshape | solution.py:122
  (14 shorter events, 0.1 us)
Async XLA Ops:
  7.2 53.7 %all-gather.2.cloned.1.call-start = ((), (), s32[]{:S(2)}) async-start(), calls=%async_computation.1 | async-start | bytes 3981312 | tf_op jit(solution)/shard_map/all_gather | solution.py:92
  7.9 163.8 %reduce-scatter.2.cloned.1.call-start = ((), (), s32[]{:S(2)}) async-start(), calls=%async_computation.2 | async-start | bytes 11943936 | tf_op jit(solution)/shard_map/reduce_scatter | solution.py:118
  19.6 24.1 %copy-start.1 = (s32[1024]{0:T(1024)S(1)}, s32[1024]{0:T(1024)}, u32[]{:S(2)}) copy-start(s32[1024]{0:T(1024)} %param.12) | copy-start | bytes 12292
  19.6 24.1 %copy-start.2 = (s32[1024]{0:T(1024)S(1)}, s32[1024]{0:T(1024)}, u32[]{:S(2)}) copy-start(s32[1024]{0:T(1024)} %param.11) | copy-start | bytes 12292
  58.7 0.7 copy-start.3
  60.9 4.2 %copy-start = (bf16[24,8,9216]{2,1,0:T(8,128)(2,1)S(1)}, bf16[24,8,9216]{2,1,0:T(8,128)(2,1)}, u32[]{:S(2)}) copy-start(bf16[24,8,9216]{2,1,0:T(8,128)(2,1)} %all-gather.2.cloned.1.call-done) | copy-start | bytes 10616836
Sparse Core Ops, SparseCore 0:
  9.6 44.2 all-gather.1
  58.8 112.8 reduce-scatter.1

commit v3 on v2

--- a/solution.py
+++ b/solution.py
@@ -115,7 +115,8 @@
     poses = jnp.arange(block_classes * rotations, dtype=jnp.int32)
     selector = (poses[:, None] == pose[None, :]).astype(jnp.bfloat16)
     partial = jnp.dot(selector, payload, preferred_element_type=jnp.float32)
-    sums = lax.psum_scatter(partial, "dom", scatter_dimension=0, tiled=True)
+    sums = lax.psum_scatter(partial.astype(jnp.bfloat16), "dom", scatter_dimension=0, tiled=True)
+    sums = sums.astype(jnp.float32)
     numerator = sums[:, : 2 * pixels]
     denominator = sums[:, 2 * pixels :]
     class_images = numerator / (jnp.concatenate([denominator, denominator], axis=1) + 1.0)

time: 182 us -> 131 us (0.72)
  waiting for transfers between devices: 75.8 us -> 26.2 us
    reduce_scatter x1, waiting for transfers between devices: 75.1 us -> 25.5 us  [on_device(): lax.psum_scatter(partial.astype(jnp.bfloat16), 'dom', scatter_dimension=0...]
  transfers between devices with their start and end apart: 2 -> 2, of which waited for: 1 -> 1; matrix products, arithmetic and copies ran while one was open for 28% -> 38% of each run, Pallas kernels for 13% -> 18%
where the time goes in v3:
time: 131 us
  matrix products  33.4 us (25%)
  waiting for transfers between devices  26.2 us (20%)
  Pallas kernels  24.1 us (18%)
  other arithmetic  17.2 us (13%)
  between operations  14.8 us (11%)
  blocking collectives  11.7 us (9%)
  local copies, waits for them, and re-layouts  3.19 us (2%)
    reduce_scatter x1, waiting for transfers between devices, on_device(): lax.psum_scatter(partial.astype(jnp.bfloat16), 'dom', scatter_dimension=0...  25.5 us
    pallas_call x1, Pallas kernels, weighted_rows(): pl.pallas_call(weights_kernel, grid=(rows // block,), in_specs=[pl.BlockS...  24.1 us
    dot_general x1, matrix products, on_device(): lax.dot_general(payload, templates, (((1,), (1,)), ((), ())), preferred_e...  19.4 us
    dot_general x1, matrix products, on_device(): partial = jnp.dot(selector, payload, preferred_element_type=jnp.float32)  14.1 us
    pmax x1, blocking collectives, on_device(): best_score = lax.pmax(jnp.max(score, axis=1), 'cls')  11.7 us
    mul x1, other arithmetic, on_device(): power * jnp.bfloat16(-0.5)  4.12 us
    sin x1, other arithmetic, contrast_tables(): jnp.sin(column_angle)  3.05 us
  transfers between devices with their start and end apart: 2, of which 1 were waited for; matrix products, arithmetic and copies ran while one was open for 38% of the time, Pallas kernels for 18%

profile of v3, /device:TPU:0, one launch (start us, length us, event | category | flops | bytes accessed | tf_op | source)
XLA Modules:
  0.0 130.8 jit_solution(15512897918921777030)
XLA Ops:
  7.2 0.0 all-gather.2.cloned.1.call-start
  7.2 0.7 all-gather.2.cloned.1.call-update
  7.9 0.0 reduce-scatter.2.cloned.1.call-start
  7.9 1.3 %broadcast_in_dim.7.noise_ref = f32[1,4608]{1,0:T(1,128)} reshape(f32[4608]{0:T(1024)} %param.9) | data formatting | bytes 36864 | tf_op jit(solution)/shard_map/broadcast_in_dim | solution.py:80
  9.3 0.7 broadcast_multiply_fusion
  10.0 2.5 %reduce-precision_convert_fusion.1 = (bf16[1024,72]{1,0:T(8,128)(2,1)S(1)}, bf16[1024,72]{1,0:T(8,128)(2,1)S(1)}, bf16[1024,72]{1,0:T(8,128)(2,1)S(1)}, bf16[102...) fusion(f32[1024]{0:T(1024)S(1)} %broadcast_multiply_fusion, ...), kind=kLoop, calls=%fused_computation.24 | loop fusion | flops 1400832 | bytes 889120 | tf_op jit(solution)/shard_map/convert_element_type | solution.py:19
  12.5 1.7 %fusion.25 = (bf16[1024,256]{1,0:T(8,128)(2,1)}, bf16[1024,256]{1,0:T(8,128)(2,1)}) fusion(bf16[1024,72]{1,0:T(8,128)(2,1)S(1)} %get-tuple-element.6, bf16[1024,72]{1,0:T(8,128)(2,1)S(1)} %get-tuple-element.5, bf16[1024,72]{1,0:T(8,128)(2,1)S(1)} %get-tuple-element.9, bf16[1024,72]{1,0:T(8,128)(2,1)S(1)} %get-tuple-element.8, ...), kind=kLoop, calls=%fused_computation.38 | loop fusion | flops 4980736 | bytes 1933312 | tf_op jit(solution)/shard_map/concatenate | solution.py:21
  14.2 3.1 %fusion.28 = (f32[1024,128]{1,0:T(8,128)}, f32[1024,128]{1,0:T(8,128)}) fusion(f32[128]{0:T(128)S(1)} %fusion.36, f32[1024]{0:T(1024)S(1)} %broadcast_multiply_fusion), kind=kLoop, calls=%fused_computation.42 | loop fusion | flops 262144 | bytes 1053184 | tf_op jit(solution)/shard_map/sin | solution.py:38
  17.2 2.4 %and_convert_fusion.expand_ref = bf16[256,4608]{1,0:T(8,128)(2,1)} fusion(s32[4608]{0:T(1024)S(1)} %add_select_fusion, s32[256]{0:T(256)S(1)} %and_select_fusion.1, pred[256]{0:T(512)(128)(4,1)S(1)} %iota_compare_fusion.3), kind=kLoop, calls=%fused_computation.5 | loop fusion | flops 3538944 | bytes 2379008 | tf_op jit(solution)/shard_map/convert_element_type | solution.py:37
  19.6 24.1 %shard_map.86 = bf16[1024,13824]{1,0:T(8,128)(2,1)} custom-call(bf16[1024,256]{1,0:T(8,128)(2,1)} %get-tuple-element.10.row_sin_ref, bf16[1024,256]{1,0:T(8,128)(2,1)} %get-tuple-element.11.row_cos_ref, bf16[256,4608]{1,0:T(8,128)(2,1)} %and_convert_fusion.expand_ref, f32[1024,128]{1,0:T(8,128)} %get-tuple-element.3.col_cos_ref, ...), custom_call_target="tpu_custom_call" | custom-call | tf_op jit(solution)/shard_map/pallas_call | solution.py:66
  43.7 14.1 %convolution_convert_fusion = bf16[192,13824]{1,0:T(8,128)(2,1)} fusion(bf16[1024,13824]{1,0:T(8,128)(2,1)} %shard_map.86, s32[1024]{0:T(1024)S(1)} %add_select_fusion.1), kind=kOutput, calls=%fused_computation | convolution fusion | flops 5438668800 | bytes 33624064 | tf_op jit(solution)/shard_map/dot_general | solution.py:117
  57.8 0.6 copy-done.3
  58.4 0.6 reduce_sum.9
  59.7 0.1 dynamic_slice.3
  59.8 0.1 broadcast_in_dim.8
  59.9 0.1 add.86
  60.0 0.0 all-gather.2.cloned.1.call-done
  60.0 4.1 %fusion.4 = bf16[192,4608]{1,0:T(8,128)(2,1)} fusion(bf16[192,9216]{1,0:T(8,128)(2,1)} %bitcast.5), kind=kLoop, calls=%fused_computation.7 | loop fusion | flops 6193152 | bytes 5308416 | tf_op jit(solution)/shard_map/mul | solution.py:97
  64.1 19.4 %fusion.8 = f32[1024]{0:T(1024)S(1)} fusion(bf16[1024,13824]{1,0:T(8,128)(2,1)} %shard_map.86, bf16[192,4608]{1,0:T(8,128)(2,1)} %fusion.4, bf16[192,9216]{1,0:T(8,128)(2,1)S(1)} %bitcast.6, f32[192]{0:T(256)S(1)} %add.86), kind=kOutput, calls=%fused_computation.9 | convolution fusion | flops 5446827008 | bytes 33624832 | tf_op jit(solution)/shard_map/dot_general | solution.py:106
  83.5 11.7 %pmax.7 = f32[1024]{0:T(1024)} all-reduce(f32[1024]{0:T(1024)S(1)} %fusion.8), channel_id=1, replica_groups=mesh['dom'=8,'cls'=4] {'cls'}, use_global_device_ids=true, to_apply=%region_2.3 | all-reduce | flops 1024 | bytes 8192 | tf_op jit(solution)/shard_map/pmax | solution.py:110
  95.2 25.5 %reduce-scatter.2.cloned.1.call-done = bf16[24,13824]{1,0:T(8,128)(2,1)} async-done(((bf16[192,13824]{1,0:T(8,128)(2,1)}), bf16[24,13824]{1,0:T(8,128)(2,1)}) %reduce-scatter.2.cloned.1.call-update) | async-done | bytes 663568 | tf_op jit(solution)/shard_map/reduce_scatter | solution.py:118
  120.7 1.2 convert_element_type.75
  121.9 1.0 slice.19
  122.9 1.0 fusion.17
  (15 shorter events, 0.1 us)
Async XLA Ops:
  7.2 52.8 %all-gather.2.cloned.1.call-start = ((), (), s32[]{:S(2)}) async-start(), calls=%async_computation.1 | async-start | bytes 3981312 | tf_op jit(solution)/shard_map/all_gather | solution.py:92
  7.9 112.8 %reduce-scatter.2.cloned.1.call-start = ((), (), s32[]{:S(2)}) async-start(), calls=%async_computation.2 | async-start | bytes 5971968 | tf_op jit(solution)/shard_map/reduce_scatter | solution.py:118
  19.6 24.1 %copy-start.1 = (s32[1024]{0:T(1024)S(1)}, s32[1024]{0:T(1024)}, u32[]{:S(2)}) copy-start(s32[1024]{0:T(1024)} %param.12) | copy-start | bytes 12292
  19.6 24.1 %copy-start.2 = (s32[1024]{0:T(1024)S(1)}, s32[1024]{0:T(1024)}, u32[]{:S(2)}) copy-start(s32[1024]{0:T(1024)} %param.11) | copy-start | bytes 12292
  57.8 0.7 copy-start.3
  60.0 4.1 %copy-start = (bf16[24,8,9216]{2,1,0:T(8,128)(2,1)S(1)}, bf16[24,8,9216]{2,1,0:T(8,128)(2,1)}, u32[]{:S(2)}) copy-start(bf16[24,8,9216]{2,1,0:T(8,128)(2,1)} %all-gather.2.cloned.1.call-done) | copy-start | bytes 10616836
Sparse Core Ops, SparseCore 0:
  9.6 44.2 all-gather.1
  57.9 62.7 reduce-scatter.1

commit v4 on v2

--- a/solution.py
+++ b/solution.py
@@ -109,13 +109,29 @@
     score = score + jnp.repeat(class_prior, rotations)[None, :]
     best_score = lax.pmax(jnp.max(score, axis=1), "cls")
 
+    dom_index = lax.axis_index("dom")
+    chips = dom_size // 2
+    chip = dom_index // 2
+    core = dom_index % 2
+    block_rows = owned * rotations
     local_class = part_class - block_first
     in_block = (local_class >= 0) & (local_class < block_classes)
-    pose = jnp.where(in_block, local_class * rotations + part_rot, -1)
-    poses = jnp.arange(block_classes * rotations, dtype=jnp.int32)
-    selector = (poses[:, None] == pose[None, :]).astype(jnp.bfloat16)
+    owner = local_class // owned
+    mine = (owner % 2 == core).astype(jnp.int32)
+    offset = (owner // 2 - chip) % chips
+    row = ((mine * chips + offset) * owned + local_class % owned) * rotations + part_rot
+    row = jnp.where(in_block, row, -1)
+    rows = jnp.arange(2 * chips * block_rows, dtype=jnp.int32)
+    selector = (rows[:, None] == row[None, :]).astype(jnp.bfloat16)
     partial = jnp.dot(selector, payload, preferred_element_type=jnp.float32)
-    sums = lax.psum_scatter(partial, "dom", scatter_dimension=0, tiled=True)
+    partial = partial.reshape(2, chips, block_rows, 3 * pixels)
+    partner = [(d, d ^ 1) for d in range(dom_size)]
+    chip_sum = partial[1] + lax.ppermute(partial[0], "dom", partner)
+    sums = chip_sum[0]
+    for shift in range(1, chips):
+        pairs = [(d, 2 * ((d // 2 + shift) % chips) + d % 2) for d in range(dom_size)]
+        sent = lax.ppermute(chip_sum[shift].astype(jnp.bfloat16), "dom", pairs)
+        sums = sums + sent.astype(jnp.float32)
     numerator = sums[:, : 2 * pixels]
     denominator = sums[:, 2 * pixels :]
     class_images = numerator / (jnp.concatenate([denominator, denominator], axis=1) + 1.0)

time: 182 us -> 203 us (1.12)
  other arithmetic: 17.3 us -> 25.4 us
  waiting for transfers between devices: 75.8 us -> 83.5 us
  starting transfers between devices: 0.08 us -> 6.3 us
  local copies, waits for them, and re-layouts: 3.26 us -> 7.21 us
  matrix products: 34.7 us -> 30.8 us
    ppermute x0 -> x4, waiting for transfers between devices: none -> 83.5 us  [the longest x3 74.8 us: on_device(): sent = lax.ppermute(chip_sum[shift].astype(jnp.bfloat16), 'dom', pairs)]
    reduce_scatter x1 -> x0, waiting for transfers between devices: 75.1 us -> none  [on_device(): sums = lax.psum_scatter(partial, 'dom', scatter_dimension=0, tiled=True)]
    another operation x0 -> x1, other arithmetic: none -> 7.53 us
    ppermute x0 -> x4, starting transfers between devices: none -> 6.26 us  [the longest x3 5.81 us: on_device(): sent = lax.ppermute(chip_sum[shift].astype(jnp.bfloat16), 'dom', pairs)]
    slice x0 -> x1, local copies, waits for them, and re-layouts: none -> 4.62 us  [on_device(): chip_sum = partial[1] + lax.ppermute(partial[0], 'dom', partner)]
    dot_general x1, matrix products: 14.9 us -> 12 us  [on_device(): partial = jnp.dot(selector, payload, preferred_element_type=jnp.float32)]
  transfers between devices with their start and end apart: 2 -> 5, of which waited for: 1 -> 4; matrix products, arithmetic and copies ran while one was open for 28% -> 6% of each run, Pallas kernels for 13% -> 0%
where the time goes in v4:
time: 203 us; the launch traced here: 202 us
  waiting for transfers between devices  83.5 us (41%)
  matrix products  30.8 us (15%)
  other arithmetic  25.4 us (13%)
  Pallas kernels  23.7 us (12%)
  between operations  14.8 us (7%)
  blocking collectives  10.4 us (5%)
  local copies, waits for them, and re-layouts  7.21 us (4%)
  starting transfers between devices  6.3 us (3%)
    ppermute x3, waiting for transfers between devices, on_device(): sent = lax.ppermute(chip_sum[shift].astype(jnp.bfloat16), 'dom', pairs)  74.8 us
    pallas_call x1, Pallas kernels, weighted_rows(): pl.pallas_call(weights_kernel, grid=(rows // block,), in_specs=[pl.BlockS...  23.7 us
    dot_general x1, matrix products, on_device(): lax.dot_general(payload, templates, (((1,), (1,)), ((), ())), preferred_e...  18.8 us
    dot_general x1, matrix products, on_device(): partial = jnp.dot(selector, payload, preferred_element_type=jnp.float32)  12 us
    pmax x1, blocking collectives, on_device(): best_score = lax.pmax(jnp.max(score, axis=1), 'cls')  10.4 us
    ppermute x1, waiting for transfers between devices, on_device(): chip_sum = partial[1] + lax.ppermute(partial[0], 'dom', partner)  8.7 us
    another operation x1, other arithmetic  7.53 us
    ppermute x3, starting transfers between devices, on_device(): sent = lax.ppermute(chip_sum[shift].astype(jnp.bfloat16), 'dom', pairs)  5.81 us
  transfers between devices with their start and end apart: 5, of which 4 were waited for; matrix products, arithmetic and copies ran while one was open for 6% of the time, Pallas kernels for 0%

profile of v4, /device:TPU:0, one launch (start us, length us, event | category | flops | bytes accessed | tf_op | source)
XLA Modules:
  0.0 202.2 jit_solution(14536073934725312064)
XLA Ops:
  7.3 0.7 broadcast_multiply_fusion
  8.0 1.3 broadcast_in_dim.5.noise_ref
  9.3 3.1 %fusion.32 = (f32[1024,128]{1,0:T(8,128)}, f32[1024,128]{1,0:T(8,128)}) fusion(f32[128]{0:T(128)S(1)} %fusion.52, f32[1024]{0:T(1024)S(1)} %broadcast_multiply_fusion), kind=kLoop, calls=%fused_computation.49 | loop fusion | flops 262144 | bytes 1053184 | tf_op jit(solution)/shard_map/sin | solution.py:38
  12.4 2.5 %reduce-precision_convert_fusion.1 = (bf16[1024,72]{1,0:T(8,128)(2,1)S(1)}, bf16[1024,72]{1,0:T(8,128)(2,1)S(1)}, bf16[1024,72]{1,0:T(8,128)(2,1)S(1)}, bf16[102...) fusion(f32[1024]{0:T(1024)S(1)} %broadcast_multiply_fusion, ...), kind=kLoop, calls=%fused_computation.28 | loop fusion | flops 1400832 | bytes 889120 | tf_op jit(solution)/shard_map/convert_element_type | solution.py:19
  14.9 2.4 %and_convert_fusion.expand_ref = bf16[256,4608]{1,0:T(8,128)(2,1)} fusion(s32[4608]{0:T(1024)S(1)} %add_select_fusion, s32[256]{0:T(256)S(1)} %and_select_fusion.1, pred[256]{0:T(512)(128)(4,1)S(1)} %iota_compare_fusion.3), kind=kLoop, calls=%fused_computation.4 | loop fusion | flops 3538944 | bytes 2379008 | tf_op jit(solution)/shard_map/convert_element_type | solution.py:37
  17.3 1.7 fusion.29
  19.0 23.7 %shard_map.86 = bf16[1024,13824]{1,0:T(8,128)(2,1)} custom-call(bf16[1024,256]{1,0:T(8,128)(2,1)} %get-tuple-element.17.row_sin_ref, bf16[1024,256]{1,0:T(8,128)(2,1)} %get-tuple-element.18.row_cos_ref, bf16[256,4608]{1,0:T(8,128)(2,1)} %and_convert_fusion.expand_ref, f32[1024,128]{1,0:T(8,128)} %get-tuple-element.10.col_cos_ref, ...), custom_call_target="tpu_custom_call" | custom-call | tf_op jit(solution)/shard_map/pallas_call | solution.py:66
  42.7 12.0 %fusion.21 = f32[192,13824]{1,0:T(8,128)S(1)} fusion(bf16[1024,13824]{1,0:T(8,128)(2,1)} %shard_map.86, s32[1024]{0:T(1024)S(1)} %fusion.46), kind=kOutput, calls=%fused_computation.24 | convolution fusion | flops 5436014592 | bytes 38932480 | tf_op jit(solution)/shard_map/dot_general | solution.py:126
  54.7 4.6 %fusion.55 = (f32[96,13824]{1,0:T(8,128)}, f32[96,13824]{1,0:T(8,128)}) fusion(f32[192,13824]{1,0:T(8,128)S(1)} %fusion.21), kind=kLoop, calls=%fused_computation.94 | loop fusion | bytes 21233664 | tf_op jit(solution)/shard_map/slice | solution.py:129
  59.8 8.7 %collective-permute-done = f32[4,24,13824]{2,1,0:T(8,128)} collective-permute-done((f32[4,24,13824]{2,1,0:T(8,128)}, f32[4,24,13824]{2,1,0:T(8,128)}, u32[]{:S(2)}, u32[]{:S(2)}) %collective-permute-start) | collective-permute-done | bytes 5308448 | tf_op jit(solution)/shard_map/ppermute | solution.py:129
  68.5 7.5 %fusion.54 = (bf16[4,24,13824]{2,1,0:T(8,128)(2,1)S(1)}, f32[4,24,13824]{2,1,0:T(8,128)}) fusion(f32[4,24,13824]{2,1,0:T(8,128)} %bitcast.21, f32[4,24,13824]{2,1,0:T(8,128)} %collective-permute-done), kind=kLoop, calls=%fused_computation.93 | loop fusion | flops 2654208 | bytes 18579456 | tf_op jit(solution)/shard_map/convert.2
  76.0 1.0 slice_bitcast_fusion.3
  77.0 2.8 %collective-permute-start.1 = (bf16[24,13824]{1,0:T(8,128)(2,1)}, bf16[24,13824]{1,0:T(8,128)(2,1)S(1)}, u32[]{:S(2)}, u32[]{:S(2)}) collective-permute-start(bf16[24,13824]{1,0:T(8,128)(2,1)} %get-tuple-element.6), channel_id=1, source_target_pairs={{0,8},{4,12},{8,16},{12,20},{16,24},{20,28},{24,0},{28,4},{1,9},{5... | collective-permute-start | bytes 1990664 | tf_op jit(solution)/shard_map/ppermute | solution.py:133
  79.7 2.0 collective-permute-start.3
  81.7 1.0 collective-permute-start.2
  82.8 0.6 reduce_sum.9
  84.3 27.6 %collective-permute-done.1 = bf16[24,13824]{1,0:T(8,128)(2,1)S(1)} collective-permute-done((bf16[24,13824]{1,0:T(8,128)(2,1)}, bf16[24,13824]{1,0:T(8,128)(2,1)S(1)}, u32[]{:S(2)}, u32[]{:S(2)}) %collective-permute-start.1) | collective-permute-done | bytes 663584 | tf_op jit(solution)/shard_map/ppermute | solution.py:133
  111.9 17.7 %collective-permute-done.3 = bf16[24,13824]{1,0:T(8,128)(2,1)S(1)} collective-permute-done((bf16[24,13824]{1,0:T(8,128)(2,1)S(1)}, bf16[24,13824]{1,0:T(8,128)(2,1)S(1)}, u32[]{:S(2)}, u32[]{:S(2)}) %collective-permute-start.3) | collective-permute-done | bytes 663584 | tf_op jit(solution)/shard_map/ppermute | solution.py:133
  129.5 29.6 %collective-permute-done.2 = bf16[24,13824]{1,0:T(8,128)(2,1)S(1)} collective-permute-done((bf16[24,13824]{1,0:T(8,128)(2,1)S(1)}, bf16[24,13824]{1,0:T(8,128)(2,1)S(1)}, u32[]{:S(2)}, u32[]{:S(2)}) %collective-permute-start.2) | collective-permute-done | bytes 663584 | tf_op jit(solution)/shard_map/ppermute | solution.py:133
  159.1 1.6 fusion.7
  160.8 1.0 fusion.20
  161.8 4.2 %fusion.4 = bf16[192,4608]{1,0:T(8,128)(2,1)} fusion(bf16[192,9216]{1,0:T(8,128)(2,1)} %bitcast.23), kind=kLoop, calls=%fused_computation.6 | loop fusion | flops 6193152 | bytes 5308416 | tf_op jit(solution)/shard_map/mul | solution.py:97
  166.0 18.8 %fusion.11 = f32[1024]{0:T(1024)S(1)} fusion(bf16[1024,13824]{1,0:T(8,128)(2,1)} %shard_map.86, bf16[192,4608]{1,0:T(8,128)(2,1)} %fusion.4, bf16[192,9216]{1,0:T(8,128)(2,1)S(1)} %bitcast.24, f32[192]{0:T(256)S(1)} %add.123), kind=kOutput, calls=%fused_computation.12 | convolution fusion | flops 5446827008 | bytes 33624832 | tf_op jit(solution)/shard_map/dot_general | solution.py:106
  184.9 10.4 %pmax.7 = f32[1024]{0:T(1024)} all-reduce(f32[1024]{0:T(1024)S(1)} %fusion.11), channel_id=1, replica_groups=mesh['dom'=8,'cls'=4] {'cls'}, use_global_device_ids=true, to_apply=%region_2.3 | all-reduce | flops 1024 | bytes 8192 | tf_op jit(solution)/shard_map/pmax | solution.py:110
  (23 shorter events, 0.9 us)
Async XLA Ops:
  7.2 10.1 %copy-start.1 = (s32[1024]{0:T(1024)S(1)}, s32[1024]{0:T(1024)}, u32[]{:S(2)}) copy-start(s32[1024]{0:T(1024)} %param.12) | copy-start | bytes 12292
  7.2 10.1 %copy-start.2 = (s32[1024]{0:T(1024)S(1)}, s32[1024]{0:T(1024)}, u32[]{:S(2)}) copy-start(s32[1024]{0:T(1024)} %param.11) | copy-start | bytes 12292
  7.2 154.6 %all-gather.2.cloned.1.call-start = ((), (), s32[]{:S(2)}) async-start(), calls=%async_computation | async-start | bytes 3981312 | tf_op jit(solution)/shard_map/all_gather | solution.py:92
  59.3 9.2 %collective-permute-start = (f32[4,24,13824]{2,1,0:T(8,128)}, f32[4,24,13824]{2,1,0:T(8,128)}, u32[]{:S(2)}, u32[]{:S(2)}) collective-permute-start(f32[4,24,13824]{2,1,0:T(8,128)} %bitcast.22), channel_id=1, source_target_pairs={{0,4},{4,0},{8,12},{12,8},{16,20},{20,16},{24,28},{28,24},{1,5},{5... | collective-permute-start | bytes 15925256 | tf_op jit(solution)/shard_map/ppermute | solution.py:129
  76.0 6.8 %copy-start.3 = (s32[96]{0:T(128)S(1)}, s32[96]{0:T(128)}, u32[]{:S(2)}) copy-start(s32[96]{0:T(128)} %param.13) | copy-start | bytes 1156
  77.0 34.9 %collective-permute-start.1 = (bf16[24,13824]{1,0:T(8,128)(2,1)}, bf16[24,13824]{1,0:T(8,128)(2,1)S(1)}, u32[]{:S(2)}, u32[]{:S(2)}) collective-permute-start(bf16[24,13824]{1,0:T(8,128)(2,1)} %get-tuple-element.6), channel_id=1, source_target_pairs={{0,8},{4,12},{8,16},{12,20},{16,24},{20,28},{24,0},{28,4},{1,9},{5... | collective-permute-start | bytes 1990664 | tf_op jit(solution)/shard_map/ppermute | solution.py:133
  79.7 49.8 %collective-permute-start.3 = (bf16[24,13824]{1,0:T(8,128)(2,1)S(1)}, bf16[24,13824]{1,0:T(8,128)(2,1)S(1)}, u32[]{:S(2)}, u32[]{:S(2)}) collective-permute-start(bf16[24,13824]{1,0:T(8,128)(2,1)S(1)} %get-tuple-element.7), channel_id=1, source_target_pairs={{0,24},{4,28},{8,0},{12,4},{16,8},{20,12},{24,16},{28,20},{1,25},{... | collective-permute-start | bytes 1990664 | tf_op jit(solution)/shard_map/ppermute | solution.py:133
  81.7 77.4 %collective-permute-start.2 = (bf16[24,13824]{1,0:T(8,128)(2,1)S(1)}, bf16[24,13824]{1,0:T(8,128)(2,1)S(1)}, u32[]{:S(2)}, u32[]{:S(2)}) collective-permute-start(bf16[24,13824]{1,0:T(8,128)(2,1)S(1)} %get-tuple-element.8), channel_id=1, source_target_pairs={{0,16},{4,20},{8,24},{12,28},{16,0},{20,4},{24,8},{28,12},{1,17},{... | collective-permute-start | bytes 1990664 | tf_op jit(solution)/shard_map/ppermute | solution.py:133
  161.8 4.2 %copy-start = (bf16[24,8,9216]{2,1,0:T(8,128)(2,1)S(1)}, bf16[24,8,9216]{2,1,0:T(8,128)(2,1)}, u32[]{:S(2)}) copy-start(bf16[24,8,9216]{2,1,0:T(8,128)(2,1)} %all-gather.2.cloned.1.call-done) | copy-start | bytes 10616836
Sparse Core Ops, SparseCore 0:
  59.9 67.7 all-gather.1

commit v5 on v3

--- a/solution.py
+++ b/solution.py
@@ -4,7 +4,7 @@
 import jax.numpy as jnp
 from jax import lax
 from jax.experimental import pallas as pl
-from jax.sharding import PartitionSpec as P
+from jax.sharding import Mesh, PartitionSpec as P
 
 AMPLITUDE = math.hypot(0.995, 0.1)
 PHASE = math.atan2(0.1, 0.995)
@@ -84,12 +84,12 @@
     pixels = inv_noise.shape[0]
     owned = references.shape[0]
     rotations = references.shape[1]
-    dom_size = lax.axis_size("dom")
+    dom_size = lax.axis_size(("chip", "core"))
     cls_index = lax.axis_index("cls")
     block_classes = dom_size * owned
     block_first = cls_index * block_classes
 
-    images = lax.all_gather(references, "dom", axis=0, tiled=True)
+    images = lax.all_gather(references, ("chip", "core"), axis=0, tiled=True)
     flat_images = images.reshape(block_classes * rotations, 2 * pixels)
     real_part = flat_images[:, :pixels].astype(jnp.float32)
     imag_part = flat_images[:, pixels:].astype(jnp.float32)
@@ -109,13 +109,18 @@
     score = score + jnp.repeat(class_prior, rotations)[None, :]
     best_score = lax.pmax(jnp.max(score, axis=1), "cls")
 
+    chips = dom_size // 2
+    block_rows = owned * rotations
     local_class = part_class - block_first
     in_block = (local_class >= 0) & (local_class < block_classes)
-    pose = jnp.where(in_block, local_class * rotations + part_rot, -1)
-    poses = jnp.arange(block_classes * rotations, dtype=jnp.int32)
-    selector = (poses[:, None] == pose[None, :]).astype(jnp.bfloat16)
+    owner = local_class // owned
+    row = (((owner % 2) * chips + owner // 2) * owned + local_class % owned) * rotations + part_rot
+    row = jnp.where(in_block, row, -1)
+    rows = jnp.arange(dom_size * block_rows, dtype=jnp.int32)
+    selector = (rows[:, None] == row[None, :]).astype(jnp.bfloat16)
     partial = jnp.dot(selector, payload, preferred_element_type=jnp.float32)
-    sums = lax.psum_scatter(partial.astype(jnp.bfloat16), "dom", scatter_dimension=0, tiled=True)
+    chip_sums = lax.psum_scatter(partial, "core", scatter_dimension=0, tiled=True)
+    sums = lax.psum_scatter(chip_sums.astype(jnp.bfloat16), "chip", scatter_dimension=0, tiled=True)
     sums = sums.astype(jnp.float32)
     numerator = sums[:, : 2 * pixels]
     denominator = sums[:, 2 * pixels :]
@@ -124,11 +129,14 @@
 
 
 def solution(mesh):
-    placed = (P("dom", None), P("dom"), P(), P(("cls", "dom"), None, None), P("dom"), P("dom"), P())
+    dom_size, cls_size = mesh.devices.shape
+    split = Mesh(mesh.devices.reshape(dom_size // 2, 2, cls_size), ("chip", "core", "cls"))
+    dom = ("chip", "core")
+    placed = (P(dom, None), P(dom), P(), P(("cls",) + dom, None, None), P(dom), P(dom), P())
     return jax.shard_map(
         on_device,
-        mesh=mesh,
+        mesh=split,
         in_specs=placed,
-        out_specs=(P("dom"), P(("cls", "dom"), None, None)),
+        out_specs=(P(dom), P(("cls",) + dom, None, None)),
         check_vma=False,
     )

time: 131 us -> 164 us (1.25)
  waiting for transfers between devices: 26.2 us -> 54.5 us
  other arithmetic: 17.2 us -> 22.4 us
    all_gather x1, waiting for transfers between devices: 0.02 us -> 32.7 us  [on_device(): images = lax.all_gather(references, ('chip', 'core'), axis=0, tiled=True)]
    convert_element_type x0 -> x1, other arithmetic: none -> 4.41 us  [on_device(): chip_sums.astype(jnp.bfloat16)]
    reduce_scatter x1 -> x2, waiting for transfers between devices: 25.5 us -> 21.3 us  [the longest x1 21.3 us: on_device(): lax.psum_scatter(partial, 'core', scatter_dimension=0, tiled=True)]
  transfers between devices with their start and end apart: 2 -> 3, of which waited for: 1 -> 2; matrix products, arithmetic and copies ran while one was open for 38% -> 17% of each run, Pallas kernels for 18% -> 0%
where the time goes in v5:
time: 164 us
  waiting for transfers between devices  54.5 us (33%)
  matrix products  33.5 us (20%)
  Pallas kernels  23.7 us (14%)
  other arithmetic  22.4 us (14%)
  between operations  16.2 us (10%)
  blocking collectives  10.4 us (6%)
  local copies, waits for them, and re-layouts  2.55 us (2%)
    all_gather x1, waiting for transfers between devices, on_device(): images = lax.all_gather(references, ('chip', 'core'), axis=0, tiled=True)  32.7 us
    pallas_call x1, Pallas kernels, weighted_rows(): pl.pallas_call(weights_kernel, grid=(rows // block,), in_specs=[pl.BlockS...  23.7 us
    reduce_scatter x1, waiting for transfers between devices, on_device(): lax.psum_scatter(partial, 'core', scatter_dimension=0, tiled=True)  21.3 us
    dot_general x1, matrix products, on_device(): lax.dot_general(payload, templates, (((1,), (1,)), ((), ())), preferred_e...  18.9 us
    dot_general x1, matrix products, on_device(): partial = jnp.dot(selector, payload, preferred_element_type=jnp.float32)  14.5 us
    pmax x1, blocking collectives, on_device(): best_score = lax.pmax(jnp.max(score, axis=1), 'cls')  10.4 us
    convert_element_type x1, other arithmetic, on_device(): chip_sums.astype(jnp.bfloat16)  4.41 us
    mul x1, other arithmetic, on_device(): power * jnp.bfloat16(-0.5)  4.1 us
  transfers between devices with their start and end apart: 3, of which 2 were waited for; matrix products, arithmetic and copies ran while one was open for 17% of the time, Pallas kernels for 0%

profile of v5, /device:TPU:0, one launch (start us, length us, event | category | flops | bytes accessed | tf_op | source)
XLA Modules:
  0.0 163.5 jit_solution(13383404922978656480)
XLA Ops:
  8.1 0.7 broadcast_multiply_fusion
  8.8 1.3 broadcast_in_dim.5.noise_ref
  10.1 3.1 %fusion.29 = (f32[1024,128]{1,0:T(8,128)}, f32[1024,128]{1,0:T(8,128)}) fusion(f32[128]{0:T(128)S(1)} %fusion.49, f32[1024]{0:T(1024)S(1)} %broadcast_multiply_fusion), kind=kLoop, calls=%fused_computation.42 | loop fusion | flops 262144 | bytes 1053184 | tf_op jit(solution)/shard_map/sin | solution.py:38
  13.2 2.5 %reduce-precision_convert_fusion.1 = (bf16[1024,72]{1,0:T(8,128)(2,1)S(1)}, bf16[1024,72]{1,0:T(8,128)(2,1)S(1)}, bf16[1024,72]{1,0:T(8,128)(2,1)S(1)}, bf16[102...) fusion(f32[1024]{0:T(1024)S(1)} %broadcast_multiply_fusion, ...), kind=kLoop, calls=%fused_computation.24 | loop fusion | flops 1400832 | bytes 889120 | tf_op jit(solution)/shard_map/convert_element_type | solution.py:19
  15.7 0.7 fusion.41
  16.4 2.4 %and_convert_fusion.expand_ref = bf16[256,4608]{1,0:T(8,128)(2,1)} fusion(s32[4608]{0:T(1024)S(1)} %add_select_fusion, s32[256]{0:T(256)S(1)} %and_select_fusion.1, pred[256]{0:T(512)(128)(4,1)S(1)} %iota_compare_fusion.3), kind=kLoop, calls=%fused_computation.4 | loop fusion | flops 3538944 | bytes 2379008 | tf_op jit(solution)/shard_map/convert_element_type | solution.py:37
  18.8 1.6 %fusion.26 = (bf16[1024,256]{1,0:T(8,128)(2,1)}, bf16[1024,256]{1,0:T(8,128)(2,1)}) fusion(bf16[1024,72]{1,0:T(8,128)(2,1)S(1)} %get-tuple-element.6, bf16[1024,72]{1,0:T(8,128)(2,1)S(1)} %get-tuple-element.5, bf16[1024,72]{1,0:T(8,128)(2,1)S(1)} %get-tuple-element.9, bf16[1024,72]{1,0:T(8,128)(2,1)S(1)} %get-tuple-element.8, ...), kind=kLoop, calls=%fused_computation.38 | loop fusion | flops 4980736 | bytes 1933312 | tf_op jit(solution)/shard_map/concatenate | solution.py:21
  20.4 23.7 %shard_map.86 = bf16[1024,13824]{1,0:T(8,128)(2,1)} custom-call(bf16[1024,256]{1,0:T(8,128)(2,1)} %get-tuple-element.10.row_sin_ref, bf16[1024,256]{1,0:T(8,128)(2,1)} %get-tuple-element.11.row_cos_ref, bf16[256,4608]{1,0:T(8,128)(2,1)} %and_convert_fusion.expand_ref, f32[1024,128]{1,0:T(8,128)} %get-tuple-element.3.col_cos_ref, ...), custom_call_target="tpu_custom_call" | custom-call | tf_op jit(solution)/shard_map/pallas_call | solution.py:66
  44.1 14.5 %fusion.18 = f32[192,13824]{1,0:T(8,128)} fusion(bf16[1024,13824]{1,0:T(8,128)(2,1)} %shard_map.86, s32[1024]{0:T(1024)S(1)} %fusion.41), kind=kOutput, calls=%fused_computation.20 | convolution fusion | flops 5436014592 | bytes 38932480 | tf_op jit(solution)/shard_map/dot_general | solution.py:121
  58.7 0.5 all-gather.2.cloned.1.call-update
  59.3 0.2 reduce-scatter.5.cloned.1.call-start
  59.5 21.3 %reduce-scatter.3.cloned.1.call-done = f32[96,13824]{1,0:T(8,128)} async-done(((f32[192,13824]{1,0:T(8,128)}), f32[96,13824]{1,0:T(8,128)}) %reduce-scatter.3.cloned.1.call-update) | async-done | bytes 5308432 | tf_op jit(solution)/shard_map/reduce_scatter | solution.py:122
  80.7 4.4 %convert_element_type.74 = bf16[96,13824]{1,0:T(8,128)(2,1)} convert(f32[96,13824]{1,0:T(8,128)} %reduce-scatter.3.cloned.1.call-done) | non-fusion elementwise | flops 1327104 | bytes 7962624 | tf_op jit(solution)/shard_map/convert_element_type | solution.py:123
  85.2 0.6 reduce_sum.9
  86.5 0.1 dynamic_slice.3
  86.6 0.1 broadcast_in_dim.6
  86.6 0.1 add.106
  86.7 32.7 %all-gather.2.cloned.1.call-done = bf16[24,8,9216]{2,1,0:T(8,128)(2,1)} async-done(((bf16[3,8,9216]{2,1,0:T(8,128)(2,1)}), bf16[24,8,9216]{2,1,0:T(8,128)(2,1)}) %all-gather.2.cloned.1.call-update) | async-done | bytes 3538960 | tf_op jit(solution)/shard_map/all_gather | solution.py:92
  119.4 4.1 %fusion.4 = bf16[192,4608]{1,0:T(8,128)(2,1)} fusion(bf16[192,9216]{1,0:T(8,128)(2,1)} %bitcast.5), kind=kLoop, calls=%fused_computation.6 | loop fusion | flops 6193152 | bytes 5308416 | tf_op jit(solution)/shard_map/mul | solution.py:97
  123.5 18.9 %fusion.8 = f32[1024]{0:T(1024)S(1)} fusion(bf16[1024,13824]{1,0:T(8,128)(2,1)} %shard_map.86, bf16[192,4608]{1,0:T(8,128)(2,1)} %fusion.4, bf16[192,9216]{1,0:T(8,128)(2,1)S(1)} %bitcast.6, f32[192]{0:T(256)S(1)} %add.106), kind=kOutput, calls=%fused_computation.8 | convolution fusion | flops 5446827008 | bytes 33624832 | tf_op jit(solution)/shard_map/dot_general | solution.py:106
  142.5 10.4 %pmax.7 = f32[1024]{0:T(1024)} all-reduce(f32[1024]{0:T(1024)S(1)} %fusion.8), channel_id=1, replica_groups=mesh['chip'=4,'core'=2,'cls'=4] {'cls'}, use_global_device_ids=true, to_apply=%region_2.3 | all-reduce | flops 1024 | bytes 8192 | tf_op jit(solution)/shard_map/pmax | solution.py:110
  152.9 1.0 slice.19
  153.9 1.2 convert_element_type.75
  155.1 1.0 fusion.17
  (15 shorter events, 0.2 us)
Async XLA Ops:
  8.0 72.8 %reduce-scatter.3.cloned.1.call-start = ((), (), s32[]{:S(2)}) async-start(), calls=%async_computation.3 | async-start | bytes 15925248 | tf_op jit(solution)/shard_map/reduce_scatter | solution.py:122
  58.7 60.7 %all-gather.2.cloned.1.call-start = ((), (), s32[]{:S(2)}) async-start(), calls=%async_computation.2 | async-start | bytes 3981312 | tf_op jit(solution)/shard_map/all_gather | solution.py:92
  59.2 25.9 %copy-start.1 = (s32[96]{0:T(128)S(1)}, s32[96]{0:T(128)}, u32[]{:S(2)}) copy-start(s32[96]{0:T(128)} %param.13) | copy-start | bytes 1156
  59.3 93.6 %reduce-scatter.5.cloned.1.call-start = ((), (), s32[]{:S(2)}) async-start(), calls=%async_computation.4 | async-start | bytes 3317760 | tf_op jit(solution)/shard_map/reduce_scatter | solution.py:123
  119.4 4.1 %copy-start = (bf16[24,8,9216]{2,1,0:T(8,128)(2,1)S(1)}, bf16[24,8,9216]{2,1,0:T(8,128)(2,1)}, u32[]{:S(2)}) copy-start(bf16[24,8,9216]{2,1,0:T(8,128)(2,1)} %all-gather.2.cloned.1.call-done) | copy-start | bytes 10616836
Sparse Core Ops, SparseCore 0:
  58.8 21.9 reduce-scatter.2
  85.3 61.5 reduce-scatter.4
Sparse Core Ops, SparseCore 1:
  60.8 58.6 all-gather.1

commit v6 on v2

v6 whole, which is shorter than its diff:
```python
import math

import jax
import jax.numpy as jnp
from jax import lax
from jax.experimental import pallas as pl
from jax.sharding import PartitionSpec as P

AMPLITUDE = math.hypot(0.995, 0.1)
PHASE = math.atan2(0.1, 0.995)
ROW_BLOCK = 128


def split_pieces(values, width):
    pieces = []
    rest = values
    for _ in range(3):
        piece = lax.reduce_precision(rest, exponent_bits=8, mantissa_bits=7)
        pieces.append(piece.astype(jnp.bfloat16))
        rest = rest - piece
    joined = jnp.concatenate(pieces, axis=1)
    return jnp.pad(joined, ((0, 0), (0, width - joined.shape[1])))


def contrast_tables(defocus, pixels):
    groups = pixels // 64
    scaled = 12.0 * defocus
    row_offset = (jnp.arange(groups, dtype=jnp.int32) - pixels // 128).astype(jnp.float32)
    row_angle = scaled[:, None] * (row_offset * row_offset / 4096.0)[None, :]
    column = (jnp.arange(128, dtype=jnp.int32) % 64).astype(jnp.float32)
    column_angle = scaled[:, None] * (column * column / 4096.0)[None, :] + PHASE
    width = -(-3 * groups // 128) * 128
    row_sin = split_pieces(-AMPLITUDE * jnp.sin(row_angle), width)
    row_cos = split_pieces(-AMPLITUDE * jnp.cos(row_angle), width)
    slot = jnp.arange(width, dtype=jnp.int32)[:, None]
    group_of = (jnp.arange(pixels, dtype=jnp.int32) // 64)[None, :]
    expand = ((slot < 3 * groups) & (slot % groups == group_of)).astype(jnp.bfloat16)
    return row_sin, row_cos, expand, jnp.cos(column_angle), jnp.sin(column_angle)


def contrast_tile(row_sin, row_cos, col_cos, col_sin, tile):
    lanes = slice(tile * 128, (tile + 1) * 128)
    return row_sin[:, lanes] * col_cos + row_cos[:, lanes] * col_sin


def weights_kernel(row_sin_ref, row_cos_ref, expand_ref, col_cos_ref, col_sin_ref, noise_ref, particles_ref, out_ref, power_ref):
    pixels = noise_ref.shape[1]
    row_sin = jnp.dot(row_sin_ref[...], expand_ref[...], preferred_element_type=jnp.float32)
    row_cos = jnp.dot(row_cos_ref[...], expand_ref[...], preferred_element_type=jnp.float32)
    col_cos = col_cos_ref[...]
    col_sin = col_sin_ref[...]
    for tile in range(pixels // 128):
        lanes = slice(tile * 128, (tile + 1) * 128)
        imag = slice(pixels + tile * 128, pixels + (tile + 1) * 128)
        contrast_rows = contrast_tile(row_sin, row_cos, col_cos, col_sin, tile)
        factor = noise_ref[:, lanes] * contrast_rows
        out_ref[:, lanes] = (particles_ref[:, lanes].astype(jnp.float32) * factor).astype(jnp.bfloat16)
        out_ref[:, imag] = (particles_ref[:, imag].astype(jnp.float32) * factor).astype(jnp.bfloat16)
        power_ref[:, lanes] = (factor * contrast_rows).astype(jnp.bfloat16)


def power_kernel(row_sin_ref, row_cos_ref, expand_ref, col_cos_ref, col_sin_ref, noise_ref, power_ref):
    pixels = noise_ref.shape[1]
    row_sin = jnp.dot(row_sin_ref[...], expand_ref[...], preferred_element_type=jnp.float32)
    row_cos = jnp.dot(row_cos_ref[...], expand_ref[...], preferred_element_type=jnp.float32)
    col_cos = col_cos_ref[...]
    col_sin = col_sin_ref[...]
    for tile in range(pixels // 128):
        lanes = slice(tile * 128, (tile + 1) * 128)
        contrast_rows = contrast_tile(row_sin, row_cos, col_cos, col_sin, tile)
        factor = noise_ref[:, lanes] * contrast_rows
        power_ref[:, lanes] = (factor * contrast_rows).astype(jnp.bfloat16)


def table_specs(block, width, pixels):
    return [
        pl.BlockSpec((block, width), lambda i: (i, 0)),
        pl.BlockSpec((block, width), lambda i: (i, 0)),
        pl.BlockSpec((width, pixels), lambda i: (0, 0)),
        pl.BlockSpec((block, 128), lambda i: (i, 0)),
        pl.BlockSpec((block, 128), lambda i: (i, 0)),
        pl.BlockSpec((1, pixels), lambda i: (0, 0)),
    ]


def weighted_rows(particles, defocus, inv_noise):
    rows = particles.shape[0]
    pixels = inv_noise.shape[0]
    block = min(ROW_BLOCK, rows)
    tables = contrast_tables(defocus, pixels)
    width = tables[0].shape[1]
    return pl.pallas_call(
        weights_kernel,
        grid=(rows // block,),
        in_specs=table_specs(block, width, pixels) + [pl.BlockSpec((block, 2 * pixels), lambda i: (i, 0))],
        out_specs=[
            pl.BlockSpec((block, 2 * pixels), lambda i: (i, 0)),
            pl.BlockSpec((block, pixels), lambda i: (i, 0)),
        ],
        out_shape=[
            jax.ShapeDtypeStruct((rows, 2 * pixels), jnp.bfloat16),
            jax.ShapeDtypeStruct((rows, pixels), jnp.bfloat16),
        ],
    )(*tables, inv_noise[None, :], particles)


def power_rows(defocus, inv_noise):
    rows = defocus.shape[0]
    pixels = inv_noise.shape[0]
    block = min(ROW_BLOCK, rows)
    tables = contrast_tables(defocus, pixels)
    width = tables[0].shape[1]
    return pl.pallas_call(
        power_kernel,
        grid=(rows // block,),
        in_specs=table_specs(block, width, pixels),
        out_specs=pl.BlockSpec((block, pixels), lambda i: (i, 0)),
        out_shape=jax.ShapeDtypeStruct((rows, pixels), jnp.bfloat16),
    )(*tables, inv_noise[None, :])


def on_device(particles, defocus, inv_noise, references, part_class, part_rot, counts):
    local_rows = particles.shape[0]
    pixels = inv_noise.shape[0]
    owned = references.shape[0]
    rotations = references.shape[1]
    dom_size = lax.axis_size("dom")
    cls_size = lax.axis_size("cls")
    cls_index = lax.axis_index("cls")
    block_classes = dom_size * owned
    block_first = cls_index * block_classes
    own_first = (block_first + lax.axis_index("dom") * owned) * rotations

    images = lax.all_gather(references, "dom", axis=0, tiled=True)
    flat_images = images.reshape(block_classes * rotations, 2 * pixels)
    real_part = flat_images[:, :pixels].astype(jnp.float32)
    imag_part = flat_images[:, pixels:].astype(jnp.float32)
    power = (real_part * real_part + imag_part * imag_part).astype(jnp.bfloat16)

    weighted, power_weight = weighted_rows(particles, defocus, inv_noise)

    local_class = part_class - block_first
    in_block = (local_class >= 0) & (local_class < block_classes)
    pose = jnp.where(in_block, local_class * rotations + part_rot, -1)
    poses = jnp.arange(block_classes * rotations, dtype=jnp.int32)
    selector = (poses[:, None] == pose[None, :]).astype(jnp.bfloat16)
    partial = jnp.dot(selector, weighted, preferred_element_type=jnp.float32)
    numerator = lax.psum_scatter(partial, "dom", scatter_dimension=0, tiled=True)

    class_total = counts.shape[0]
    log_prior = jnp.log(
        (counts + 1).astype(jnp.float32) / (jnp.sum(counts) + class_total).astype(jnp.float32)
    )
    class_prior = lax.dynamic_slice_in_dim(log_prior, block_first, block_classes)
    score = lax.dot_general(
        weighted, flat_images, (((1,), (1,)), ((), ())), preferred_element_type=jnp.float32
    ) + lax.dot_general(
        power_weight, power * jnp.bfloat16(-0.5), (((1,), (1,)), ((), ())), preferred_element_type=jnp.float32
    )
    score = score + jnp.repeat(class_prior, rotations)[None, :]
    best_score = lax.pmax(jnp.max(score, axis=1), "cls")

    capacity = max(2, 3 * local_rows // (dom_size * cls_size))
    slots = dom_size * capacity
    every_defocus = lax.all_gather(defocus, "dom", axis=0, tiled=True)
    every_pose = lax.all_gather(part_class * rotations + part_rot, "dom", axis=0, tiled=True)
    own_pose = every_pose - own_first
    owned_here = (own_pose >= 0) & (own_pose < owned * rotations)
    running = jnp.cumsum(owned_here.astype(jnp.int32))
    slot_ids = jnp.arange(slots, dtype=jnp.int32)
    source = jnp.minimum(jnp.searchsorted(running, slot_ids + 1), every_pose.shape[0] - 1)
    filled = slot_ids < running[-1]
    slot_defocus = jnp.where(filled, jnp.take(every_defocus, source), 1.0)
    slot_pose = jnp.where(filled, jnp.take(own_pose, source), -1)
    slot_power = power_rows(slot_defocus, inv_noise)
    own_poses = jnp.arange(owned * rotations, dtype=jnp.int32)
    gather_own = (own_poses[:, None] == slot_pose[None, :]).astype(jnp.bfloat16)
    denominator = jnp.dot(gather_own, slot_power, preferred_element_type=jnp.float32)

    class_images = numerator / (jnp.concatenate([denominator, denominator], axis=1) + 1.0)
    return best_score, class_images.reshape(owned, rotations, 2 * pixels)


def solution(mesh):
    placed = (P("dom", None), P("dom"), P(), P(("cls", "dom"), None, None), P("dom"), P("dom"), P())
    return jax.shard_map(
        on_device,
        mesh=mesh,
        in_specs=placed,
        out_specs=(P("dom"), P(("cls", "dom"), None, None)),
        check_vma=False,
    )
```

time: 182 us -> 222 us (1.22)
  waiting for transfers between devices: 75.8 us -> 0.7 us
  local copies, waits for them, and re-layouts: 3.26 us -> 74.4 us
  blocking collectives: 11.7 us -> 40 us
  Pallas kernels: 24.1 us -> 33.7 us
  other arithmetic: 17.3 us -> 21.2 us
    reduce_scatter x1, waiting for transfers between devices: 75.1 us -> 0.01 us  [on_device(): lax.psum_scatter(partial, 'dom', scatter_dimension=0, tiled=True)]
    gather x0 -> x16, local copies, waits for them, and re-layouts: none -> 71.4 us  [the longest x14 62.5 us: on_device(): jnp.searchsorted(running, slot_ids + 1)]
    all_gather x0 -> x2, blocking collectives: none -> 29.5 us  [the longest x1 15.3 us: on_device(): lax.all_gather(part_class * rotations + part_rot, 'dom', axis=0, tiled=True)]
    pallas_call x1 -> x2, Pallas kernels: 24.1 us -> 33.7 us  [the longest x1 24.1 us: weighted_rows(): pl.pallas_call(weights_kernel, grid=(rows // block,), in_specs=table_spec...]
    mul x1 -> x0, other arithmetic: 4.18 us -> none  [on_device(): power * jnp.bfloat16(-0.5)]
    sin x1 -> x2, other arithmetic: 3.05 us -> 5.57 us  [contrast_tables(): jnp.sin(column_angle)]
    dot_general x2 -> x4, matrix products: 34.7 us -> 35.5 us  [the longest x1 13.1 us: on_device(): partial = jnp.dot(selector, weighted, preferred_element_type=jnp.float32)]
  transfers between devices with their start and end apart: 2 -> 2, of which waited for: 1 -> 0; matrix products, arithmetic and copies ran while one was open for 28% -> 58% of each run, Pallas kernels for 13% -> 15%
where the time goes in v6:
time: 222 us; the launch traced here: 221 us
  local copies, waits for them, and re-layouts  74.4 us (34%)
  blocking collectives  40 us (18%)
  matrix products  35.5 us (16%)
  Pallas kernels  33.7 us (15%)
  other arithmetic  21.2 us (10%)
  between operations  14.9 us (7%)
    gather x14, local copies, waits for them, and re-layouts, on_device(): jnp.searchsorted(running, slot_ids + 1)  62.5 us
    pallas_call x1, Pallas kernels, weighted_rows(): pl.pallas_call(weights_kernel, grid=(rows // block,), in_specs=table_spec...  24.1 us
    all_gather x1, blocking collectives, on_device(): lax.all_gather(part_class * rotations + part_rot, 'dom', axis=0, tiled=True)  15.3 us
    all_gather x1, blocking collectives, on_device(): every_defocus = lax.all_gather(defocus, 'dom', axis=0, tiled=True)  14.2 us
    dot_general x1, matrix products, on_device(): partial = jnp.dot(selector, weighted, preferred_element_type=jnp.float32)  13.1 us
    pmax x1, blocking collectives, on_device(): best_score = lax.pmax(jnp.max(score, axis=1), 'cls')  10.5 us
    dot_general x1, matrix products, on_device(): lax.dot_general(weighted, flat_images, (((1,), (1,)), ((), ())), preferre...  10.3 us
    pallas_call x1, Pallas kernels, power_rows(): pl.pallas_call(power_kernel, grid=(rows // block,), in_specs=table_specs(...  9.65 us
  transfers between devices with their start and end apart: 2, of which 0 were waited for; matrix products, arithmetic and copies ran while one was open for 58% of the time, Pallas kernels for 15%

profile of v6, /device:TPU:0, one launch (start us, length us, event | category | flops | bytes accessed | tf_op | source)
XLA Modules:
  0.0 221.3 jit_solution(12475942914214335740)
XLA Ops:
  19.5 24.1 %shard_map.86 = (bf16[1024,9216]{1,0:T(8,128)(2,1)}, bf16[1024,4608]{1,0:T(8,128)(2,1)}) custom-call(bf16[1024,256]{1,0:T(8,128)(2,1)} %get-tuple-element.121.row_sin_ref, bf16[1024,256]{1,0:T(8,128)(2,1)} %get-tuple-element.122.row_cos_ref, bf16[256,4608]{1,0:T(8,128)(2,1)} %and_convert_fusion.expand_ref, f32[1024,128]{1,0:T(8,128)} %get-tuple-element.114.col_cos_ref, ...), custom_call_target="tpu_custom_call" | custom-call | tf_op jit(solution)/shard_map/pallas_call | solution.py:92
  43.6 13.1 %fusion.24 = f32[192,9216]{1,0:T(8,128)} fusion(bf16[1024,9216]{1,0:T(8,128)(2,1)} %get-tuple-element.69, s32[1024]{0:T(1024)S(1)} %get-tuple-element.104), kind=kOutput, calls=%fused_computation.37 | convolution fusion | flops 3624075264 | bytes 25956352 | tf_op jit(solution)/shard_map/dot_general | solution.py:147
  58.9 15.3 %all_gather.10 = s32[8192]{0:T(1024)S(1)} all-gather(s32[1024]{0:T(1024)S(1)} %get-tuple-element.103), channel_id=1, replica_groups=mesh['dom'=8,'cls'=4] {'dom'}, dimensions={0}, use_global_device_ids=true | all-gather | bytes 36864 | tf_op jit(solution)/shard_map/all_gather | solution.py:166
  75.5 63.8 %while.24 = (s32[]{:T(128)}, u32[768]{0:T(1024)S(1)}, u32[768]{0:T(1024)S(1)}, s32[8192]{0:T(1024)S(1)}, s32[]{:T(128)}, /*index=5*/s32[]{:T(128)}, s32[]{}) while((s32[]{:T(128)}, u32[768]{0:T(1024)S(1)}, u32[768]{0:T(1024)S(1)}, s32[8192]{0:T(1024)S(1)}, s32[]{:T(128)}, /*index=5*/s32[]{:T(128)}, s32[]{}) %tuple.54), condition=%wide.region_7.8_spmd.clone, body=%wide.region_6.7_spmd.clone.sunk | while | flops 15620 | bytes 54893 | solution.py:171
  75.5 4.5 %gather_fusion = s32[768]{0:T(1024)S(1)} fusion(s32[8192]{0:T(1024)S(1)} %get-tuple-element.171, u32[1024]{0:T(1024)S(1)} %pad_clamp_fusion.3), kind=kCustom, calls=%fused_computation.clone.clone.1 | custom fusion | bytes 9216 | tf_op jit(solution)/shard_map/jit(searchsorted)/jit(_searchsorted_scan_impl)/vmap(jit(_searchsorted_scan_impl))/while/body/eval_jaxpr/gather | solution.py:171
  80.1 4.5 %gather_fusion = s32[768]{0:T(1024)S(1)} fusion(s32[8192]{0:T(1024)S(1)} %get-tuple-element.171, u32[1024]{0:T(1024)S(1)} %pad_clamp_fusion.3), kind=kCustom, calls=%fused_computation.clone.clone.1 | custom fusion | bytes 9216 | tf_op jit(solution)/shard_map/jit(searchsorted)/jit(_searchsorted_scan_impl)/vmap(jit(_searchsorted_scan_impl))/while/body/eval_jaxpr/gather | solution.py:171
  84.6 4.5 %gather_fusion = s32[768]{0:T(1024)S(1)} fusion(s32[8192]{0:T(1024)S(1)} %get-tuple-element.171, u32[1024]{0:T(1024)S(1)} %pad_clamp_fusion.3), kind=kCustom, calls=%fused_computation.clone.clone.1 | custom fusion | bytes 9216 | tf_op jit(solution)/shard_map/jit(searchsorted)/jit(_searchsorted_scan_impl)/vmap(jit(_searchsorted_scan_impl))/while/body/eval_jaxpr/gather | solution.py:171
  89.2 4.5 %gather_fusion = s32[768]{0:T(1024)S(1)} fusion(s32[8192]{0:T(1024)S(1)} %get-tuple-element.171, u32[1024]{0:T(1024)S(1)} %pad_clamp_fusion.3), kind=kCustom, calls=%fused_computation.clone.clone.1 | custom fusion | bytes 9216 | tf_op jit(solution)/shard_map/jit(searchsorted)/jit(_searchsorted_scan_impl)/vmap(jit(_searchsorted_scan_impl))/while/body/eval_jaxpr/gather | solution.py:171
  93.7 4.5 %gather_fusion = s32[768]{0:T(1024)S(1)} fusion(s32[8192]{0:T(1024)S(1)} %get-tuple-element.171, u32[1024]{0:T(1024)S(1)} %pad_clamp_fusion.3), kind=kCustom, calls=%fused_computation.clone.clone.1 | custom fusion | bytes 9216 | tf_op jit(solution)/shard_map/jit(searchsorted)/jit(_searchsorted_scan_impl)/vmap(jit(_searchsorted_scan_impl))/while/body/eval_jaxpr/gather | solution.py:171
  98.3 4.5 %gather_fusion = s32[768]{0:T(1024)S(1)} fusion(s32[8192]{0:T(1024)S(1)} %get-tuple-element.171, u32[1024]{0:T(1024)S(1)} %pad_clamp_fusion.3), kind=kCustom, calls=%fused_computation.clone.clone.1 | custom fusion | bytes 9216 | tf_op jit(solution)/shard_map/jit(searchsorted)/jit(_searchsorted_scan_impl)/vmap(jit(_searchsorted_scan_impl))/while/body/eval_jaxpr/gather | solution.py:171
  102.8 4.5 %gather_fusion = s32[768]{0:T(1024)S(1)} fusion(s32[8192]{0:T(1024)S(1)} %get-tuple-element.171, u32[1024]{0:T(1024)S(1)} %pad_clamp_fusion.3), kind=kCustom, calls=%fused_computation.clone.clone.1 | custom fusion | bytes 9216 | tf_op jit(solution)/shard_map/jit(searchsorted)/jit(_searchsorted_scan_impl)/vmap(jit(_searchsorted_scan_impl))/while/body/eval_jaxpr/gather | solution.py:171
  107.4 4.5 %gather_fusion = s32[768]{0:T(1024)S(1)} fusion(s32[8192]{0:T(1024)S(1)} %get-tuple-element.171, u32[1024]{0:T(1024)S(1)} %pad_clamp_fusion.3), kind=kCustom, calls=%fused_computation.clone.clone.1 | custom fusion | bytes 9216 | tf_op jit(solution)/shard_map/jit(searchsorted)/jit(_searchsorted_scan_impl)/vmap(jit(_searchsorted_scan_impl))/while/body/eval_jaxpr/gather | solution.py:171
  111.9 4.5 %gather_fusion = s32[768]{0:T(1024)S(1)} fusion(s32[8192]{0:T(1024)S(1)} %get-tuple-element.171, u32[1024]{0:T(1024)S(1)} %pad_clamp_fusion.3), kind=kCustom, calls=%fused_computation.clone.clone.1 | custom fusion | bytes 9216 | tf_op jit(solution)/shard_map/jit(searchsorted)/jit(_searchsorted_scan_impl)/vmap(jit(_searchsorted_scan_impl))/while/body/eval_jaxpr/gather | solution.py:171
  116.5 4.5 %gather_fusion = s32[768]{0:T(1024)S(1)} fusion(s32[8192]{0:T(1024)S(1)} %get-tuple-element.171, u32[1024]{0:T(1024)S(1)} %pad_clamp_fusion.3), kind=kCustom, calls=%fused_computation.clone.clone.1 | custom fusion | bytes 9216 | tf_op jit(solution)/shard_map/jit(searchsorted)/jit(_searchsorted_scan_impl)/vmap(jit(_searchsorted_scan_impl))/while/body/eval_jaxpr/gather | solution.py:171
  121.1 4.5 %gather_fusion = s32[768]{0:T(1024)S(1)} fusion(s32[8192]{0:T(1024)S(1)} %get-tuple-element.171, u32[1024]{0:T(1024)S(1)} %pad_clamp_fusion.3), kind=kCustom, calls=%fused_computation.clone.clone.1 | custom fusion | bytes 9216 | tf_op jit(solution)/shard_map/jit(searchsorted)/jit(_searchsorted_scan_impl)/vmap(jit(_searchsorted_scan_impl))/while/body/eval_jaxpr/gather | solution.py:171
  125.6 4.5 %gather_fusion = s32[768]{0:T(1024)S(1)} fusion(s32[8192]{0:T(1024)S(1)} %get-tuple-element.171, u32[1024]{0:T(1024)S(1)} %pad_clamp_fusion.3), kind=kCustom, calls=%fused_computation.clone.clone.1 | custom fusion | bytes 9216 | tf_op jit(solution)/shard_map/jit(searchsorted)/jit(_searchsorted_scan_impl)/vmap(jit(_searchsorted_scan_impl))/while/body/eval_jaxpr/gather | solution.py:171
  130.2 4.5 %gather_fusion = s32[768]{0:T(1024)S(1)} fusion(s32[8192]{0:T(1024)S(1)} %get-tuple-element.171, u32[1024]{0:T(1024)S(1)} %pad_clamp_fusion.3), kind=kCustom, calls=%fused_computation.clone.clone.1 | custom fusion | bytes 9216 | tf_op jit(solution)/shard_map/jit(searchsorted)/jit(_searchsorted_scan_impl)/vmap(jit(_searchsorted_scan_impl))/while/body/eval_jaxpr/gather | solution.py:171
  134.7 4.5 %gather_fusion = s32[768]{0:T(1024)S(1)} fusion(s32[8192]{0:T(1024)S(1)} %get-tuple-element.171, u32[1024]{0:T(1024)S(1)} %pad_clamp_fusion.3), kind=kCustom, calls=%fused_computation.clone.clone.1 | custom fusion | bytes 9216 | tf_op jit(solution)/shard_map/jit(searchsorted)/jit(_searchsorted_scan_impl)/vmap(jit(_searchsorted_scan_impl))/while/body/eval_jaxpr/gather | solution.py:171
  139.3 4.5 %gather_fusion.1 = s32[768]{0:T(1024)S(1)} fusion(s32[8192]{0:T(1024)S(1)} %get-tuple-element.102, s32[1024]{0:T(1024)S(1)} %pad_clamp_fusion.1), kind=kCustom, calls=%fused_computation.1 | custom fusion | bytes 9216 | tf_op jit(solution)/shard_map/jit(_take)/gather | solution.py:174
  143.8 14.2 %all_gather.11 = f32[8192]{0:T(1024)S(1)} all-gather(f32[1024]{0:T(1024)S(1)} %copy-done), channel_id=1, replica_groups=mesh['dom'=8,'cls'=4] {'dom'}, dimensions={0}, use_global_device_ids=true | all-gather | bytes 36864 | tf_op jit(solution)/shard_map/all_gather | solution.py:165
  169.6 9.7 %shard_map.87 = bf16[768,4608]{1,0:T(8,128)(2,1)} custom-call(bf16[768,256]{1,0:T(8,128)(2,1)} %get-tuple-element.123.row_sin_ref, bf16[768,256]{1,0:T(8,128)(2,1)} %get-tuple-element.124.row_cos_ref, bf16[256,4608]{1,0:T(8,128)(2,1)} %and_convert_fusion.expand_ref, f32[768,128]{1,0:T(8,128)} %get-tuple-element.106.col_cos_ref, ...), custom_call_target="tpu_custom_call" | custom-call | tf_op jit(solution)/shard_map/pallas_call | solution.py:113
  183.3 8.1 %fusion.3 = f32[1024,192]{0,1:T(8,128)S(1)} fusion(bf16[1024,4608]{1,0:T(8,128)(2,1)} %get-tuple-element.70, bf16[192,9216]{1,0:T(8,128)(2,1)} %bitcast.14), kind=kOutput, calls=%fused_computation.12 | convolution fusion | flops 1818132480 | bytes 13762560 | tf_op jit(solution)/shard_map/dot_general | solution.py:157
  191.4 10.3 %fusion.8 = f32[1024]{0:T(1024)S(1)} fusion(f32[1024,192]{0,1:T(8,128)S(1)} %fusion.3, bf16[1024,9216]{1,0:T(8,128)(2,1)} %get-tuple-element.69, f32[192]{0:T(256)S(1)} %add.144, bf16[24,8,9216]{2,1,0:T(8,128)(2,1)S(1)} %copy-done.3), kind=kOutput, calls=%fused_computation.17 | convolution fusion | flops 3624467456 | bytes 23204608 | tf_op jit(solution)/shard_map/dot_general | solution.py:155
  201.7 10.5 %pmax.7 = f32[1024]{0:T(1024)} all-reduce(f32[1024]{0:T(1024)S(1)} %fusion.8), channel_id=1, replica_groups=mesh['dom'=8,'cls'=4] {'cls'}, use_global_device_ids=true, to_apply=%region_2.3 | all-reduce | flops 1024 | bytes 8192 | tf_op jit(solution)/shard_map/pmax | solution.py:161
  (122 shorter events, 33.5 us)
Async XLA Ops:
  7.2 176.1 %all-gather.2.cloned.1.call-start = ((), (), s32[]{:S(2)}) async-start(), calls=%async_computation.1 | async-start | bytes 3981312 | tf_op jit(solution)/shard_map/all_gather | solution.py:134
  7.9 204.2 %reduce-scatter.2.cloned.1.call-start = ((), (), s32[]{:S(2)}) async-start(), calls=%async_computation.2 | async-start | bytes 7962624 | tf_op jit(solution)/shard_map/reduce_scatter | solution.py:148
  19.5 24.1 %copy-start.1 = (s32[1024]{0:T(1024)S(1)}, s32[1024]{0:T(1024)}, u32[]{:S(2)}) copy-start(s32[1024]{0:T(1024)} %param.14) | copy-start | bytes 12292
  19.5 24.1 %copy-start.2 = (s32[1024]{0:T(1024)S(1)}, s32[1024]{0:T(1024)}, u32[]{:S(2)}) copy-start(s32[1024]{0:T(1024)} %param.13) | copy-start | bytes 12292
  56.7 0.7 copy-start.4
  139.3 4.5 %copy-start = (f32[1024]{0:T(1024)S(1)}, f32[1024]{0:T(1024)}, u32[]{:S(2)}) copy-start(f32[1024]{0:T(1024)} %param.10) | copy-start | bytes 12292
  183.3 8.1 %copy-start.3 = (bf16[24,8,9216]{2,1,0:T(8,128)(2,1)S(1)}, bf16[24,8,9216]{2,1,0:T(8,128)(2,1)}, u32[]{:S(2)}) copy-start(bf16[24,8,9216]{2,1,0:T(8,128)(2,1)} %all-gather.2.cloned.1.call-done) | copy-start | bytes 10616836
Sparse Core Ops, SparseCore 0:
  9.6 44.2 all-gather.1
  56.9 79.7 reduce-scatter.1

commit v7 on v6

--- a/solution.py
+++ b/solution.py
@@ -129,17 +129,27 @@
     cls_index = lax.axis_index("cls")
     block_classes = dom_size * owned
     block_first = cls_index * block_classes
-    own_first = (block_first + lax.axis_index("dom") * owned) * rotations
-
-    images = lax.all_gather(references, "dom", axis=0, tiled=True)
-    flat_images = images.reshape(block_classes * rotations, 2 * pixels)
+
+    local_class = part_class - block_first
+    facts = split_pieces(defocus[None, :], 3 * local_rows).reshape(3, local_rows)
+    block_class = jnp.clip(local_class, -1, block_classes).astype(jnp.bfloat16)
+    facts = jnp.concatenate([facts, block_class[None, :], part_rot.astype(jnp.bfloat16)[None, :]], axis=0)
+    extra_rows = -(-facts.size // (2 * pixels))
+    facts = jnp.pad(facts.reshape(-1), (0, extra_rows * 2 * pixels - facts.size))
+    ref_rows = owned * rotations
+    sending = jnp.concatenate(
+        [references.reshape(ref_rows, 2 * pixels), facts.reshape(extra_rows, 2 * pixels)], axis=0
+    )
+    gathered = lax.all_gather(sending, "dom", axis=0, tiled=False)
+    flat_images = gathered[:, :ref_rows].reshape(block_classes * rotations, 2 * pixels)
+    every_fact = gathered[:, ref_rows:].reshape(dom_size, -1)[:, : 5 * local_rows]
+    every_fact = every_fact.reshape(dom_size, 5, local_rows).transpose(1, 0, 2).reshape(5, dom_size * local_rows)
     real_part = flat_images[:, :pixels].astype(jnp.float32)
     imag_part = flat_images[:, pixels:].astype(jnp.float32)
     power = (real_part * real_part + imag_part * imag_part).astype(jnp.bfloat16)
 
     weighted, power_weight = weighted_rows(particles, defocus, inv_noise)
 
-    local_class = part_class - block_first
     in_block = (local_class >= 0) & (local_class < block_classes)
     pose = jnp.where(in_block, local_class * rotations + part_rot, -1)
     poses = jnp.arange(block_classes * rotations, dtype=jnp.int32)
@@ -162,16 +172,19 @@
 
     capacity = max(2, 3 * local_rows // (dom_size * cls_size))
     slots = dom_size * capacity
-    every_defocus = lax.all_gather(defocus, "dom", axis=0, tiled=True)
-    every_pose = lax.all_gather(part_class * rotations + part_rot, "dom", axis=0, tiled=True)
-    own_pose = every_pose - own_first
-    owned_here = (own_pose >= 0) & (own_pose < owned * rotations)
+    fact_class = every_fact[3].astype(jnp.float32).astype(jnp.int32) - lax.axis_index("dom") * owned
+    owned_here = (fact_class >= 0) & (fact_class < owned)
     running = jnp.cumsum(owned_here.astype(jnp.int32))
+    slot_of = jnp.where(owned_here, running - 1, -1)
     slot_ids = jnp.arange(slots, dtype=jnp.int32)
-    source = jnp.minimum(jnp.searchsorted(running, slot_ids + 1), every_pose.shape[0] - 1)
+    picker = (slot_ids[:, None] == slot_of[None, :]).astype(jnp.bfloat16)
+    picked = lax.dot_general(
+        every_fact, picker, (((1,), (1,)), ((), ())), preferred_element_type=jnp.float32
+    )
     filled = slot_ids < running[-1]
-    slot_defocus = jnp.where(filled, jnp.take(every_defocus, source), 1.0)
-    slot_pose = jnp.where(filled, jnp.take(own_pose, source), -1)
+    slot_defocus = jnp.where(filled, (picked[0] + picked[1]) + picked[2], 1.0)
+    slot_pose = picked[3].astype(jnp.int32) - lax.axis_index("dom") * owned
+    slot_pose = jnp.where(filled, slot_pose * rotations + picked[4].astype(jnp.int32), -1)
     slot_power = power_rows(slot_defocus, inv_noise)
     own_poses = jnp.arange(owned * rotations, dtype=jnp.int32)
     gather_own = (own_poses[:, None] == slot_pose[None, :]).astype(jnp.bfloat16)

time: 222 us -> 154 us (0.69)
  local copies, waits for them, and re-layouts: 74.4 us -> 6.93 us
  blocking collectives: 40 us -> 10.4 us
  waiting for transfers between devices: 0.7 us -> 24.4 us
  matrix products: 35.5 us -> 39.1 us
    gather x16 -> x0, local copies, waits for them, and re-layouts: 71.4 us -> none  [the longest x14 62.5 us: on_device(): jnp.searchsorted(running, slot_ids + 1)]
    all_gather x2 -> x0, blocking collectives: 29.5 us -> none  [the longest x1 15.3 us: on_device(): lax.all_gather(part_class * rotations + part_rot, 'dom', axis=0, tiled=True)]
    reduce_scatter x1, waiting for transfers between devices: 0.01 us -> 20 us  [on_device(): lax.psum_scatter(partial, 'dom', scatter_dimension=0, tiled=True)]
    dot_general x0 -> x1, matrix products: none -> 4.46 us  [on_device(): lax.dot_general(every_fact, picker, (((1,), (1,)), ((), ())), preferred_e...]
    all_gather x1, waiting for transfers between devices: 0.01 us -> 4.34 us  [on_device(): gathered = lax.all_gather(sending, 'dom', axis=0, tiled=False)]
    slice x1 -> x4, local copies, waits for them, and re-layouts: 0.08 us -> 3.78 us  [the longest x1 2.27 us: on_device(): gathered[:, :ref_rows].reshape(block_classes * rotations, 2 * pixels)]
    convert_element_type x2 -> x3, other arithmetic: 4.33 us -> 5.05 us  [split_pieces(): pieces.append(piece.astype(jnp.bfloat16))]
  transfers between devices with their start and end apart: 2 -> 2, of which waited for: 0 -> 2; matrix products, arithmetic and copies ran while one was open for 58% -> 41% of each run, Pallas kernels for 15% -> 22%
where the time goes in v7:
time: 154 us; the launch traced here: 153 us
  matrix products  39.1 us (25%)
  Pallas kernels  33.7 us (22%)
  waiting for transfers between devices  24.4 us (16%)
  other arithmetic  23.3 us (15%)
  between operations  14.9 us (10%)
  blocking collectives  10.4 us (7%)
  local copies, waits for them, and re-layouts  6.93 us (4%)
    pallas_call x1, Pallas kernels, weighted_rows(): pl.pallas_call(weights_kernel, grid=(rows // block,), in_specs=table_spec...  24 us
    reduce_scatter x1, waiting for transfers between devices, on_device(): lax.psum_scatter(partial, 'dom', scatter_dimension=0, tiled=True)  20 us
    dot_general x1, matrix products, on_device(): partial = jnp.dot(selector, weighted, preferred_element_type=jnp.float32)  13.2 us
    pmax x1, blocking collectives, on_device(): best_score = lax.pmax(jnp.max(score, axis=1), 'cls')  10.4 us
    dot_general x1, matrix products, on_device(): lax.dot_general(weighted, flat_images, (((1,), (1,)), ((), ())), preferre...  10.4 us
    pallas_call x1, Pallas kernels, power_rows(): pl.pallas_call(power_kernel, grid=(rows // block,), in_specs=table_specs(...  9.73 us
    dot_general x1, matrix products, on_device(): lax.dot_general(power_weight, power * jnp.bfloat16(-0.5), (((1,), (1,)),...  7.03 us
    sin x2, other arithmetic, contrast_tables(): jnp.sin(column_angle)  5.57 us
  transfers between devices with their start and end apart: 2, of which 2 were waited for; matrix products, arithmetic and copies ran while one was open for 41% of the time, Pallas kernels for 22%

profile of v7, /device:TPU:0, one launch (start us, length us, event | category | flops | bytes accessed | tf_op | source)
XLA Modules:
  0.0 152.8 jit_solution(1293035199103260127)
XLA Ops:
  7.2 0.8 add_select_fusion.2
  8.0 0.7 reduce-precision_convert_fusion.9
  8.9 1.9 %maximum_bitcast_fusion = bf16[1,25,9216]{2,1,0:T(8,128)(2,1)} fusion(bf16[1,9216]{1,0:T(2,128)(2,1)S(1)} %reshape.181, bf16[24,9216]{1,0:T(8,128)(2,1)} %bitcast.30), kind=kLoop, calls=%fused_computation.42 | loop fusion | flops 921600 | bytes 921600
  10.9 1.3 broadcast_in_dim.18.noise_ref
  12.3 2.5 %reduce-precision_convert_fusion.1 = (bf16[1024,72]{1,0:T(8,128)(2,1)S(1)}, bf16[1024,72]{1,0:T(8,128)(2,1)S(1)}, bf16[1024,72]{1,0:T(8,128)(2,1)S(1)}, bf16[102...) fusion(f32[1024]{0:T(1024)S(1)} %get-tuple-element.31, ...), kind=kLoop, calls=%fused_computation.35 | loop fusion | flops 1400832 | bytes 889120 | tf_op jit(solution)/shard_map/convert_element_type | solution.py:19
  14.8 1.6 %fusion.32 = (bf16[1024,256]{1,0:T(8,128)(2,1)}, bf16[1024,256]{1,0:T(8,128)(2,1)}) fusion(bf16[1024,72]{1,0:T(8,128)(2,1)S(1)} %get-tuple-element.22, bf16[1024,72]{1,0:T(8,128)(2,1)S(1)} %get-tuple-element.21, bf16[1024,72]{1,0:T(8,128)(2,1)S(1)} %get-tuple-element.25, bf16[1024,72]{1,0:T(8,128)(2,1)S(1)} %get-tuple-element.24, ...), kind=kLoop, calls=%fused_computation.60 | loop fusion | flops 4980736 | bytes 1933312 | tf_op jit(solution)/shard_map/concatenate | solution.py:21
  16.4 3.1 %fusion.35 = (f32[1024,128]{1,0:T(8,128)}, f32[1024,128]{1,0:T(8,128)}) fusion(f32[128]{0:T(128)S(1)} %fusion.67, f32[1024]{0:T(1024)S(1)} %get-tuple-element.31), kind=kLoop, calls=%fused_computation.64 | loop fusion | flops 262144 | bytes 1053184 | tf_op jit(solution)/shard_map/sin | solution.py:38
  19.5 2.2 %and_convert_fusion.expand_ref = bf16[256,4608]{1,0:T(8,128)(2,1)} fusion(s32[4608]{0:T(1024)S(1)} %add_select_fusion.1, s32[256]{0:T(256)S(1)} %and_select_fusion.1, pred[256]{0:T(512)(128)(4,1)S(1)} %iota_compare_fusion.9), kind=kLoop, calls=%fused_computation.3 | loop fusion | flops 3538944 | bytes 2379008 | tf_op jit(solution)/shard_map/convert_element_type | solution.py:37
  21.7 24.0 %shard_map.86 = (bf16[1024,9216]{1,0:T(8,128)(2,1)}, bf16[1024,4608]{1,0:T(8,128)(2,1)}) custom-call(bf16[1024,256]{1,0:T(8,128)(2,1)} %get-tuple-element.33.row_sin_ref, bf16[1024,256]{1,0:T(8,128)(2,1)} %get-tuple-element.34.row_cos_ref, bf16[256,4608]{1,0:T(8,128)(2,1)} %and_convert_fusion.expand_ref, f32[1024,128]{1,0:T(8,128)} %get-tuple-element.19.col_cos_ref, ...), custom_call_target="tpu_custom_call" | custom-call | tf_op jit(solution)/shard_map/pallas_call | solution.py:92
  45.7 13.2 %fusion.24 = f32[192,9216]{1,0:T(8,128)} fusion(bf16[1024,9216]{1,0:T(8,128)(2,1)} %get-tuple-element.4, s32[1024]{0:T(1024)S(1)} %get-tuple-element.26), kind=kOutput, calls=%fused_computation.31 | convolution fusion | flops 3624075264 | bytes 25956352 | tf_op jit(solution)/shard_map/dot_general | solution.py:157
  61.0 4.3 %all-gather.4.cloned.1.call-done = bf16[8,25,9216]{2,1,0:T(8,128)(2,1)} async-done(((bf16[1,25,9216]{2,1,0:T(8,128)(2,1)}), bf16[8,25,9216]{2,1,0:T(8,128)(2,1)}) %all-gather.4.cloned.1.call-update) | async-done | bytes 3686416 | tf_op jit(solution)/shard_map/all_gather | solution.py:143
  65.4 1.4 slice.61
  68.3 4.5 %fusion = f32[5,768]{1,0:T(8,128)S(1)} fusion(bf16[5,8192]{1,0:T(8,128)(2,1)S(1)} %bitcast.34, s32[8192]{0:T(1024)S(1)} %get-tuple-element.6), kind=kOutput, calls=%fused_computation.1 | convolution fusion | flops 69206016 | bytes 130048 | tf_op jit(solution)/shard_map/dot_general | solution.py:181
  73.4 1.9 %reduce-precision_convert_fusion.5 = (bf16[768,72]{1,0:T(8,128)(2,1)S(1)}, bf16[768,72]{1,0:T(8,128)(2,1)S(1)}, bf16[768,72]{1,0:T(8,128)(2,1)S(1)}, bf16[768,72...) fusion(f32[768]{0:T(1024)S(1)} %select_multiply_fusion, f32[72]{0:T(128)S(1)} %multiply_multiply_fusion), kind=kLoop, calls=%fused_computation.46 | loop fusion | flops 1050624 | bytes 666912 | tf_op jit(solution)/shard_map/convert_element_type | solution.py:19
  75.2 1.4 fusion.44
  76.6 2.5 %fusion.47 = (f32[768,128]{1,0:T(8,128)}, f32[768,128]{1,0:T(8,128)}) fusion(f32[128]{0:T(128)S(1)} %fusion.67, f32[768]{0:T(1024)S(1)} %select_multiply_fusion), kind=kLoop, calls=%fused_computation.77 | loop fusion | flops 196608 | bytes 790016 | tf_op jit(solution)/shard_map/sin | solution.py:38
  79.1 9.7 %shard_map.87 = bf16[768,4608]{1,0:T(8,128)(2,1)} custom-call(bf16[768,256]{1,0:T(8,128)(2,1)} %get-tuple-element.35.row_sin_ref, bf16[768,256]{1,0:T(8,128)(2,1)} %get-tuple-element.36.row_cos_ref, bf16[256,4608]{1,0:T(8,128)(2,1)} %and_convert_fusion.expand_ref, f32[768,128]{1,0:T(8,128)} %get-tuple-element.11.col_cos_ref, ...), custom_call_target="tpu_custom_call" | custom-call | tf_op jit(solution)/shard_map/pallas_call | solution.py:113
  88.9 2.3 %slice.58 = bf16[8,24,9216]{2,1,0:T(8,128)(2,1)S(1)} slice(bf16[8,25,9216]{2,1,0:T(8,128)(2,1)} %all-gather.4.cloned.1.call-done), slice={[0:8], [0:24], [0:9216]} | slice | bytes 7077888 | tf_op jit(solution)/shard_map/slice | solution.py:144
  91.1 7.0 %fusion.3 = f32[1024,192]{0,1:T(8,128)S(1)} fusion(bf16[1024,4608]{1,0:T(8,128)(2,1)} %get-tuple-element.5, bf16[192,9216]{1,0:T(8,128)(2,1)S(1)} %bitcast.28), kind=kOutput, calls=%fused_computation.6 | convolution fusion | flops 1818132480 | bytes 13762560 | tf_op jit(solution)/shard_map/dot_general | solution.py:167
  98.2 10.4 %fusion.8 = f32[1024]{0:T(1024)S(1)} fusion(f32[1024,192]{0,1:T(8,128)S(1)} %fusion.3, bf16[1024,9216]{1,0:T(8,128)(2,1)} %get-tuple-element.4, bf16[192,9216]{1,0:T(8,128)(2,1)S(1)} %bitcast.29, f32[192]{0:T(256)S(1)} %add.137), kind=kOutput, calls=%fused_computation.11 | convolution fusion | flops 3624467456 | bytes 23204608 | tf_op jit(solution)/shard_map/dot_general | solution.py:165
  108.6 10.4 %pmax.7 = f32[1024]{0:T(1024)} all-reduce(f32[1024]{0:T(1024)S(1)} %fusion.8), channel_id=1, replica_groups=mesh['dom'=8,'cls'=4] {'cls'}, use_global_device_ids=true, to_apply=%region_2.3 | all-reduce | flops 1024 | bytes 8192 | tf_op jit(solution)/shard_map/pmax | solution.py:171
  119.7 4.1 %fusion.50 = f32[24,4608]{1,0:T(8,128)S(1)} fusion(bf16[768,4608]{1,0:T(8,128)(2,1)} %shard_map.87, s32[768]{0:T(1024)S(1)} %fusion.60), kind=kOutput, calls=%fused_computation.82 | convolution fusion | flops 169887744 | bytes 7523328 | tf_op jit(solution)/shard_map/dot_general | solution.py:191
  123.8 20.0 %reduce-scatter.2.cloned.1.call-done = f32[24,9216]{1,0:T(8,128)} async-done(((f32[192,9216]{1,0:T(8,128)}), f32[24,9216]{1,0:T(8,128)}) %reduce-scatter.2.cloned.1.call-update) | async-done | bytes 884752 | tf_op jit(solution)/shard_map/reduce_scatter | solution.py:158
  143.8 2.2 %fusion.16 = f32[3,8,9216]{2,1,0:T(8,128)} fusion(f32[24,9216]{1,0:T(8,128)} %reduce-scatter.2.cloned.1.call-done, f32[24,4608]{1,0:T(8,128)S(1)} %fusion.50), kind=kLoop, calls=%fused_computation.21 | loop fusion | flops 663552 | bytes 2211840 | tf_op jit(solution)/shard_map/reshape | solution.py:194
  (41 shorter events, 4.5 us)
Async XLA Ops:
  7.2 58.2 %all-gather.4.cloned.1.call-start = ((), (), s32[]{:S(2)}) async-start(), calls=%async_computation.2 | async-start | bytes 5308416 | tf_op jit(solution)/shard_map/all_gather | solution.py:143
  10.8 133.0 %reduce-scatter.2.cloned.1.call-start = ((), (), s32[]{:S(2)}) async-start(), calls=%async_computation.1 | async-start | bytes 7962624 | tf_op jit(solution)/shard_map/reduce_scatter | solution.py:158
  58.8 0.7 copy-start
Sparse Core Ops, SparseCore 0:
  10.9 54.4 all-gather.3
  67.7 76.0 reduce-scatter.1

commit v8 on v7

--- a/solution.py
+++ b/solution.py
@@ -43,7 +43,10 @@
     return row_sin[:, lanes] * col_cos + row_cos[:, lanes] * col_sin
 
 
-def weights_kernel(row_sin_ref, row_cos_ref, expand_ref, col_cos_ref, col_sin_ref, noise_ref, particles_ref, out_ref, power_ref):
+def weights_kernel(
+    row_sin_ref, row_cos_ref, expand_ref, col_cos_ref, col_sin_ref, noise_ref, particles_ref, selector_ref,
+    out_ref, power_ref, sums_ref,
+):
     pixels = noise_ref.shape[1]
     row_sin = jnp.dot(row_sin_ref[...], expand_ref[...], preferred_element_type=jnp.float32)
     row_cos = jnp.dot(row_cos_ref[...], expand_ref[...], preferred_element_type=jnp.float32)
@@ -58,6 +61,12 @@
         out_ref[:, imag] = (particles_ref[:, imag].astype(jnp.float32) * factor).astype(jnp.bfloat16)
         power_ref[:, lanes] = (factor * contrast_rows).astype(jnp.bfloat16)
 
+    @pl.when(pl.program_id(0) == 0)
+    def _():
+        sums_ref[...] = jnp.zeros_like(sums_ref)
+
+    sums_ref[...] += jnp.dot(selector_ref[...], out_ref[...], preferred_element_type=jnp.float32)
+
 
 def power_kernel(row_sin_ref, row_cos_ref, expand_ref, col_cos_ref, col_sin_ref, noise_ref, power_ref):
     pixels = noise_ref.shape[1]
@@ -83,8 +92,9 @@
     ]
 
 
-def weighted_rows(particles, defocus, inv_noise):
+def weighted_rows(particles, defocus, inv_noise, selector):
     rows = particles.shape[0]
+    poses = selector.shape[0]
     pixels = inv_noise.shape[0]
     block = min(ROW_BLOCK, rows)
     tables = contrast_tables(defocus, pixels)
@@ -92,16 +102,19 @@
     return pl.pallas_call(
         weights_kernel,
         grid=(rows // block,),
-        in_specs=table_specs(block, width, pixels) + [pl.BlockSpec((block, 2 * pixels), lambda i: (i, 0))],
+        in_specs=table_specs(block, width, pixels)
+        + [pl.BlockSpec((block, 2 * pixels), lambda i: (i, 0)), pl.BlockSpec((poses, block), lambda i: (0, i))],
         out_specs=[
             pl.BlockSpec((block, 2 * pixels), lambda i: (i, 0)),
             pl.BlockSpec((block, pixels), lambda i: (i, 0)),
+            pl.BlockSpec((poses, 2 * pixels), lambda i: (0, 0)),
         ],
         out_shape=[
             jax.ShapeDtypeStruct((rows, 2 * pixels), jnp.bfloat16),
             jax.ShapeDtypeStruct((rows, pixels), jnp.bfloat16),
+            jax.ShapeDtypeStruct((poses, 2 * pixels), jnp.float32),
         ],
-    )(*tables, inv_noise[None, :], particles)
+    )(*tables, inv_noise[None, :], particles, selector)
 
 
 def power_rows(defocus, inv_noise):
@@ -148,13 +161,11 @@
     imag_part = flat_images[:, pixels:].astype(jnp.float32)
     power = (real_part * real_part + imag_part * imag_part).astype(jnp.bfloat16)
 
-    weighted, power_weight = weighted_rows(particles, defocus, inv_noise)
-
     in_block = (local_class >= 0) & (local_class < block_classes)
     pose = jnp.where(in_block, local_class * rotations + part_rot, -1)
     poses = jnp.arange(block_classes * rotations, dtype=jnp.int32)
     selector = (poses[:, None] == pose[None, :]).astype(jnp.bfloat16)
-    partial = jnp.dot(selector, weighted, preferred_element_type=jnp.float32)
+    weighted, power_weight, partial = weighted_rows(particles, defocus, inv_noise, selector)
     numerator = lax.psum_scatter(partial, "dom", scatter_dimension=0, tiled=True)
 
     class_total = counts.shape[0]

time: 154 us -> 154 us (level)
  matrix products: 39.1 us -> 25.9 us
  waiting for transfers between devices: 24.4 us -> 33.6 us
  Pallas kernels: 33.7 us -> 36.7 us
    dot_general x1 -> x0, matrix products: 13.2 us -> none  [on_device(): partial = jnp.dot(selector, weighted, preferred_element_type=jnp.float32)]
    all_gather x1, waiting for transfers between devices: 4.34 us -> 13.8 us  [on_device(): gathered = lax.all_gather(sending, 'dom', axis=0, tiled=False)]
    pallas_call x1, Pallas kernels: 24 us -> 27 us  [weighted_rows(): pl.pallas_call(weights_kernel, grid=(rows // block,), in_specs=table_spec...]
    convert_element_type x0 -> x2, other arithmetic: none -> 1.6 us  [the longest x1 0.83 us: on_device(): selector = (poses[:, None] == pose[None, :]).astype(jnp.bfloat16)]
  transfers between devices with their start and end apart: 2 -> 2, of which waited for: 2 -> 2; matrix products, arithmetic and copies ran while one was open for 41% -> 33% of each run, Pallas kernels for 22% -> 24%
where the time goes in v8:
time: 154 us; the launch traced here: 153 us
  Pallas kernels  36.7 us (24%)
  waiting for transfers between devices  33.6 us (22%)
  matrix products  25.9 us (17%)
  other arithmetic  24.2 us (16%)
  between operations  14.9 us (10%)
  blocking collectives  10.4 us (7%)
  local copies, waits for them, and re-layouts  6.9 us (4%)
    pallas_call x1, Pallas kernels, weighted_rows(): pl.pallas_call(weights_kernel, grid=(rows // block,), in_specs=table_spec...  27 us
    reduce_scatter x1, waiting for transfers between devices, on_device(): lax.psum_scatter(partial, 'dom', scatter_dimension=0, tiled=True)  19.9 us
    all_gather x1, waiting for transfers between devices, on_device(): gathered = lax.all_gather(sending, 'dom', axis=0, tiled=False)  13.8 us
    pmax x1, blocking collectives, on_device(): best_score = lax.pmax(jnp.max(score, axis=1), 'cls')  10.4 us
    dot_general x1, matrix products, on_device(): lax.dot_general(weighted, flat_images, (((1,), (1,)), ((), ())), preferre...  10.4 us
    pallas_call x1, Pallas kernels, power_rows(): pl.pallas_call(power_kernel, grid=(rows // block,), in_specs=table_specs(...  9.72 us
    dot_general x1, matrix products, on_device(): lax.dot_general(power_weight, power * jnp.bfloat16(-0.5), (((1,), (1,)),...  7.03 us
    sin x2, other arithmetic, contrast_tables(): jnp.sin(column_angle)  5.54 us
  transfers between devices with their start and end apart: 2, of which 2 were waited for; matrix products, arithmetic and copies ran while one was open for 33% of the time, Pallas kernels for 24%

profile of v8, /device:TPU:0, one launch (start us, length us, event | category | flops | bytes accessed | tf_op | source)
XLA Modules:
  0.0 152.8 jit_solution(706918634252532571)
XLA Ops:
  7.2 0.8 clamp_convert_fusion
  8.0 0.7 reduce-precision_convert_fusion.9
  8.9 1.9 %maximum_bitcast_fusion = bf16[1,25,9216]{2,1,0:T(8,128)(2,1)} fusion(bf16[1,9216]{1,0:T(2,128)(2,1)S(1)} %reshape.181, bf16[24,9216]{1,0:T(8,128)(2,1)} %bitcast.29), kind=kLoop, calls=%fused_computation.42 | loop fusion | flops 921600 | bytes 921600
  10.9 1.3 broadcast_in_dim.21.noise_ref
  12.3 2.5 %reduce-precision_convert_fusion.1 = (bf16[1024,72]{1,0:T(8,128)(2,1)S(1)}, bf16[1024,72]{1,0:T(8,128)(2,1)S(1)}, bf16[1024,72]{1,0:T(8,128)(2,1)S(1)}, bf16[102...) fusion(f32[1024]{0:T(1024)S(1)} %get-tuple-element.30, ...), kind=kLoop, calls=%fused_computation.35 | loop fusion | flops 1400832 | bytes 889120 | tf_op jit(solution)/shard_map/convert_element_type | solution.py:19
  14.8 1.6 %fusion.32 = (bf16[1024,256]{1,0:T(8,128)(2,1)}, bf16[1024,256]{1,0:T(8,128)(2,1)}) fusion(bf16[1024,72]{1,0:T(8,128)(2,1)S(1)} %get-tuple-element.24, bf16[1024,72]{1,0:T(8,128)(2,1)S(1)} %get-tuple-element.23, bf16[1024,72]{1,0:T(8,128)(2,1)S(1)} %get-tuple-element.27, bf16[1024,72]{1,0:T(8,128)(2,1)S(1)} %get-tuple-element.26, ...), kind=kLoop, calls=%fused_computation.60 | loop fusion | flops 4980736 | bytes 1933312 | tf_op jit(solution)/shard_map/concatenate | solution.py:21
  16.4 0.8 fusion.24.selector_ref
  17.2 3.0 %fusion.35 = (f32[1024,128]{1,0:T(8,128)}, f32[1024,128]{1,0:T(8,128)}) fusion(f32[128]{0:T(128)S(1)} %fusion.66, f32[1024]{0:T(1024)S(1)} %get-tuple-element.30), kind=kLoop, calls=%fused_computation.64 | loop fusion | flops 262144 | bytes 1053184 | tf_op jit(solution)/shard_map/sin | solution.py:38
  20.3 2.2 %and_convert_fusion.expand_ref = bf16[256,4608]{1,0:T(8,128)(2,1)} fusion(s32[4608]{0:T(1024)S(1)} %add_select_fusion.1, s32[256]{0:T(256)S(1)} %and_select_fusion.1, pred[256]{0:T(512)(128)(4,1)S(1)} %iota_compare_fusion.8), kind=kLoop, calls=%fused_computation.3 | loop fusion | flops 3538944 | bytes 2379008 | tf_op jit(solution)/shard_map/convert_element_type | solution.py:37
  22.5 27.0 %shard_map.86 = (bf16[1024,9216]{1,0:T(8,128)(2,1)}, bf16[1024,4608]{1,0:T(8,128)(2,1)}, f32[192,9216]{1,0:T(8,128)}) custom-call(bf16[1024,256]{1,0:T(8,128)(2,1)} %get-tuple-element.35.row_sin_ref, bf16[1024,256]{1,0:T(8,128)(2,1)} %get-tuple-element.36.row_cos_ref, bf16[256,4608]{1,0:T(8,128)(2,1)} %and_convert_fusion.expand_ref, ...), custom_call_target="tpu_custom_call" | custom-call | tf_op jit(solution)/shard_map/pallas_call | solution.py:102
  51.7 13.8 %all-gather.4.cloned.1.call-done = bf16[8,25,9216]{2,1,0:T(8,128)(2,1)} async-done(((bf16[1,25,9216]{2,1,0:T(8,128)(2,1)}), bf16[8,25,9216]{2,1,0:T(8,128)(2,1)}) %all-gather.4.cloned.1.call-update) | async-done | bytes 3686416 | tf_op jit(solution)/shard_map/all_gather | solution.py:156
  65.4 1.4 slice.61
  68.3 4.5 %fusion = f32[5,768]{1,0:T(8,128)S(1)} fusion(bf16[5,8192]{1,0:T(8,128)(2,1)S(1)} %bitcast.33, s32[8192]{0:T(1024)S(1)} %get-tuple-element.8), kind=kOutput, calls=%fused_computation.1 | convolution fusion | flops 69206016 | bytes 130048 | tf_op jit(solution)/shard_map/dot_general | solution.py:192
  73.4 2.1 %reduce-precision_convert_fusion.5 = (bf16[768,72]{1,0:T(8,128)(2,1)S(1)}, bf16[768,72]{1,0:T(8,128)(2,1)S(1)}, bf16[768,72]{1,0:T(8,128)(2,1)S(1)}, bf16[768,72...) fusion(f32[768]{0:T(1024)S(1)} %select_multiply_fusion, f32[72]{0:T(128)S(1)} %multiply_multiply_fusion), kind=kLoop, calls=%fused_computation.46 | loop fusion | flops 1050624 | bytes 666912 | tf_op jit(solution)/shard_map/convert_element_type | solution.py:19
  75.4 1.4 fusion.44
  76.9 2.5 %fusion.47 = (f32[768,128]{1,0:T(8,128)}, f32[768,128]{1,0:T(8,128)}) fusion(f32[128]{0:T(128)S(1)} %fusion.66, f32[768]{0:T(1024)S(1)} %select_multiply_fusion), kind=kLoop, calls=%fused_computation.77 | loop fusion | flops 196608 | bytes 790016 | tf_op jit(solution)/shard_map/sin | solution.py:38
  79.4 9.7 %shard_map.87 = bf16[768,4608]{1,0:T(8,128)(2,1)} custom-call(bf16[768,256]{1,0:T(8,128)(2,1)} %get-tuple-element.37.row_sin_ref, bf16[768,256]{1,0:T(8,128)(2,1)} %get-tuple-element.38.row_cos_ref, bf16[256,4608]{1,0:T(8,128)(2,1)} %and_convert_fusion.expand_ref, f32[768,128]{1,0:T(8,128)} %get-tuple-element.13.col_cos_ref, ...), custom_call_target="tpu_custom_call" | custom-call | tf_op jit(solution)/shard_map/pallas_call | solution.py:126
  89.1 2.3 %slice.58 = bf16[8,24,9216]{2,1,0:T(8,128)(2,1)S(1)} slice(bf16[8,25,9216]{2,1,0:T(8,128)(2,1)} %all-gather.4.cloned.1.call-done), slice={[0:8], [0:24], [0:9216]} | slice | bytes 7077888 | tf_op jit(solution)/shard_map/slice | solution.py:157
  91.3 7.0 %fusion.3 = f32[1024,192]{0,1:T(8,128)S(1)} fusion(bf16[1024,4608]{1,0:T(8,128)(2,1)} %get-tuple-element.6, bf16[192,9216]{1,0:T(8,128)(2,1)S(1)} %bitcast.27), kind=kOutput, calls=%fused_computation.6 | convolution fusion | flops 1818132480 | bytes 13762560 | tf_op jit(solution)/shard_map/dot_general | solution.py:178
  98.4 10.4 %fusion.8 = f32[1024]{0:T(1024)S(1)} fusion(f32[1024,192]{0,1:T(8,128)S(1)} %fusion.3, bf16[1024,9216]{1,0:T(8,128)(2,1)} %get-tuple-element.5, bf16[192,9216]{1,0:T(8,128)(2,1)S(1)} %bitcast.28, f32[192]{0:T(256)S(1)} %add.138), kind=kOutput, calls=%fused_computation.11 | convolution fusion | flops 3624467456 | bytes 23204608 | tf_op jit(solution)/shard_map/dot_general | solution.py:176
  108.7 10.4 %pmax.7 = f32[1024]{0:T(1024)} all-reduce(f32[1024]{0:T(1024)S(1)} %fusion.8), channel_id=1, replica_groups=mesh['dom'=8,'cls'=4] {'cls'}, use_global_device_ids=true, to_apply=%region_2.3 | all-reduce | flops 1024 | bytes 8192 | tf_op jit(solution)/shard_map/pmax | solution.py:182
  119.8 4.1 %fusion.49 = f32[24,4608]{1,0:T(8,128)S(1)} fusion(bf16[768,4608]{1,0:T(8,128)(2,1)} %shard_map.87, s32[768]{0:T(1024)S(1)} %fusion.59), kind=kOutput, calls=%fused_computation.81 | convolution fusion | flops 169887744 | bytes 7523328 | tf_op jit(solution)/shard_map/dot_general | solution.py:202
  123.9 19.9 %reduce-scatter.2.cloned.1.call-done = f32[24,9216]{1,0:T(8,128)} async-done(((f32[192,9216]{1,0:T(8,128)}), f32[24,9216]{1,0:T(8,128)}) %reduce-scatter.2.cloned.1.call-update) | async-done | bytes 884752 | tf_op jit(solution)/shard_map/reduce_scatter | solution.py:169
  143.8 2.2 %fusion.16 = f32[3,8,9216]{2,1,0:T(8,128)} fusion(f32[24,9216]{1,0:T(8,128)} %reduce-scatter.2.cloned.1.call-done, f32[24,4608]{1,0:T(8,128)S(1)} %fusion.49), kind=kLoop, calls=%fused_computation.21 | loop fusion | flops 663552 | bytes 2211840 | tf_op jit(solution)/shard_map/reshape | solution.py:205
  (41 shorter events, 4.5 us)
Async XLA Ops:
  7.2 58.2 %all-gather.4.cloned.1.call-start = ((), (), s32[]{:S(2)}) async-start(), calls=%async_computation.2 | async-start | bytes 5308416 | tf_op jit(solution)/shard_map/all_gather | solution.py:156
  10.8 133.0 %reduce-scatter.2.cloned.1.call-start = ((), (), s32[]{:S(2)}) async-start(), calls=%async_computation.1 | async-start | bytes 7962624 | tf_op jit(solution)/shard_map/reduce_scatter | solution.py:169
  49.5 0.7 copy-start
Sparse Core Ops, SparseCore 0:
  10.9 54.4 all-gather.3
  67.7 76.0 reduce-scatter.1

commit v9 on v8

--- a/solution.py
+++ b/solution.py
@@ -147,15 +147,15 @@
     facts = split_pieces(defocus[None, :], 3 * local_rows).reshape(3, local_rows)
     block_class = jnp.clip(local_class, -1, block_classes).astype(jnp.bfloat16)
     facts = jnp.concatenate([facts, block_class[None, :], part_rot.astype(jnp.bfloat16)[None, :]], axis=0)
-    extra_rows = -(-facts.size // (2 * pixels))
-    facts = jnp.pad(facts.reshape(-1), (0, extra_rows * 2 * pixels - facts.size))
     ref_rows = owned * rotations
+    extra_lanes = -(-facts.size // (ref_rows * 128)) * 128
+    facts = jnp.pad(facts.reshape(-1), (0, extra_lanes * ref_rows - facts.size))
     sending = jnp.concatenate(
-        [references.reshape(ref_rows, 2 * pixels), facts.reshape(extra_rows, 2 * pixels)], axis=0
+        [references.reshape(ref_rows, 2 * pixels), facts.reshape(ref_rows, extra_lanes)], axis=1
     )
     gathered = lax.all_gather(sending, "dom", axis=0, tiled=False)
-    flat_images = gathered[:, :ref_rows].reshape(block_classes * rotations, 2 * pixels)
-    every_fact = gathered[:, ref_rows:].reshape(dom_size, -1)[:, : 5 * local_rows]
+    flat_images = gathered[:, :, : 2 * pixels].reshape(block_classes * rotations, 2 * pixels)
+    every_fact = gathered[:, :, 2 * pixels :].reshape(dom_size, -1)[:, : 5 * local_rows]
     every_fact = every_fact.reshape(dom_size, 5, local_rows).transpose(1, 0, 2).reshape(5, dom_size * local_rows)
     real_part = flat_images[:, :pixels].astype(jnp.float32)
     imag_part = flat_images[:, pixels:].astype(jnp.float32)

time: 154 us -> 145 us (0.942)
  waiting for transfers between devices: 33.6 us -> 14.3 us
  other arithmetic: 24.2 us -> 29.2 us
  local copies, waits for them, and re-layouts: 6.9 us -> 11.9 us
    all_gather x1, waiting for transfers between devices: 13.8 us -> 3.68 us  [on_device(): gathered = lax.all_gather(sending, 'dom', axis=0, tiled=False)]
    reduce_scatter x1, waiting for transfers between devices: 19.9 us -> 10.6 us  [on_device(): lax.psum_scatter(partial, 'dom', scatter_dimension=0, tiled=True)]
    another operation x2, other arithmetic: 0.39 us -> 3.11 us
    unnamed x4 -> x11, local copies, waits for them, and re-layouts: 0.73 us -> 3.12 us
    unnamed x1 -> x0, other arithmetic: 1.89 us -> none
    concatenate x0 -> x1, other arithmetic: none -> 1.8 us  [on_device(): jnp.concatenate([references.reshape(ref_rows, 2 * pixels), facts.reshape(...]
    slice x4 -> x3, local copies, waits for them, and re-layouts: 3.76 us -> 3.68 us  [the longest x1 2.23 us: on_device(): gathered[:, :, :2 * pixels].reshape(block_classes * rotations, 2 * pixels)]
  transfers between devices with their start and end apart: 2 -> 2, of which waited for: 2 -> 2; matrix products, arithmetic and copies ran while one was open for 33% -> 42% of each run, Pallas kernels for 24% -> 26%
where the time goes in v9:
time: 145 us; the launch traced here: 144 us
  Pallas kernels  36.7 us (25%)
  other arithmetic  29.2 us (20%)
  matrix products  25.9 us (18%)
  between operations  14.9 us (10%)
  waiting for transfers between devices  14.3 us (10%)
  local copies, waits for them, and re-layouts  11.9 us (8%)
  blocking collectives  10.4 us (7%)
    pallas_call x1, Pallas kernels, weighted_rows(): pl.pallas_call(weights_kernel, grid=(rows // block,), in_specs=table_spec...  27 us
    reduce_scatter x1, waiting for transfers between devices, on_device(): lax.psum_scatter(partial, 'dom', scatter_dimension=0, tiled=True)  10.6 us
    pmax x1, blocking collectives, on_device(): best_score = lax.pmax(jnp.max(score, axis=1), 'cls')  10.4 us
    dot_general x1, matrix products, on_device(): lax.dot_general(weighted, flat_images, (((1,), (1,)), ((), ())), preferre...  10.4 us
    pallas_call x1, Pallas kernels, power_rows(): pl.pallas_call(power_kernel, grid=(rows // block,), in_specs=table_specs(...  9.69 us
    dot_general x1, matrix products, on_device(): lax.dot_general(power_weight, power * jnp.bfloat16(-0.5), (((1,), (1,)),...  7 us
    sin x2, other arithmetic, contrast_tables(): jnp.sin(column_angle)  5.52 us
    convert_element_type x3, other arithmetic, split_pieces(): pieces.append(piece.astype(jnp.bfloat16))  5.23 us
  transfers between devices with their start and end apart: 2, of which 2 were waited for; matrix products, arithmetic and copies ran while one was open for 42% of the time, Pallas kernels for 26%

profile of v9, /device:TPU:0, one launch (start us, length us, event | category | flops | bytes accessed | tf_op | source)
XLA Modules:
  0.0 143.5 jit_solution(16703109376601566608)
XLA Ops:
  8.9 1.8 %pad_maximum_fusion = bf16[24,9472]{1,0:T(8,128)(2,1)} fusion(bf16[24,256]{1,0:T(8,128)(2,1)S(1)} %reshape.181, bf16[24,9216]{1,0:T(8,128)(2,1)} %bitcast.30), kind=kLoop, calls=%fused_computation.65 | loop fusion | flops 909312 | bytes 909312 | tf_op jit(solution)/shard_map/concatenate | solution.py:153
  12.2 2.5 %reduce-precision_convert_fusion.1 = (bf16[1024,72]{1,0:T(8,128)(2,1)S(1)}, bf16[1024,72]{1,0:T(8,128)(2,1)S(1)}, bf16[1024,72]{1,0:T(8,128)(2,1)S(1)}, bf16[102...) fusion(f32[1024]{0:T(1024)S(1)} %get-tuple-element.30, ...), kind=kLoop, calls=%fused_computation.35 | loop fusion | flops 1400832 | bytes 889120 | tf_op jit(solution)/shard_map/convert_element_type | solution.py:19
  14.7 1.6 %fusion.32 = (bf16[1024,256]{1,0:T(8,128)(2,1)}, bf16[1024,256]{1,0:T(8,128)(2,1)}) fusion(bf16[1024,72]{1,0:T(8,128)(2,1)S(1)} %get-tuple-element.24, bf16[1024,72]{1,0:T(8,128)(2,1)S(1)} %get-tuple-element.23, bf16[1024,72]{1,0:T(8,128)(2,1)S(1)} %get-tuple-element.27, bf16[1024,72]{1,0:T(8,128)(2,1)S(1)} %get-tuple-element.26, ...), kind=kLoop, calls=%fused_computation.59 | loop fusion | flops 4980736 | bytes 1933312 | tf_op jit(solution)/shard_map/concatenate | solution.py:21
  17.1 3.0 %fusion.35 = (f32[1024,128]{1,0:T(8,128)}, f32[1024,128]{1,0:T(8,128)}) fusion(f32[128]{0:T(128)S(1)} %fusion.66, f32[1024]{0:T(1024)S(1)} %get-tuple-element.30), kind=kLoop, calls=%fused_computation.63 | loop fusion | flops 262144 | bytes 1053184 | tf_op jit(solution)/shard_map/sin | solution.py:38
  20.2 2.3 %and_convert_fusion.expand_ref = bf16[256,4608]{1,0:T(8,128)(2,1)} fusion(s32[4608]{0:T(1024)S(1)} %add_select_fusion.1, s32[256]{0:T(256)S(1)} %and_select_fusion.1, pred[256]{0:T(512)(128)(4,1)S(1)} %iota_compare_fusion.8), kind=kLoop, calls=%fused_computation.3 | loop fusion | flops 3538944 | bytes 2379008 | tf_op jit(solution)/shard_map/convert_element_type | solution.py:37
  22.4 27.0 %shard_map.86 = (bf16[1024,9216]{1,0:T(8,128)(2,1)}, bf16[1024,4608]{1,0:T(8,128)(2,1)}, f32[192,9216]{1,0:T(8,128)}) custom-call(bf16[1024,256]{1,0:T(8,128)(2,1)} %get-tuple-element.35.row_sin_ref, bf16[1024,256]{1,0:T(8,128)(2,1)} %get-tuple-element.36.row_cos_ref, bf16[256,4608]{1,0:T(8,128)(2,1)} %and_convert_fusion.expand_ref, ...), custom_call_target="tpu_custom_call" | custom-call | tf_op jit(solution)/shard_map/pallas_call | solution.py:102
  52.2 3.7 %all-gather.3.cloned.1.call-done = bf16[192,9472]{1,0:T(8,128)(2,1)} async-done(((bf16[24,9472]{1,0:T(8,128)(2,1)}), bf16[192,9472]{1,0:T(8,128)(2,1)}) %all-gather.3.cloned.1.call-update) | async-done | bytes 3637264 | tf_op jit(solution)/shard_map/all_gather | solution.py:156
  55.9 2.2 %slice.58 = bf16[8,24,9216]{2,1,0:T(8,128)(2,1)S(1)} slice(bf16[8,24,9472]{2,1,0:T(8,128)(2,1)} %bitcast.26), slice={[0:8], [0:24], [0:9216]} | slice | bytes 7077888 | tf_op jit(solution)/shard_map/slice | solution.py:157
  60.3 1.4 reshape.190
  61.7 1.7 %reduce-window.9 = s32[64,128]{1,0:T(8,128)} reduce-window(s32[64,128]{1,0:T(8,128)} %reshape.190, s32[]{:T(128)} %constant.91.clone.1), window={size=1x128 pad=0_0x127_0}, to_apply=%region_4.5 | reduce-window | flops 1040384 | bytes 65540 | tf_op jit(solution)/shard_map/reduce-window
  63.4 1.4 %slice.64 = s32[64,1]{1,0:T(8,128)} slice(s32[64,128]{1,0:T(8,128)} %reduce-window.9), slice={[0:64], [127:128]} | slice | bytes 512 | tf_op jit(solution)/shard_map/slice
  64.8 1.4 %reduce-window.12 = s32[65,1]{1,0:T(8,128)} reduce-window(s32[64,1]{1,0:T(8,128)} %slice.64, s32[]{:T(128)} %constant.91.clone.1), window={size=64x1 pad=64_0x0_0}, to_apply=%region_5.6 | reduce-window | flops 4095 | bytes 520 | tf_op jit(solution)/shard_map/reduce-window.2
  69.6 4.5 %fusion = f32[5,768]{1,0:T(8,128)S(1)} fusion(bf16[5,8192]{1,0:T(8,128)(2,1)S(1)} %bitcast.34, s32[8192]{0:T(1024)S(1)} %get-tuple-element.8), kind=kOutput, calls=%fused_computation.1 | convolution fusion | flops 69206016 | bytes 130048 | tf_op jit(solution)/shard_map/dot_general | solution.py:192
  74.8 2.1 %reduce-precision_convert_fusion.5 = (bf16[768,72]{1,0:T(8,128)(2,1)S(1)}, bf16[768,72]{1,0:T(8,128)(2,1)S(1)}, bf16[768,72]{1,0:T(8,128)(2,1)S(1)}, bf16[768,72...) fusion(f32[768]{0:T(1024)S(1)} %select_multiply_fusion, f32[72]{0:T(128)S(1)} %multiply_multiply_fusion), kind=kLoop, calls=%fused_computation.45 | loop fusion | flops 1050624 | bytes 666912 | tf_op jit(solution)/shard_map/convert_element_type | solution.py:19
  76.8 1.4 fusion.44
  78.2 2.5 %fusion.47 = (f32[768,128]{1,0:T(8,128)}, f32[768,128]{1,0:T(8,128)}) fusion(f32[128]{0:T(128)S(1)} %fusion.66, f32[768]{0:T(1024)S(1)} %select_multiply_fusion), kind=kLoop, calls=%fused_computation.77 | loop fusion | flops 196608 | bytes 790016 | tf_op jit(solution)/shard_map/sin | solution.py:38
  80.7 9.7 %shard_map.87 = bf16[768,4608]{1,0:T(8,128)(2,1)} custom-call(bf16[768,256]{1,0:T(8,128)(2,1)} %get-tuple-element.37.row_sin_ref, bf16[768,256]{1,0:T(8,128)(2,1)} %get-tuple-element.38.row_cos_ref, bf16[256,4608]{1,0:T(8,128)(2,1)} %and_convert_fusion.expand_ref, f32[768,128]{1,0:T(8,128)} %get-tuple-element.13.col_cos_ref, ...), custom_call_target="tpu_custom_call" | custom-call | tf_op jit(solution)/shard_map/pallas_call | solution.py:126
  90.4 7.0 %fusion.3 = f32[1024,192]{0,1:T(8,128)S(1)} fusion(bf16[1024,4608]{1,0:T(8,128)(2,1)} %get-tuple-element.6, bf16[192,9216]{1,0:T(8,128)(2,1)S(1)} %bitcast.28), kind=kOutput, calls=%fused_computation.6 | convolution fusion | flops 1818132480 | bytes 13762560 | tf_op jit(solution)/shard_map/dot_general | solution.py:178
  97.4 10.4 %fusion.8 = f32[1024]{0:T(1024)S(1)} fusion(f32[1024,192]{0,1:T(8,128)S(1)} %fusion.3, bf16[1024,9216]{1,0:T(8,128)(2,1)} %get-tuple-element.5, bf16[192,9216]{1,0:T(8,128)(2,1)S(1)} %bitcast.29, f32[192]{0:T(256)S(1)} %copy-done.2), kind=kOutput, calls=%fused_computation.11 | convolution fusion | flops 3624467456 | bytes 23204608 | tf_op jit(solution)/shard_map/dot_general | solution.py:176
  107.8 10.4 %pmax.7 = f32[1024]{0:T(1024)} all-reduce(f32[1024]{0:T(1024)S(1)} %fusion.8), channel_id=1, replica_groups=mesh['dom'=8,'cls'=4] {'cls'}, use_global_device_ids=true, to_apply=%region_2.3 | all-reduce | flops 1024 | bytes 8192 | tf_op jit(solution)/shard_map/pmax | solution.py:182
  118.2 1.5 %fusion.59 = s32[768]{0:T(1024)S(1)} fusion(f32[5,768]{1,0:T(8,128)} %copy-done.1, s32[]{:T(128)S(6)} %mul.151, s32[]{:T(128)} %bitcast.6), kind=kLoop, calls=%fused_computation.110 | loop fusion | flops 5376 | bytes 9224 | tf_op jit(solution)/shard_map/jit(_where)/select_n | solution.py:198
  119.8 4.1 %fusion.49 = f32[24,4608]{1,0:T(8,128)S(1)} fusion(bf16[768,4608]{1,0:T(8,128)(2,1)} %shard_map.87, s32[768]{0:T(1024)S(1)} %fusion.59), kind=kOutput, calls=%fused_computation.81 | convolution fusion | flops 169887744 | bytes 7523328 | tf_op jit(solution)/shard_map/dot_general | solution.py:202
  123.9 10.6 %reduce-scatter.2.cloned.1.call-done = f32[24,9216]{1,0:T(8,128)} async-done(((f32[192,9216]{1,0:T(8,128)}), f32[24,9216]{1,0:T(8,128)}) %reduce-scatter.2.cloned.1.call-update) | async-done | bytes 884752 | tf_op jit(solution)/shard_map/reduce_scatter | solution.py:169
  134.5 2.2 %fusion.16 = f32[3,8,9216]{2,1,0:T(8,128)} fusion(f32[24,9216]{1,0:T(8,128)} %reduce-scatter.2.cloned.1.call-done, f32[24,4608]{1,0:T(8,128)S(1)} %fusion.49), kind=kLoop, calls=%fused_computation.21 | loop fusion | flops 663552 | bytes 2211840 | tf_op jit(solution)/shard_map/reshape | solution.py:205
  (47 shorter events, 12.2 us)
Async XLA Ops:
  7.2 48.8 %all-gather.3.cloned.1.call-start = ((), (), s32[]{:S(2)}) async-start(), calls=%async_computation.2 | async-start | bytes 4091904 | tf_op jit(solution)/shard_map/all_gather | solution.py:156
  10.7 123.7 %reduce-scatter.2.cloned.1.call-start = ((), (), s32[]{:S(2)}) async-start(), calls=%async_computation.1 | async-start | bytes 7962624 | tf_op jit(solution)/shard_map/reduce_scatter | solution.py:169
  49.5 0.7 copy-start.3
  59.1 0.6 copy-start
  74.0 6.6 %copy-start.1 = (f32[5,768]{1,0:T(8,128)}, f32[5,768]{1,0:T(8,128)S(1)}, u32[]{:S(2)}) copy-start(f32[5,768]{1,0:T(8,128)S(1)} %fusion) | copy-start | bytes 46084
  90.4 7.0 %copy-start.2 = (f32[192]{0:T(256)S(1)}, f32[192]{0:T(256)}, u32[]{:S(2)}) copy-start(f32[192]{0:T(256)} %add.138) | copy-start | bytes 2308
Sparse Core Ops, SparseCore 0:
  10.8 45.0 all-gather.2
  58.2 76.1 reduce-scatter.1

commit v10 on v9

--- a/solution.py
+++ b/solution.py
@@ -4,7 +4,7 @@
 import jax.numpy as jnp
 from jax import lax
 from jax.experimental import pallas as pl
-from jax.sharding import PartitionSpec as P
+from jax.sharding import Mesh, PartitionSpec as P
 
 AMPLITUDE = math.hypot(0.995, 0.1)
 PHASE = math.atan2(0.1, 0.995)
@@ -137,11 +137,16 @@
     pixels = inv_noise.shape[0]
     owned = references.shape[0]
     rotations = references.shape[1]
-    dom_size = lax.axis_size("dom")
+    chips = lax.axis_size("chip")
+    dom_size = 2 * chips
     cls_size = lax.axis_size("cls")
     cls_index = lax.axis_index("cls")
+    chip = lax.axis_index("chip")
+    core = lax.axis_index("core")
+    dom_index = 2 * chip + core
     block_classes = dom_size * owned
     block_first = cls_index * block_classes
+    swap = [(0, 1), (1, 0)]
 
     local_class = part_class - block_first
     facts = split_pieces(defocus[None, :], 3 * local_rows).reshape(3, local_rows)
@@ -153,37 +158,46 @@
     sending = jnp.concatenate(
         [references.reshape(ref_rows, 2 * pixels), facts.reshape(ref_rows, extra_lanes)], axis=1
     )
-    gathered = lax.all_gather(sending, "dom", axis=0, tiled=False)
-    flat_images = gathered[:, :, : 2 * pixels].reshape(block_classes * rotations, 2 * pixels)
-    every_fact = gathered[:, :, 2 * pixels :].reshape(dom_size, -1)[:, : 5 * local_rows]
+    fetched = lax.all_gather(sending, "chip", axis=0, tiled=False)
+    gathered = jnp.stack([fetched, lax.ppermute(fetched, "core", swap)])
+    flat_images = gathered[:, :, :, : 2 * pixels].reshape(block_classes * rotations, 2 * pixels)
+    every_fact = gathered[:, :, :, 2 * pixels :].reshape(dom_size, -1)[:, : 5 * local_rows]
+    row_ids = jnp.arange(block_classes * rotations, dtype=jnp.int32) // rotations
+    row_core = jnp.where(row_ids // (chips * owned) == 0, core, 1 - core)
+    row_block = 2 * ((row_ids // owned) % chips) + row_core
+    row_class = block_first + row_block * owned + row_ids % owned
     every_fact = every_fact.reshape(dom_size, 5, local_rows).transpose(1, 0, 2).reshape(5, dom_size * local_rows)
     real_part = flat_images[:, :pixels].astype(jnp.float32)
     imag_part = flat_images[:, pixels:].astype(jnp.float32)
     power = (real_part * real_part + imag_part * imag_part).astype(jnp.bfloat16)
 
     in_block = (local_class >= 0) & (local_class < block_classes)
-    pose = jnp.where(in_block, local_class * rotations + part_rot, -1)
+    owner = local_class // owned
+    mine = (owner % 2 == core).astype(jnp.int32)
+    pose = ((mine * chips + owner // 2) * owned + local_class % owned) * rotations + part_rot
+    pose = jnp.where(in_block, pose, -1)
     poses = jnp.arange(block_classes * rotations, dtype=jnp.int32)
     selector = (poses[:, None] == pose[None, :]).astype(jnp.bfloat16)
     weighted, power_weight, partial = weighted_rows(particles, defocus, inv_noise, selector)
-    numerator = lax.psum_scatter(partial, "dom", scatter_dimension=0, tiled=True)
+    partial = partial.reshape(2, chips * owned * rotations, 2 * pixels)
+    chip_sums = partial[1] + lax.ppermute(partial[0], "core", swap)
+    numerator = lax.psum_scatter(chip_sums, "chip", scatter_dimension=0, tiled=True)
 
     class_total = counts.shape[0]
     log_prior = jnp.log(
         (counts + 1).astype(jnp.float32) / (jnp.sum(counts) + class_total).astype(jnp.float32)
     )
-    class_prior = lax.dynamic_slice_in_dim(log_prior, block_first, block_classes)
     score = lax.dot_general(
         weighted, flat_images, (((1,), (1,)), ((), ())), preferred_element_type=jnp.float32
     ) + lax.dot_general(
         power_weight, power * jnp.bfloat16(-0.5), (((1,), (1,)), ((), ())), preferred_element_type=jnp.float32
     )
-    score = score + jnp.repeat(class_prior, rotations)[None, :]
+    score = score + jnp.take(log_prior, row_class)[None, :]
     best_score = lax.pmax(jnp.max(score, axis=1), "cls")
 
     capacity = max(2, 3 * local_rows // (dom_size * cls_size))
     slots = dom_size * capacity
-    fact_class = every_fact[3].astype(jnp.float32).astype(jnp.int32) - lax.axis_index("dom") * owned
+    fact_class = every_fact[3].astype(jnp.float32).astype(jnp.int32) - dom_index * owned
     owned_here = (fact_class >= 0) & (fact_class < owned)
     running = jnp.cumsum(owned_here.astype(jnp.int32))
     slot_of = jnp.where(owned_here, running - 1, -1)
@@ -194,7 +208,7 @@
     )
     filled = slot_ids < running[-1]
     slot_defocus = jnp.where(filled, (picked[0] + picked[1]) + picked[2], 1.0)
-    slot_pose = picked[3].astype(jnp.int32) - lax.axis_index("dom") * owned
+    slot_pose = picked[3].astype(jnp.int32) - dom_index * owned
     slot_pose = jnp.where(filled, slot_pose * rotations + picked[4].astype(jnp.int32), -1)
     slot_power = power_rows(slot_defocus, inv_noise)
     own_poses = jnp.arange(owned * rotations, dtype=jnp.int32)
@@ -206,11 +220,14 @@
 
 
 def solution(mesh):
-    placed = (P("dom", None), P("dom"), P(), P(("cls", "dom"), None, None), P("dom"), P("dom"), P())
+    dom_size, cls_size = mesh.devices.shape
+    split = Mesh(mesh.devices.reshape(dom_size // 2, 2, cls_size), ("chip", "core", "cls"))
+    dom = ("chip", "core")
+    placed = (P(dom, None), P(dom), P(), P(("cls",) + dom, None, None), P(dom), P(dom), P())
     return jax.shard_map(
         on_device,
-        mesh=mesh,
+        mesh=split,
         in_specs=placed,
-        out_specs=(P("dom"), P(("cls", "dom"), None, None)),
+        out_specs=(P(dom), P(("cls",) + dom, None, None)),
         check_vma=False,
     )

time: 145 us -> 177 us (1.22)
  waiting for transfers between devices: 14.3 us -> 48.4 us
  local copies, waits for them, and re-layouts: 11.9 us -> 8.6 us
    all_gather x1, waiting for transfers between devices: 3.68 us -> 43.4 us  [on_device(): fetched = lax.all_gather(sending, 'chip', axis=0, tiled=False)]
    reduce_scatter x1, waiting for transfers between devices: 10.6 us -> 4.95 us  [on_device(): lax.psum_scatter(chip_sums, 'chip', scatter_dimension=0, tiled=True)]
    add x0 -> x1, other arithmetic: none -> 5.25 us  [on_device(): chip_sums = partial[1] + lax.ppermute(partial[0], 'core', swap)]
    unnamed x11 -> x8, local copies, waits for them, and re-layouts: 3.12 us -> 0.7 us
  transfers between devices with their start and end apart: 2 -> 4, of which waited for: 2 -> 2; matrix products, arithmetic and copies ran while one was open for 42% -> 26% of each run, Pallas kernels for 26% -> 5%
where the time goes in v10:
time: 177 us
  waiting for transfers between devices  48.4 us (27%)
  Pallas kernels  36.5 us (21%)
  other arithmetic  30.8 us (17%)
  matrix products  26 us (15%)
  between operations  14.9 us (8%)
  blocking collectives  10.4 us (6%)
  local copies, waits for them, and re-layouts  8.6 us (5%)
    all_gather x1, waiting for transfers between devices, on_device(): fetched = lax.all_gather(sending, 'chip', axis=0, tiled=False)  43.4 us
    pallas_call x1, Pallas kernels, weighted_rows(): pl.pallas_call(weights_kernel, grid=(rows // block,), in_specs=table_spec...  26.9 us
    dot_general x1, matrix products, on_device(): lax.dot_general(weighted, flat_images, (((1,), (1,)), ((), ())), preferre...  10.5 us
    pmax x1, blocking collectives, on_device(): best_score = lax.pmax(jnp.max(score, axis=1), 'cls')  10.4 us
    pallas_call x1, Pallas kernels, power_rows(): pl.pallas_call(power_kernel, grid=(rows // block,), in_specs=table_specs(...  9.61 us
    dot_general x1, matrix products, on_device(): lax.dot_general(power_weight, power * jnp.bfloat16(-0.5), (((1,), (1,)),...  7 us
    sin x2, other arithmetic, contrast_tables(): jnp.sin(column_angle)  5.54 us
    add x1, other arithmetic, on_device(): chip_sums = partial[1] + lax.ppermute(partial[0], 'core', swap)  5.25 us
  transfers between devices with their start and end apart: 4, of which 2 were waited for; matrix products, arithmetic and copies ran while one was open for 26% of the time, Pallas kernels for 5%

profile of v10, /device:TPU:0, one launch (start us, length us, event | category | flops | bytes accessed | tf_op | source)
XLA Modules:
  0.0 176.6 jit_solution(6919675164490860183)
XLA Ops:
  8.0 1.3 broadcast_in_dim.36.noise_ref
  10.1 0.8 fusion.25.selector_ref
  10.9 3.1 %fusion.36 = (f32[1024,128]{1,0:T(8,128)}, f32[1024,128]{1,0:T(8,128)}) fusion(f32[128]{0:T(128)S(1)} %fusion.85, f32[1024]{0:T(1024)S(1)} %get-tuple-element.30), kind=kLoop, calls=%fused_computation.68 | loop fusion | flops 262144 | bytes 1053184 | tf_op jit(solution)/shard_map/sin | solution.py:38
  14.0 2.5 %reduce-precision_convert_fusion.1 = (bf16[1024,72]{1,0:T(8,128)(2,1)S(1)}, bf16[1024,72]{1,0:T(8,128)(2,1)S(1)}, bf16[1024,72]{1,0:T(8,128)(2,1)S(1)}, bf16[102...) fusion(f32[1024]{0:T(1024)S(1)} %get-tuple-element.30, ...), kind=kLoop, calls=%fused_computation.40 | loop fusion | flops 1400832 | bytes 889120 | tf_op jit(solution)/shard_map/convert_element_type | solution.py:19
  16.5 2.3 %and_convert_fusion.expand_ref = bf16[256,4608]{1,0:T(8,128)(2,1)} fusion(s32[4608]{0:T(1024)S(1)} %add_select_fusion.1, s32[256]{0:T(256)S(1)} %and_select_fusion.12, pred[256]{0:T(512)(128)(4,1)S(1)} %iota_compare_fusion.8), kind=kLoop, calls=%fused_computation.4 | loop fusion | flops 3538944 | bytes 2379008 | tf_op jit(solution)/shard_map/convert_element_type | solution.py:37
  18.8 1.7 fusion.33
  20.4 26.9 %shard_map.86 = (bf16[1024,9216]{1,0:T(8,128)(2,1)}, bf16[1024,4608]{1,0:T(8,128)(2,1)}, f32[192,9216]{1,0:T(8,128)}) custom-call(bf16[1024,256]{1,0:T(8,128)(2,1)} %get-tuple-element.35.row_sin_ref, bf16[1024,256]{1,0:T(8,128)(2,1)} %get-tuple-element.36.row_cos_ref, bf16[256,4608]{1,0:T(8,128)(2,1)} %and_convert_fusion.expand_ref, ...), custom_call_target="tpu_custom_call" | custom-call | tf_op jit(solution)/shard_map/pallas_call | solution.py:102
  47.4 4.1 %slice.56 = f32[96,9216]{1,0:T(8,128)} slice(f32[192,9216]{1,0:T(8,128)} %get-tuple-element.7), slice={[0:96], [0:9216]} | slice | bytes 7077888 | tf_op jit(solution)/shard_map/slice | solution.py:183
  53.3 43.4 %all-gather.3.cloned.1.call-done = bf16[96,9472]{1,0:T(8,128)(2,1)} async-done(((bf16[24,9472]{1,0:T(8,128)(2,1)}), bf16[96,9472]{1,0:T(8,128)(2,1)}) %all-gather.3.cloned.1.call-update) | async-done | bytes 1818640 | tf_op jit(solution)/shard_map/all_gather | solution.py:161
  96.7 5.2 %slice_add_fusion = f32[96,9216]{1,0:T(8,128)} fusion(f32[96,9216]{1,0:T(8,128)} %collective-permute-done.1, f32[192,9216]{1,0:T(8,128)} %get-tuple-element.7), kind=kLoop, calls=%fused_computation.8 | loop fusion | flops 884736 | bytes 10616832 | tf_op jit(solution)/shard_map/add | solution.py:183
  104.0 1.6 gather_fusion
  105.6 0.8 pad_maximum_fusion.1
  107.8 4.5 %fusion = f32[5,768]{1,0:T(8,128)S(1)} fusion(bf16[5,8192]{1,0:T(8,128)(2,1)S(1)} %bitcast.39, s32[8192]{0:T(1024)S(1)} %get-tuple-element.8), kind=kOutput, calls=%fused_computation.2 | convolution fusion | flops 69206016 | bytes 130048 | tf_op jit(solution)/shard_map/dot_general | solution.py:206
  112.9 1.9 %reduce-precision_convert_fusion.5 = (bf16[768,72]{1,0:T(8,128)(2,1)S(1)}, bf16[768,72]{1,0:T(8,128)(2,1)S(1)}, bf16[768,72]{1,0:T(8,128)(2,1)S(1)}, bf16[768,72...) fusion(f32[768]{0:T(1024)S(1)} %select_multiply_fusion, f32[72]{0:T(128)S(1)} %multiply_multiply_fusion), kind=kLoop, calls=%fused_computation.50 | loop fusion | flops 1050624 | bytes 666912 | tf_op jit(solution)/shard_map/convert_element_type | solution.py:19
  114.8 1.4 fusion.45
  116.2 2.5 %fusion.48 = (f32[768,128]{1,0:T(8,128)}, f32[768,128]{1,0:T(8,128)}) fusion(f32[128]{0:T(128)S(1)} %fusion.85, f32[768]{0:T(1024)S(1)} %select_multiply_fusion), kind=kLoop, calls=%fused_computation.82 | loop fusion | flops 196608 | bytes 790016 | tf_op jit(solution)/shard_map/sin | solution.py:38
  118.7 9.6 %shard_map.87 = bf16[768,4608]{1,0:T(8,128)(2,1)} custom-call(bf16[768,256]{1,0:T(8,128)(2,1)} %get-tuple-element.37.row_sin_ref, bf16[768,256]{1,0:T(8,128)(2,1)} %get-tuple-element.38.row_cos_ref, bf16[256,4608]{1,0:T(8,128)(2,1)} %and_convert_fusion.expand_ref, f32[768,128]{1,0:T(8,128)} %get-tuple-element.13.col_cos_ref, ...), custom_call_target="tpu_custom_call" | custom-call | tf_op jit(solution)/shard_map/pallas_call | solution.py:126
  128.3 1.6 fusion.2
  129.9 7.0 %fusion.4 = f32[1024,192]{0,1:T(8,128)S(1)} fusion(bf16[1024,4608]{1,0:T(8,128)(2,1)} %get-tuple-element.6, bf16[192,9216]{1,0:T(8,128)(2,1)S(1)} %bitcast.32), kind=kOutput, calls=%fused_computation.11 | convolution fusion | flops 1818132480 | bytes 13762560 | tf_op jit(solution)/shard_map/dot_general | solution.py:192
  136.9 10.5 %fusion.9 = f32[1024]{0:T(1024)S(1)} fusion(f32[1024,192]{0,1:T(8,128)S(1)} %fusion.4, bf16[1024,9216]{1,0:T(8,128)(2,1)} %get-tuple-element.5, bf16[192,9216]{1,0:T(8,128)(2,1)S(1)} %bitcast.33, f32[192]{0:T(256)S(1)} %and_select_fusion.5), kind=kOutput, calls=%fused_computation.16 | convolution fusion | flops 3624467456 | bytes 23204608 | tf_op jit(solution)/shard_map/dot_general | solution.py:190
  147.4 10.4 %pmax.7 = f32[1024]{0:T(1024)} all-reduce(f32[1024]{0:T(1024)S(1)} %fusion.9), channel_id=1, replica_groups=mesh['chip'=4,'core'=2,'cls'=4] {'cls'}, use_global_device_ids=true, to_apply=%region_2.3 | all-reduce | flops 1024 | bytes 8192 | tf_op jit(solution)/shard_map/pmax | solution.py:196
  158.5 4.0 %fusion.50 = f32[24,4608]{1,0:T(8,128)S(1)} fusion(bf16[768,4608]{1,0:T(8,128)(2,1)} %shard_map.87, s32[768]{0:T(1024)S(1)} %fusion.70), kind=kOutput, calls=%fused_computation.86 | convolution fusion | flops 169887744 | bytes 7523328 | tf_op jit(solution)/shard_map/dot_general | solution.py:216
  162.6 4.9 %reduce-scatter.2.cloned.1.call-done = f32[24,9216]{1,0:T(8,128)} async-done(((f32[96,9216]{1,0:T(8,128)}), f32[24,9216]{1,0:T(8,128)}) %reduce-scatter.2.cloned.1.call-update) | async-done | bytes 884752 | tf_op jit(solution)/shard_map/reduce_scatter | solution.py:184
  167.5 2.2 %fusion.17 = f32[3,8,9216]{2,1,0:T(8,128)} fusion(f32[24,9216]{1,0:T(8,128)} %reduce-scatter.2.cloned.1.call-done, f32[24,4608]{1,0:T(8,128)S(1)} %fusion.50), kind=kLoop, calls=%fused_computation.26 | loop fusion | flops 663552 | bytes 2211840 | tf_op jit(solution)/shard_map/reshape | solution.py:219
  (52 shorter events, 7.3 us)
Async XLA Ops:
  7.2 89.5 %all-gather.3.cloned.1.call-start = ((), (), s32[]{:S(2)}) async-start(), calls=%async_computation.2 | async-start | bytes 2273280 | tf_op jit(solution)/shard_map/all_gather | solution.py:161
  47.4 4.8 %copy-start.1 = (bf16[3,8,9216]{2,1,0:T(8,128)(2,1)S(1)}, bf16[3,8,9216]{2,1,0:T(8,128)(2,1)}, u32[]{:S(2)}) copy-start(bf16[3,8,9216]{2,1,0:T(8,128)(2,1)} %param.10) | copy-start | bytes 1327108
  51.5 45.2 %collective-permute-start.1 = (f32[96,9216]{1,0:T(8,128)}, f32[96,9216]{1,0:T(8,128)}, u32[]{:S(2)}, u32[]{:S(2)}) collective-permute-start(f32[96,9216]{1,0:T(8,128)} %slice.56), channel_id=1, source_target_pairs={{0,4},{4,0},{1,5},{5,1},{2,6},{6,2},{3,7},{7,3},{8,12},{12,8},{9,1... | collective-permute-start | bytes 10616840 | tf_op jit(solution)/shard_map/ppermute | solution.py:183
  53.0 114.5 %reduce-scatter.2.cloned.1.call-start = ((), (), s32[]{:S(2)}) async-start(), calls=%async_computation.1 | async-start | bytes 4423680 | tf_op jit(solution)/shard_map/reduce_scatter | solution.py:184
  96.7 8.9 %collective-permute-start = (bf16[4,24,9472]{2,1,0:T(8,128)(2,1)}, bf16[4,24,9472]{2,1,0:T(8,128)(2,1)}, u32[]{:S(2)}, u32[]{:S(2)}) collective-permute-start(bf16[4,24,9472]{2,1,0:T(8,128)(2,1)} %bitcast.29), channel_id=1, source_target_pairs={{0,4},{4,0},{1,5},{5,1},{2,6},{6,2},{3,7},{7,3},{8,12},{12,8},{9,1... | collective-permute-start | bytes 5455880 | tf_op jit(solution)/shard_map/ppermute | solution.py:162
  102.0 0.7 copy-start.2
  102.0 3.6 %copy-start = (bf16[96,9472]{1,0:T(8,128)(2,1)S(1)}, bf16[96,9472]{1,0:T(8,128)(2,1)}, u32[]{:S(2)}) copy-start(bf16[96,9472]{1,0:T(8,128)(2,1)} %all-gather.3.cloned.1.call-done) | copy-start | bytes 5455876
Sparse Core Ops, SparseCore 0:
  53.1 43.5 all-gather.2
  102.1 65.3 reduce-scatter.1

commit v11 on v10

--- a/solution.py
+++ b/solution.py
@@ -158,14 +158,10 @@
     sending = jnp.concatenate(
         [references.reshape(ref_rows, 2 * pixels), facts.reshape(ref_rows, extra_lanes)], axis=1
     )
-    fetched = lax.all_gather(sending, "chip", axis=0, tiled=False)
-    gathered = jnp.stack([fetched, lax.ppermute(fetched, "core", swap)])
-    flat_images = gathered[:, :, :, : 2 * pixels].reshape(block_classes * rotations, 2 * pixels)
-    every_fact = gathered[:, :, :, 2 * pixels :].reshape(dom_size, -1)[:, : 5 * local_rows]
-    row_ids = jnp.arange(block_classes * rotations, dtype=jnp.int32) // rotations
-    row_core = jnp.where(row_ids // (chips * owned) == 0, core, 1 - core)
-    row_block = 2 * ((row_ids // owned) % chips) + row_core
-    row_class = block_first + row_block * owned + row_ids % owned
+    gathered = lax.all_gather(sending, ("chip", "core"), axis=0, tiled=False)
+    flat_images = gathered[:, :, : 2 * pixels].reshape(block_classes * rotations, 2 * pixels)
+    every_fact = gathered[:, :, 2 * pixels :].reshape(dom_size, -1)[:, : 5 * local_rows]
+    row_class = block_first + jnp.arange(block_classes * rotations, dtype=jnp.int32) // rotations
     every_fact = every_fact.reshape(dom_size, 5, local_rows).transpose(1, 0, 2).reshape(5, dom_size * local_rows)
     real_part = flat_images[:, :pixels].astype(jnp.float32)
     imag_part = flat_images[:, pixels:].astype(jnp.float32)

time: 177 us -> 145 us (0.82)
  waiting for transfers between devices: 48.4 us -> 6.03 us
  local copies, waits for them, and re-layouts: 8.6 us -> 14.4 us
    all_gather x1, waiting for transfers between devices: 43.4 us -> 0.01 us  [on_device(): gathered = lax.all_gather(sending, ('chip', 'core'), axis=0, tiled=False)]
    ppermute x1, waiting for transfers between devices: 0.01 us -> 5.99 us  [on_device(): chip_sums = partial[1] + lax.ppermute(partial[0], 'core', swap)]
    reduce_scatter x1, waiting for transfers between devices: 4.95 us -> 0.01 us  [on_device(): lax.psum_scatter(chip_sums, 'chip', scatter_dimension=0, tiled=True)]
    slice x2 -> x3, local copies, waits for them, and re-layouts: 0.08 us -> 3.68 us  [the longest x1 2.23 us: on_device(): gathered[:, :, :2 * pixels].reshape(block_classes * rotations, 2 * pixels)]
    add x1, other arithmetic: 5.25 us -> 2.22 us  [on_device(): chip_sums = partial[1] + lax.ppermute(partial[0], 'core', swap)]
    unnamed x8 -> x15, local copies, waits for them, and re-layouts: 0.7 us -> 3.13 us
  transfers between devices with their start and end apart: 4 -> 3, of which waited for: 2 -> 1; matrix products, arithmetic and copies ran while one was open for 26% -> 46% of each run, Pallas kernels for 5% -> 26%
where the time goes in v11:
time: 145 us; the launch traced here: 144 us
  Pallas kernels  36.6 us (25%)
  other arithmetic  31.7 us (22%)
  matrix products  26.1 us (18%)
  between operations  16.4 us (11%)
  local copies, waits for them, and re-layouts  14.4 us (10%)
  blocking collectives  11.6 us (8%)
  waiting for transfers between devices  6.03 us (4%)
    pallas_call x1, Pallas kernels, weighted_rows(): pl.pallas_call(weights_kernel, grid=(rows // block,), in_specs=table_spec...  27 us
    pmax x1, blocking collectives, on_device(): best_score = lax.pmax(jnp.max(score, axis=1), 'cls')  11.6 us
    dot_general x1, matrix products, on_device(): lax.dot_general(weighted, flat_images, (((1,), (1,)), ((), ())), preferre...  10.6 us
    pallas_call x1, Pallas kernels, power_rows(): pl.pallas_call(power_kernel, grid=(rows // block,), in_specs=table_specs(...  9.61 us
    dot_general x1, matrix products, on_device(): lax.dot_general(power_weight, power * jnp.bfloat16(-0.5), (((1,), (1,)),...  6.98 us
    ppermute x1, waiting for transfers between devices, on_device(): chip_sums = partial[1] + lax.ppermute(partial[0], 'core', swap)  5.99 us
    sin x2, other arithmetic, contrast_tables(): jnp.sin(column_angle)  5.55 us
    convert_element_type x3, other arithmetic, split_pieces(): pieces.append(piece.astype(jnp.bfloat16))  5.05 us
  transfers between devices with their start and end apart: 3, of which 1 were waited for; matrix products, arithmetic and copies ran while one was open for 46% of the time, Pallas kernels for 26%

profile of v11, /device:TPU:0, one launch (start us, length us, event | category | flops | bytes accessed | tf_op | source)
XLA Modules:
  0.0 143.5 jit_solution(2630696859055578004)
XLA Ops:
  9.8 1.8 %pad_maximum_fusion = bf16[24,9472]{1,0:T(8,128)(2,1)} fusion(bf16[24,256]{1,0:T(8,128)(2,1)S(1)} %reshape.259, bf16[24,9216]{1,0:T(8,128)(2,1)} %bitcast.31), kind=kLoop, calls=%fused_computation.67 | loop fusion | flops 909312 | bytes 909312 | tf_op jit(solution)/shard_map/concatenate | solution.py:158
  11.7 2.5 %reduce-precision_convert_fusion.1 = (bf16[1024,72]{1,0:T(8,128)(2,1)S(1)}, bf16[1024,72]{1,0:T(8,128)(2,1)S(1)}, bf16[1024,72]{1,0:T(8,128)(2,1)S(1)}, bf16[102...) fusion(f32[1024]{0:T(1024)S(1)} %get-tuple-element.30, ...), kind=kLoop, calls=%fused_computation.37 | loop fusion | flops 1400832 | bytes 889120 | tf_op jit(solution)/shard_map/convert_element_type | solution.py:19
  14.2 2.3 %and_convert_fusion.expand_ref = bf16[256,4608]{1,0:T(8,128)(2,1)} fusion(s32[4608]{0:T(1024)S(1)} %add_select_fusion.1, s32[256]{0:T(256)S(1)} %and_select_fusion.4, pred[256]{0:T(512)(128)(4,1)S(1)} %iota_compare_fusion.8), kind=kLoop, calls=%fused_computation.4 | loop fusion | flops 3538944 | bytes 2379008 | tf_op jit(solution)/shard_map/convert_element_type | solution.py:37
  16.4 1.6 %fusion.32 = (bf16[1024,256]{1,0:T(8,128)(2,1)}, bf16[1024,256]{1,0:T(8,128)(2,1)}) fusion(bf16[1024,72]{1,0:T(8,128)(2,1)S(1)} %get-tuple-element.24, bf16[1024,72]{1,0:T(8,128)(2,1)S(1)} %get-tuple-element.23, bf16[1024,72]{1,0:T(8,128)(2,1)S(1)} %get-tuple-element.27, bf16[1024,72]{1,0:T(8,128)(2,1)S(1)} %get-tuple-element.26, ...), kind=kLoop, calls=%fused_computation.61 | loop fusion | flops 4980736 | bytes 1933312 | tf_op jit(solution)/shard_map/concatenate | solution.py:21
  19.5 3.0 %fusion.35 = (f32[1024,128]{1,0:T(8,128)}, f32[1024,128]{1,0:T(8,128)}) fusion(f32[128]{0:T(128)S(1)} %fusion.78, f32[1024]{0:T(1024)S(1)} %get-tuple-element.30), kind=kLoop, calls=%fused_computation.65 | loop fusion | flops 262144 | bytes 1053184 | tf_op jit(solution)/shard_map/sin | solution.py:38
  22.6 27.0 %shard_map.86 = (bf16[1024,9216]{1,0:T(8,128)(2,1)}, bf16[1024,4608]{1,0:T(8,128)(2,1)}, f32[192,9216]{1,0:T(8,128)}) custom-call(bf16[1024,256]{1,0:T(8,128)(2,1)} %get-tuple-element.35.row_sin_ref, bf16[1024,256]{1,0:T(8,128)(2,1)} %get-tuple-element.36.row_cos_ref, bf16[256,4608]{1,0:T(8,128)(2,1)} %and_convert_fusion.expand_ref, ...), custom_call_target="tpu_custom_call" | custom-call | tf_op jit(solution)/shard_map/pallas_call | solution.py:102
  49.6 2.4 %slice.56 = f32[96,9216]{1,0:T(8,128)S(1)} slice(f32[192,9216]{1,0:T(8,128)} %get-tuple-element.7), slice={[0:96], [0:9216]} | slice | bytes 7077888 | tf_op jit(solution)/shard_map/slice | solution.py:179
  52.5 6.0 %collective-permute-done = f32[96,9216]{1,0:T(8,128)S(1)} collective-permute-done((f32[96,9216]{1,0:T(8,128)S(1)}, f32[96,9216]{1,0:T(8,128)S(1)}, u32[]{:S(2)}, u32[]{:S(2)}) %collective-permute-start) | collective-permute-done | bytes 3538976 | tf_op jit(solution)/shard_map/ppermute | solution.py:179
  58.5 2.2 %slice_add_fusion = f32[96,9216]{1,0:T(8,128)} fusion(f32[96,9216]{1,0:T(8,128)S(1)} %collective-permute-done, f32[192,9216]{1,0:T(8,128)S(1)} %copy-done), kind=kLoop, calls=%fused_computation.5 | loop fusion | flops 884736 | bytes 10616832 | tf_op jit(solution)/shard_map/add | solution.py:179
  62.7 1.7 %gather_fusion = f32[192]{0:T(256)S(1)} fusion(f32[96]{0:T(128)S(1)} %divide_log_fusion, s32[1024]{0:T(1024)S(1)} %pad_clamp_fusion), kind=kCustom, calls=%fused_computation | custom fusion | bytes 2304 | tf_op jit(solution)/shard_map/jit(_take)/gather | solution.py:191
  65.0 2.2 %slice.70 = bf16[8,24,9216]{2,1,0:T(8,128)(2,1)S(1)} slice(bf16[8,24,9472]{2,1,0:T(8,128)(2,1)} %bitcast.27), slice={[0:8], [0:24], [0:9216]} | slice | bytes 7077888 | tf_op jit(solution)/shard_map/slice | solution.py:162
  70.8 1.7 %reduce-window.9 = s32[64,128]{1,0:T(8,128)} reduce-window(s32[64,128]{1,0:T(8,128)} %reshape.268, s32[]{:T(128)} %constant.156.clone.1), window={size=1x128 pad=0_0x127_0}, to_apply=%region_4.5 | reduce-window | flops 1040384 | bytes 65540 | tf_op jit(solution)/shard_map/reduce-window
  72.5 1.4 %slice.76 = s32[64,1]{1,0:T(8,128)} slice(s32[64,128]{1,0:T(8,128)} %reduce-window.9), slice={[0:64], [127:128]} | slice | bytes 512 | tf_op jit(solution)/shard_map/slice
  73.9 1.4 %reduce-window.12 = s32[65,1]{1,0:T(8,128)} reduce-window(s32[64,1]{1,0:T(8,128)} %slice.76, s32[]{:T(128)} %constant.156.clone.1), window={size=64x1 pad=64_0x0_0}, to_apply=%region_5.6 | reduce-window | flops 4095 | bytes 520 | tf_op jit(solution)/shard_map/reduce-window.2
  78.6 4.5 %fusion = f32[5,768]{1,0:T(8,128)S(1)} fusion(bf16[5,8192]{1,0:T(8,128)(2,1)S(1)} %bitcast.35, s32[8192]{0:T(1024)S(1)} %get-tuple-element.8), kind=kOutput, calls=%fused_computation.2 | convolution fusion | flops 69206016 | bytes 130048 | tf_op jit(solution)/shard_map/dot_general | solution.py:202
  83.7 1.9 %reduce-precision_convert_fusion.5 = (bf16[768,72]{1,0:T(8,128)(2,1)S(1)}, bf16[768,72]{1,0:T(8,128)(2,1)S(1)}, bf16[768,72]{1,0:T(8,128)(2,1)S(1)}, bf16[768,72...) fusion(f32[768]{0:T(1024)S(1)} %select_multiply_fusion, f32[72]{0:T(128)S(1)} %multiply_multiply_fusion), kind=kLoop, calls=%fused_computation.47 | loop fusion | flops 1050624 | bytes 666912 | tf_op jit(solution)/shard_map/convert_element_type | solution.py:19
  87.0 2.5 %fusion.47 = (f32[768,128]{1,0:T(8,128)}, f32[768,128]{1,0:T(8,128)}) fusion(f32[128]{0:T(128)S(1)} %fusion.78, f32[768]{0:T(1024)S(1)} %select_multiply_fusion), kind=kLoop, calls=%fused_computation.79 | loop fusion | flops 196608 | bytes 790016 | tf_op jit(solution)/shard_map/sin | solution.py:38
  89.5 9.6 %shard_map.87 = bf16[768,4608]{1,0:T(8,128)(2,1)} custom-call(bf16[768,256]{1,0:T(8,128)(2,1)} %get-tuple-element.37.row_sin_ref, bf16[768,256]{1,0:T(8,128)(2,1)} %get-tuple-element.38.row_cos_ref, bf16[256,4608]{1,0:T(8,128)(2,1)} %and_convert_fusion.expand_ref, f32[768,128]{1,0:T(8,128)} %get-tuple-element.13.col_cos_ref, ...), custom_call_target="tpu_custom_call" | custom-call | tf_op jit(solution)/shard_map/pallas_call | solution.py:126
  99.1 7.0 %fusion.3 = f32[1024,192]{0,1:T(8,128)S(1)} fusion(bf16[1024,4608]{1,0:T(8,128)(2,1)} %get-tuple-element.6, bf16[192,9216]{1,0:T(8,128)(2,1)S(1)} %bitcast.29), kind=kOutput, calls=%fused_computation.8 | convolution fusion | flops 1818132480 | bytes 13762560 | tf_op jit(solution)/shard_map/dot_general | solution.py:188
  106.1 10.6 %fusion.8 = f32[1024]{0:T(1024)S(1)} fusion(f32[1024,192]{0,1:T(8,128)S(1)} %fusion.3, bf16[1024,9216]{1,0:T(8,128)(2,1)} %get-tuple-element.5, bf16[192,9216]{1,0:T(8,128)(2,1)S(1)} %bitcast.30, f32[192]{0:T(256)S(1)} %copy-done.4), kind=kOutput, calls=%fused_computation.13 | convolution fusion | flops 3624467456 | bytes 23204608 | tf_op jit(solution)/shard_map/dot_general | solution.py:186
  116.7 11.6 %pmax.7 = f32[1024]{0:T(1024)} all-reduce(f32[1024]{0:T(1024)S(1)} %fusion.8), channel_id=1, replica_groups=mesh['chip'=4,'core'=2,'cls'=4] {'cls'}, use_global_device_ids=true, to_apply=%region_2.3 | all-reduce | flops 1024 | bytes 8192 | tf_op jit(solution)/shard_map/pmax | solution.py:192
  128.4 1.5 %fusion.69 = s32[768]{0:T(1024)S(1)} fusion(f32[5,768]{1,0:T(8,128)} %copy-done.3, s32[]{:T(128)S(6)} %mul.168, s32[]{:T(128)} %bitcast.7), kind=kLoop, calls=%fused_computation.134 | loop fusion | flops 5376 | bytes 9224 | tf_op jit(solution)/shard_map/jit(_where)/select_n | solution.py:208
  129.8 4.0 %fusion.49 = f32[24,4608]{1,0:T(8,128)S(1)} fusion(bf16[768,4608]{1,0:T(8,128)(2,1)} %shard_map.87, s32[768]{0:T(1024)S(1)} %fusion.69), kind=kOutput, calls=%fused_computation.83 | convolution fusion | flops 169887744 | bytes 7523328 | tf_op jit(solution)/shard_map/dot_general | solution.py:212
  133.9 2.2 %fusion.16 = f32[3,8,9216]{2,1,0:T(8,128)} fusion(f32[24,9216]{1,0:T(8,128)} %reduce-scatter.2.cloned.1.call-done, f32[24,4608]{1,0:T(8,128)S(1)} %fusion.49), kind=kLoop, calls=%fused_computation.23 | loop fusion | flops 663552 | bytes 2211840 | tf_op jit(solution)/shard_map/reshape | solution.py:215
  (56 shorter events, 14.4 us)
Async XLA Ops:
  8.0 57.0 %all-gather.3.cloned.1.call-start = ((), (), s32[]{:S(2)}) async-start(), calls=%async_computation.2 | async-start | bytes 4091904 | tf_op jit(solution)/shard_map/all_gather | solution.py:161
  11.6 6.5 %copy-start.2 = (f32[4608]{0:T(1024)S(1)}, f32[4608]{0:T(1024)}, u32[]{:S(2)}) copy-start(f32[4608]{0:T(1024)} %param.9) | copy-start | bytes 55300
  11.6 122.3 %reduce-scatter.2.cloned.1.call-start = ((), (), s32[]{:S(2)}) async-start(), calls=%async_computation.1 | async-start | bytes 4423680 | tf_op jit(solution)/shard_map/reduce_scatter | solution.py:180
  49.6 8.9 %copy-start = (f32[192,9216]{1,0:T(8,128)S(1)}, f32[192,9216]{1,0:T(8,128)}, u32[]{:S(2)}) copy-start(f32[192,9216]{1,0:T(8,128)} %get-tuple-element.7) | copy-start | bytes 21233668
  52.0 6.5 %collective-permute-start = (f32[96,9216]{1,0:T(8,128)S(1)}, f32[96,9216]{1,0:T(8,128)S(1)}, u32[]{:S(2)}, u32[]{:S(2)}) collective-permute-start(f32[96,9216]{1,0:T(8,128)S(1)} %slice.56), channel_id=1, source_target_pairs={{0,4},{4,0},{1,5},{5,1},{2,6},{6,2},{3,7},{7,3},{8,12},{12,8},{9,1... | collective-permute-start | bytes 10616840 | tf_op jit(solution)/shard_map/ppermute | solution.py:179
  60.7 0.7 copy-start.5
  68.2 0.6 copy-start.1
  83.1 6.4 %copy-start.3 = (f32[5,768]{1,0:T(8,128)}, f32[5,768]{1,0:T(8,128)S(1)}, u32[]{:S(2)}) copy-start(f32[5,768]{1,0:T(8,128)S(1)} %fusion) | copy-start | bytes 46084
  99.1 7.0 %copy-start.4 = (f32[192]{0:T(256)S(1)}, f32[192]{0:T(256)}, u32[]{:S(2)}) copy-start(f32[192]{0:T(256)} %and_select_fusion.1) | copy-start | bytes 2308
Sparse Core Ops, SparseCore 0:
  11.7 47.1 all-gather.2
Sparse Core Ops, SparseCore 1:
  60.8 68.8 reduce-scatter.1

commit v12 on v11

--- a/solution.py
+++ b/solution.py
@@ -45,7 +45,7 @@
 
 def weights_kernel(
     row_sin_ref, row_cos_ref, expand_ref, col_cos_ref, col_sin_ref, noise_ref, particles_ref, selector_ref,
-    out_ref, power_ref, sums_ref,
+    out_ref, power_ref, sums_ref, mine_ref,
 ):
     pixels = noise_ref.shape[1]
     row_sin = jnp.dot(row_sin_ref[...], expand_ref[...], preferred_element_type=jnp.float32)
@@ -64,8 +64,11 @@
     @pl.when(pl.program_id(0) == 0)
     def _():
         sums_ref[...] = jnp.zeros_like(sums_ref)
-
-    sums_ref[...] += jnp.dot(selector_ref[...], out_ref[...], preferred_element_type=jnp.float32)
+        mine_ref[...] = jnp.zeros_like(mine_ref)
+
+    half = sums_ref.shape[0]
+    sums_ref[...] += jnp.dot(selector_ref[:half, :], out_ref[...], preferred_element_type=jnp.float32)
+    mine_ref[...] += jnp.dot(selector_ref[half:, :], out_ref[...], preferred_element_type=jnp.float32)
 
 
 def power_kernel(row_sin_ref, row_cos_ref, expand_ref, col_cos_ref, col_sin_ref, noise_ref, power_ref):
@@ -107,12 +110,14 @@
         out_specs=[
             pl.BlockSpec((block, 2 * pixels), lambda i: (i, 0)),
             pl.BlockSpec((block, pixels), lambda i: (i, 0)),
-            pl.BlockSpec((poses, 2 * pixels), lambda i: (0, 0)),
+            pl.BlockSpec((poses // 2, 2 * pixels), lambda i: (0, 0)),
+            pl.BlockSpec((poses // 2, 2 * pixels), lambda i: (0, 0)),
         ],
         out_shape=[
             jax.ShapeDtypeStruct((rows, 2 * pixels), jnp.bfloat16),
             jax.ShapeDtypeStruct((rows, pixels), jnp.bfloat16),
-            jax.ShapeDtypeStruct((poses, 2 * pixels), jnp.float32),
+            jax.ShapeDtypeStruct((poses // 2, 2 * pixels), jnp.float32),
+            jax.ShapeDtypeStruct((poses // 2, 2 * pixels), jnp.float32),
         ],
     )(*tables, inv_noise[None, :], particles, selector)
 
@@ -174,9 +179,8 @@
     pose = jnp.where(in_block, pose, -1)
     poses = jnp.arange(block_classes * rotations, dtype=jnp.int32)
     selector = (poses[:, None] == pose[None, :]).astype(jnp.bfloat16)
-    weighted, power_weight, partial = weighted_rows(particles, defocus, inv_noise, selector)
-    partial = partial.reshape(2, chips * owned * rotations, 2 * pixels)
-    chip_sums = partial[1] + lax.ppermute(partial[0], "core", swap)
+    weighted, power_weight, for_other, for_me = weighted_rows(particles, defocus, inv_noise, selector)
+    chip_sums = for_me + lax.ppermute(for_other, "core", swap)
     numerator = lax.psum_scatter(chip_sums, "chip", scatter_dimension=0, tiled=True)
 
     class_total = counts.shape[0]
@@ -189,7 +193,12 @@
         power_weight, power * jnp.bfloat16(-0.5), (((1,), (1,)), ((), ())), preferred_element_type=jnp.float32
     )
     score = score + jnp.take(log_prior, row_class)[None, :]
-    best_score = lax.pmax(jnp.max(score, axis=1), "cls")
+    best_score = jnp.max(score, axis=1)
+    step = 1
+    while step < cls_size:
+        pairs = [(c, c ^ step) for c in range(cls_size)]
+        best_score = jnp.maximum(best_score, lax.ppermute(best_score, "cls", pairs))
+        step *= 2
 
     capacity = max(2, 3 * local_rows // (dom_size * cls_size))
     slots = dom_size * capacity

time: 145 us -> 141 us (0.972)
  blocking collectives: 11.6 us -> 0 us
  waiting for transfers between devices: 6.03 us -> 11.1 us
  starting transfers between devices: 0.62 us -> 5.31 us
  matrix products: 26.1 us -> 22 us
  other arithmetic: 31.7 us -> 33.5 us
    pmax x1 -> x0, blocking collectives: 11.6 us -> none  [on_device(): best_score = lax.pmax(jnp.max(score, axis=1), 'cls')]
    reduce_scatter x1, waiting for transfers between devices: 0.01 us -> 4.96 us  [on_device(): lax.psum_scatter(chip_sums, 'chip', scatter_dimension=0, tiled=True)]
    ppermute x1 -> x3, starting transfers between devices: 0.54 us -> 5.23 us  [the longest x2 4.71 us: on_device(): best_score = jnp.maximum(best_score, lax.ppermute(best_score, 'cls', pairs))]
    dot_general x1, matrix products: 10.6 us -> 6.3 us  [on_device(): lax.dot_general(weighted, flat_images, (((1,), (1,)), ((), ())), preferre...]
    slice x2 -> x1, local copies, waits for them, and re-layouts: 3.82 us -> 1.44 us  [the longest x1 2.38 us: on_device(): chip_sums = partial[1] + lax.ppermute(partial[0], 'core', swap)]
    unnamed x15 -> x11, local copies, waits for them, and re-layouts: 3.13 us -> 5.24 us
    add x1, other arithmetic: 2.22 us -> 4.21 us  [on_device(): chip_sums = for_me + lax.ppermute(for_other, 'core', swap)]
    ppermute x1 -> x3, waiting for transfers between devices: 5.99 us -> 6.15 us  [the longest x1 6.14 us: on_device(): chip_sums = for_me + lax.ppermute(for_other, 'core', swap)]
  transfers between devices with their start and end apart: 3 -> 5, of which waited for: 1 -> 2; matrix products, arithmetic and copies ran while one was open for 46% -> 44% of each run, Pallas kernels for 26% -> 26%
where the time goes in v12:
time: 141 us; the launch traced here: 140 us
  Pallas kernels  36.9 us (26%)
  other arithmetic  33.5 us (24%)
  matrix products  22 us (16%)
  between operations  16.4 us (12%)
  local copies, waits for them, and re-layouts  14.9 us (11%)
  waiting for transfers between devices  11.1 us (8%)
  starting transfers between devices  5.31 us (4%)
    pallas_call x1, Pallas kernels, weighted_rows(): pl.pallas_call(weights_kernel, grid=(rows // block,), in_specs=table_spec...  27.3 us
    pallas_call x1, Pallas kernels, power_rows(): pl.pallas_call(power_kernel, grid=(rows // block,), in_specs=table_specs(...  9.62 us
    dot_general x1, matrix products, on_device(): lax.dot_general(power_weight, power * jnp.bfloat16(-0.5), (((1,), (1,)),...  7.03 us
    dot_general x1, matrix products, on_device(): lax.dot_general(weighted, flat_images, (((1,), (1,)), ((), ())), preferre...  6.3 us
    ppermute x1, waiting for transfers between devices, on_device(): chip_sums = for_me + lax.ppermute(for_other, 'core', swap)  6.14 us
    sin x2, other arithmetic, contrast_tables(): jnp.sin(column_angle)  5.53 us
    unnamed x11, local copies, waits for them, and re-layouts  5.24 us
    convert_element_type x3, other arithmetic, split_pieces(): pieces.append(piece.astype(jnp.bfloat16))  5.05 us
  transfers between devices with their start and end apart: 5, of which 2 were waited for; matrix products, arithmetic and copies ran while one was open for 44% of the time, Pallas kernels for 26%

profile of v12, /device:TPU:0, one launch (start us, length us, event | category | flops | bytes accessed | tf_op | source)
XLA Modules:
  0.0 140.1 jit_solution(12555523288841788852)
XLA Ops:
  9.8 1.8 %pad_maximum_fusion = bf16[24,9472]{1,0:T(8,128)(2,1)} fusion(bf16[24,256]{1,0:T(8,128)(2,1)S(1)} %reshape.254, bf16[24,9216]{1,0:T(8,128)(2,1)} %bitcast.31), kind=kLoop, calls=%fused_computation.66 | loop fusion | flops 909312 | bytes 909312 | tf_op jit(solution)/shard_map/concatenate | solution.py:163
  13.0 2.5 %reduce-precision_convert_fusion.1 = (bf16[1024,72]{1,0:T(8,128)(2,1)S(1)}, bf16[1024,72]{1,0:T(8,128)(2,1)S(1)}, bf16[1024,72]{1,0:T(8,128)(2,1)S(1)}, bf16[102...) fusion(f32[1024]{0:T(1024)S(1)} %get-tuple-element.32, ...), kind=kLoop, calls=%fused_computation.36 | loop fusion | flops 1400832 | bytes 889120 | tf_op jit(solution)/shard_map/convert_element_type | solution.py:19
  15.5 1.6 %fusion.32 = (bf16[1024,256]{1,0:T(8,128)(2,1)}, bf16[1024,256]{1,0:T(8,128)(2,1)}) fusion(bf16[1024,72]{1,0:T(8,128)(2,1)S(1)} %get-tuple-element.26, bf16[1024,72]{1,0:T(8,128)(2,1)S(1)} %get-tuple-element.25, bf16[1024,72]{1,0:T(8,128)(2,1)S(1)} %get-tuple-element.29, bf16[1024,72]{1,0:T(8,128)(2,1)S(1)} %get-tuple-element.28, ...), kind=kLoop, calls=%fused_computation.60 | loop fusion | flops 4980736 | bytes 1933312 | tf_op jit(solution)/shard_map/concatenate | solution.py:21
  18.0 3.0 %fusion.35 = (f32[1024,128]{1,0:T(8,128)}, f32[1024,128]{1,0:T(8,128)}) fusion(f32[128]{0:T(128)S(1)} %fusion.78, f32[1024]{0:T(1024)S(1)} %get-tuple-element.32), kind=kLoop, calls=%fused_computation.64 | loop fusion | flops 262144 | bytes 1053184 | tf_op jit(solution)/shard_map/sin | solution.py:38
  21.1 2.2 %and_convert_fusion.expand_ref = bf16[256,4608]{1,0:T(8,128)(2,1)} fusion(s32[4608]{0:T(1024)S(1)} %add_select_fusion.1, s32[256]{0:T(256)S(1)} %and_select_fusion.4, pred[256]{0:T(512)(128)(4,1)S(1)} %iota_compare_fusion.8), kind=kLoop, calls=%fused_computation.4 | loop fusion | flops 3538944 | bytes 2379008 | tf_op jit(solution)/shard_map/convert_element_type | solution.py:37
  23.3 27.3 %shard_map.86 = (bf16[1024,9216]{1,0:T(8,128)(2,1)}, bf16[1024,4608]{1,0:T(8,128)(2,1)}, f32[96,9216]{1,0:T(8,128)}, f32[96,9216]{1,0:T(8,128)}) custom-call(bf16[1024,256]{1,0:T(8,128)(2,1)} %get-tuple-element.37.row_sin_ref, bf16[1024,256]{1,0:T(8,128)(2,1)} %get-tuple-element.38.row_cos_ref, bf16[256,4608]{1,0:T(8,128)(2,1)} %and_convert_fusion.expand_ref, ...), custom_call_target="tpu_custom_call" | custom-call | tf_op jit(solution)/shard_map/pallas_call | solution.py:105
  51.1 6.1 %collective-permute-done.2 = f32[96,9216]{1,0:T(8,128)S(1)} collective-permute-done((f32[96,9216]{1,0:T(8,128)}, f32[96,9216]{1,0:T(8,128)S(1)}, u32[]{:S(2)}, u32[]{:S(2)}) %collective-permute-start.2) | collective-permute-done | bytes 3538976 | tf_op jit(solution)/shard_map/ppermute | solution.py:183
  57.2 4.2 %add.232 = f32[96,9216]{1,0:T(8,128)} add(f32[96,9216]{1,0:T(8,128)} %get-tuple-element.8, f32[96,9216]{1,0:T(8,128)S(1)} %collective-permute-done.2) | non-fusion elementwise | flops 884736 | bytes 10616832 | tf_op jit(solution)/shard_map/add | solution.py:183
  63.4 1.7 %gather_fusion = f32[192]{0:T(256)S(1)} fusion(f32[96]{0:T(128)S(1)} %divide_log_fusion, s32[1024]{0:T(1024)S(1)} %pad_clamp_fusion), kind=kCustom, calls=%fused_computation | custom fusion | bytes 2304 | tf_op jit(solution)/shard_map/jit(_take)/gather | solution.py:195
  65.7 2.2 %slice.60 = bf16[8,24,9216]{2,1,0:T(8,128)(2,1)S(1)} slice(bf16[8,24,9472]{2,1,0:T(8,128)(2,1)} %bitcast.27), slice={[0:8], [0:24], [0:9216]} | slice | bytes 7077888 | tf_op jit(solution)/shard_map/slice | solution.py:167
  71.5 1.6 %reduce-window.9 = s32[64,128]{1,0:T(8,128)} reduce-window(s32[64,128]{1,0:T(8,128)} %reshape.263, s32[]{:T(128)} %constant.156.clone.1), window={size=1x128 pad=0_0x127_0}, to_apply=%region_3.4 | reduce-window | flops 1040384 | bytes 65540 | tf_op jit(solution)/shard_map/reduce-window
  73.2 1.4 %slice.66 = s32[64,1]{1,0:T(8,128)} slice(s32[64,128]{1,0:T(8,128)} %reduce-window.9), slice={[0:64], [127:128]} | slice | bytes 512 | tf_op jit(solution)/shard_map/slice
  79.3 7.0 %fusion.3 = f32[1024,192]{0,1:T(8,128)S(1)} fusion(bf16[1024,4608]{1,0:T(8,128)(2,1)} %get-tuple-element.7, bf16[192,9216]{1,0:T(8,128)(2,1)S(1)} %bitcast.29), kind=kOutput, calls=%fused_computation.7 | convolution fusion | flops 1818132480 | bytes 13762560 | tf_op jit(solution)/shard_map/dot_general | solution.py:192
  86.4 2.1 %copy-done.2 = bf16[1024,9216]{1,0:T(8,128)(2,1)S(1)} copy-done((bf16[1024,9216]{1,0:T(8,128)(2,1)S(1)}, bf16[1024,9216]{1,0:T(8,128)(2,1)}, u32[]{:S(2)}) %copy-start.2) | copy-done | bytes 18874392
  88.5 6.3 %fusion.8 = f32[1024]{0:T(1024)S(1)} fusion(f32[1024,192]{0,1:T(8,128)S(1)} %fusion.3, bf16[1024,9216]{1,0:T(8,128)(2,1)S(1)} %copy-done.2, bf16[192,9216]{1,0:T(8,128)(2,1)S(1)} %bitcast.30, f32[192]{0:T(256)S(1)} %copy-done.1), kind=kOutput, calls=%fused_computation.12 | convolution fusion | flops 3624467456 | bytes 23204608 | tf_op jit(solution)/shard_map/dot_general | solution.py:190
  94.8 3.1 %collective-permute-start = (f32[1024]{0:T(1024)S(1)}, f32[1024]{0:T(1024)S(1)}, u32[]{:S(2)}, u32[]{:S(2)}) collective-permute-start(f32[1024]{0:T(1024)S(1)} %fusion.8), channel_id=1, source_target_pairs={{0,1},{1,0},{2,3},{3,2},{4,5},{5,4},{6,7},{7,6},{8,9},{9,8},{10,11... | collective-permute-start | bytes 12296 | tf_op jit(solution)/shard_map/ppermute | solution.py:200
  97.9 4.7 %fusion = f32[5,768]{1,0:T(8,128)S(1)} fusion(bf16[5,8192]{1,0:T(8,128)(2,1)S(1)} %bitcast.35, s32[8192]{0:T(1024)S(1)} %get-tuple-element.10), kind=kOutput, calls=%fused_computation.2 | convolution fusion | flops 69206016 | bytes 130048 | tf_op jit(solution)/shard_map/dot_general | solution.py:211
  103.2 1.9 %reduce-precision_convert_fusion.5 = (bf16[768,72]{1,0:T(8,128)(2,1)S(1)}, bf16[768,72]{1,0:T(8,128)(2,1)S(1)}, bf16[768,72]{1,0:T(8,128)(2,1)S(1)}, bf16[768,72...) fusion(f32[768]{0:T(1024)S(1)} %select_multiply_fusion, f32[72]{0:T(128)S(1)} %multiply_multiply_fusion), kind=kLoop, calls=%fused_computation.46 | loop fusion | flops 1050624 | bytes 666912 | tf_op jit(solution)/shard_map/convert_element_type | solution.py:19
  106.5 2.5 %fusion.47 = (f32[768,128]{1,0:T(8,128)}, f32[768,128]{1,0:T(8,128)}) fusion(f32[128]{0:T(128)S(1)} %fusion.78, f32[768]{0:T(1024)S(1)} %select_multiply_fusion), kind=kLoop, calls=%fused_computation.78 | loop fusion | flops 196608 | bytes 790016 | tf_op jit(solution)/shard_map/sin | solution.py:38
  109.7 9.6 %shard_map.87 = bf16[768,4608]{1,0:T(8,128)(2,1)} custom-call(bf16[768,256]{1,0:T(8,128)(2,1)} %get-tuple-element.39.row_sin_ref, bf16[768,256]{1,0:T(8,128)(2,1)} %get-tuple-element.40.row_cos_ref, bf16[256,4608]{1,0:T(8,128)(2,1)} %and_convert_fusion.expand_ref, f32[768,128]{1,0:T(8,128)} %get-tuple-element.15.col_cos_ref, ...), custom_call_target="tpu_custom_call" | custom-call | tf_op jit(solution)/shard_map/pallas_call | solution.py:131
  119.3 1.6 %collective-permute-start.1 = (f32[1024]{0:T(1024)S(1)}, f32[1024]{0:T(1024)S(1)}, u32[]{:S(2)}, u32[]{:S(2)}) collective-permute-start(f32[1024]{0:T(1024)S(1)} %max.10), channel_id=1, source_target_pairs={{0,2},{1,3},{2,0},{3,1},{4,6},{5,7},{6,4},{7,5},{8,10},{9,11},{10,... | collective-permute-start | bytes 12296 | tf_op jit(solution)/shard_map/ppermute | solution.py:200
  120.9 4.0 %fusion.49 = f32[24,4608]{1,0:T(8,128)S(1)} fusion(bf16[768,4608]{1,0:T(8,128)(2,1)} %shard_map.87, s32[768]{0:T(1024)S(1)} %fusion.69), kind=kOutput, calls=%fused_computation.82 | convolution fusion | flops 169887744 | bytes 7523328 | tf_op jit(solution)/shard_map/dot_general | solution.py:221
  125.5 5.0 %reduce-scatter.2.cloned.1.call-done = f32[24,9216]{1,0:T(8,128)} async-done(((f32[96,9216]{1,0:T(8,128)}), f32[24,9216]{1,0:T(8,128)}) %reduce-scatter.2.cloned.1.call-update) | async-done | bytes 884752 | tf_op jit(solution)/shard_map/reduce_scatter | solution.py:184
  130.5 2.2 %fusion.16 = f32[3,8,9216]{2,1,0:T(8,128)} fusion(f32[24,9216]{1,0:T(8,128)} %reduce-scatter.2.cloned.1.call-done, f32[24,4608]{1,0:T(8,128)S(1)} %fusion.49), kind=kLoop, calls=%fused_computation.22 | loop fusion | flops 663552 | bytes 2211840 | tf_op jit(solution)/shard_map/reshape | solution.py:224
  (56 shorter events, 17.9 us)
Async XLA Ops:
  8.0 57.7 %all-gather.3.cloned.1.call-start = ((), (), s32[]{:S(2)}) async-start(), calls=%async_computation.2 | async-start | bytes 4091904 | tf_op jit(solution)/shard_map/all_gather | solution.py:166
  11.6 118.9 %reduce-scatter.2.cloned.1.call-start = ((), (), s32[]{:S(2)}) async-start(), calls=%async_computation.1 | async-start | bytes 4423680 | tf_op jit(solution)/shard_map/reduce_scatter | solution.py:184
  50.5 6.7 %collective-permute-start.2 = (f32[96,9216]{1,0:T(8,128)}, f32[96,9216]{1,0:T(8,128)S(1)}, u32[]{:S(2)}, u32[]{:S(2)}) collective-permute-start(f32[96,9216]{1,0:T(8,128)} %get-tuple-element.9), channel_id=1, source_target_pairs={{0,4},{4,0},{1,5},{5,1},{2,6},{6,2},{3,7},{7,3},{8,12},{12,8},{9,1... | collective-permute-start | bytes 10616840 | tf_op jit(solution)/shard_map/ppermute | solution.py:183
  61.4 0.7 copy-start.3
  68.9 0.6 copy-start
  79.3 7.1 %copy-start.1 = (f32[192]{0:T(256)S(1)}, f32[192]{0:T(256)}, u32[]{:S(2)}) copy-start(f32[192]{0:T(256)} %and_select_fusion.1) | copy-start | bytes 2308
  79.3 9.2 %copy-start.2 = (bf16[1024,9216]{1,0:T(8,128)(2,1)S(1)}, bf16[1024,9216]{1,0:T(8,128)(2,1)}, u32[]{:S(2)}) copy-start(bf16[1024,9216]{1,0:T(8,128)(2,1)} %get-tuple-element.6) | copy-start | bytes 56623108
  94.8 24.5 %collective-permute-start = (f32[1024]{0:T(1024)S(1)}, f32[1024]{0:T(1024)S(1)}, u32[]{:S(2)}, u32[]{:S(2)}) collective-permute-start(f32[1024]{0:T(1024)S(1)} %fusion.8), channel_id=1, source_target_pairs={{0,1},{1,0},{2,3},{3,2},{4,5},{5,4},{6,7},{7,6},{8,9},{9,8},{10,11... | collective-permute-start | bytes 12296 | tf_op jit(solution)/shard_map/ppermute | solution.py:200
  119.3 5.6 %collective-permute-start.1 = (f32[1024]{0:T(1024)S(1)}, f32[1024]{0:T(1024)S(1)}, u32[]{:S(2)}, u32[]{:S(2)}) collective-permute-start(f32[1024]{0:T(1024)S(1)} %max.10), channel_id=1, source_target_pairs={{0,2},{1,3},{2,0},{3,1},{4,6},{5,7},{6,4},{7,5},{8,10},{9,11},{10,... | collective-permute-start | bytes 12296 | tf_op jit(solution)/shard_map/ppermute | solution.py:200
Sparse Core Ops, SparseCore 0:
  11.7 45.8 all-gather.2
Sparse Core Ops, SparseCore 1:
  61.5 68.9 reduce-scatter.1

commit v13 on v12

--- a/solution.py
+++ b/solution.py
@@ -175,13 +175,18 @@
     in_block = (local_class >= 0) & (local_class < block_classes)
     owner = local_class // owned
     mine = (owner % 2 == core).astype(jnp.int32)
-    pose = ((mine * chips + owner // 2) * owned + local_class % owned) * rotations + part_rot
+    offset = (owner // 2 - chip) % chips
+    pose = ((mine * chips + offset) * owned + local_class % owned) * rotations + part_rot
     pose = jnp.where(in_block, pose, -1)
     poses = jnp.arange(block_classes * rotations, dtype=jnp.int32)
     selector = (poses[:, None] == pose[None, :]).astype(jnp.bfloat16)
     weighted, power_weight, for_other, for_me = weighted_rows(particles, defocus, inv_noise, selector)
-    chip_sums = for_me + lax.ppermute(for_other, "core", swap)
-    numerator = lax.psum_scatter(chip_sums, "chip", scatter_dimension=0, tiled=True)
+    chip_sums = (for_me + lax.ppermute(for_other, "core", swap)).reshape(chips, owned * rotations, 2 * pixels)
+    numerator = chip_sums[0]
+    for shift in range(1, chips):
+        pairs = [(c, (c + shift) % chips) for c in range(chips)]
+        arrived = lax.ppermute(chip_sums[shift].astype(jnp.bfloat16), "chip", pairs)
+        numerator = numerator + arrived.astype(jnp.float32)
 
     class_total = counts.shape[0]
     log_prior = jnp.log(

time: 141 us -> 206 us (1.46)
  waiting for transfers between devices: 11.1 us -> 60.3 us
  local copies, waits for them, and re-layouts: 14.9 us -> 20.7 us
  starting transfers between devices: 5.31 us -> 9.36 us
  matrix products: 22 us -> 25.7 us
  other arithmetic: 33.5 us -> 36.4 us
    all_gather x1, waiting for transfers between devices: 0.01 us -> 60.3 us  [on_device(): gathered = lax.all_gather(sending, ('chip', 'core'), axis=0, tiled=False)]
    ppermute x1 -> x4, waiting for transfers between devices: 6.14 us -> 0.01 us  [the longest x3 0.01 us: on_device(): arrived = lax.ppermute(chip_sums[shift].astype(jnp.bfloat16), 'chip', pairs)]
    ppermute x1 -> x4, starting transfers between devices: 0.52 us -> 6.28 us  [the longest x3 5.79 us: on_device(): arrived = lax.ppermute(chip_sums[shift].astype(jnp.bfloat16), 'chip', pairs)]
    reduce_scatter x1 -> x0, waiting for transfers between devices: 4.96 us -> none  [on_device(): lax.psum_scatter(chip_sums, 'chip', scatter_dimension=0, tiled=True)]
    add x1 -> x0, other arithmetic: 4.21 us -> none  [on_device(): chip_sums = for_me + lax.ppermute(for_other, 'core', swap)]
    dot_general x1, matrix products: 6.3 us -> 10.2 us  [on_device(): lax.dot_general(weighted, flat_images, (((1,), (1,)), ((), ())), preferre...]
    another operation x2 -> x3, other arithmetic: 3.08 us -> 6.65 us
    unnamed x11 -> x17, local copies, waits for them, and re-layouts: 5.24 us -> 4.32 us
  transfers between devices with their start and end apart: 5 -> 7, of which waited for: 2 -> 1; matrix products, arithmetic and copies ran while one was open for 44% -> 32% of each run, Pallas kernels for 26% -> 5%
where the time goes in v13:
time: 206 us; the launch traced here: 204 us
  waiting for transfers between devices  60.3 us (29%)
  Pallas kernels  36.8 us (18%)
  other arithmetic  36.4 us (18%)
  matrix products  25.7 us (12%)
  local copies, waits for them, and re-layouts  20.7 us (10%)
  between operations  15 us (7%)
  starting transfers between devices  9.36 us (5%)
    all_gather x1, waiting for transfers between devices, on_device(): gathered = lax.all_gather(sending, ('chip', 'core'), axis=0, tiled=False)  60.3 us
    pallas_call x1, Pallas kernels, weighted_rows(): pl.pallas_call(weights_kernel, grid=(rows // block,), in_specs=table_spec...  27.2 us
    dot_general x1, matrix products, on_device(): lax.dot_general(weighted, flat_images, (((1,), (1,)), ((), ())), preferre...  10.2 us
    pallas_call x1, Pallas kernels, power_rows(): pl.pallas_call(power_kernel, grid=(rows // block,), in_specs=table_specs(...  9.6 us
    dot_general x1, matrix products, on_device(): lax.dot_general(power_weight, power * jnp.bfloat16(-0.5), (((1,), (1,)),...  6.96 us
    another operation x3, other arithmetic  6.65 us
    ppermute x3, starting transfers between devices, on_device(): arrived = lax.ppermute(chip_sums[shift].astype(jnp.bfloat16), 'chip', pairs)  5.79 us
    sin x2, other arithmetic, contrast_tables(): jnp.sin(column_angle)  5.78 us
  transfers between devices with their start and end apart: 7, of which 1 were waited for; matrix products, arithmetic and copies ran while one was open for 32% of the time, Pallas kernels for 5%

profile of v13, /device:TPU:0, one launch (start us, length us, event | category | flops | bytes accessed | tf_op | source)
XLA Modules:
  0.0 204.2 jit_solution(3672025134421858020)
XLA Ops:
  12.1 3.0 %fusion.37 = (f32[1024,128]{1,0:T(8,128)}, f32[1024,128]{1,0:T(8,128)}) fusion(f32[128]{0:T(128)S(1)} %fusion.82, f32[1024]{0:T(1024)S(1)} %get-tuple-element.37), kind=kLoop, calls=%fused_computation.67 | loop fusion | flops 262144 | bytes 1053184 | tf_op jit(solution)/shard_map/sin | solution.py:38
  15.1 2.5 %reduce-precision_convert_fusion.1 = (bf16[1024,72]{1,0:T(8,128)(2,1)S(1)}, bf16[1024,72]{1,0:T(8,128)(2,1)S(1)}, bf16[1024,72]{1,0:T(8,128)(2,1)S(1)}, bf16[102...) fusion(f32[1024]{0:T(1024)S(1)} %get-tuple-element.37, ...), kind=kLoop, calls=%fused_computation.39 | loop fusion | flops 1400832 | bytes 889120 | tf_op jit(solution)/shard_map/convert_element_type | solution.py:19
  17.6 2.2 %and_convert_fusion.expand_ref = bf16[256,4608]{1,0:T(8,128)(2,1)} fusion(s32[4608]{0:T(1024)S(1)} %add_select_fusion.1, s32[256]{0:T(256)S(1)} %and_select_fusion.4, pred[256]{0:T(512)(128)(4,1)S(1)} %iota_compare_fusion.8), kind=kLoop, calls=%fused_computation.4 | loop fusion | flops 3538944 | bytes 2379008 | tf_op jit(solution)/shard_map/convert_element_type | solution.py:37
  19.8 1.7 fusion.34
  21.5 27.2 %shard_map.86 = (bf16[1024,9216]{1,0:T(8,128)(2,1)}, bf16[1024,4608]{1,0:T(8,128)(2,1)}, f32[96,9216]{1,0:T(8,128)}, f32[96,9216]{1,0:T(8,128)}) custom-call(bf16[1024,256]{1,0:T(8,128)(2,1)} %get-tuple-element.42.row_sin_ref, bf16[1024,256]{1,0:T(8,128)(2,1)} %get-tuple-element.43.row_cos_ref, bf16[256,4608]{1,0:T(8,128)(2,1)} %and_convert_fusion.expand_ref, ...), custom_call_target="tpu_custom_call" | custom-call | tf_op jit(solution)/shard_map/pallas_call | solution.py:105
  54.6 1.8 pad_maximum_fusion
  59.1 1.6 gather_fusion
  60.7 1.8 copy-done
  62.5 3.5 %fusion.86 = (bf16[96,9216]{1,0:T(8,128)(2,1)S(1)}, f32[96,9216]{1,0:T(8,128)S(1)}) fusion(f32[96,9216]{1,0:T(8,128)} %get-tuple-element.8, f32[96,9216]{1,0:T(8,128)} %copy-done), kind=kLoop, calls=%fused_computation.172 | loop fusion | flops 1769472 | bytes 12386304 | tf_op jit(solution)/shard_map/convert.2
  67.1 2.7 %collective-permute-start.3 = (bf16[24,9216]{1,0:T(8,128)(2,1)}, bf16[24,9216]{1,0:T(8,128)(2,1)}, u32[]{:S(2)}, u32[]{:S(2)}) collective-permute-start(bf16[24,9216]{1,0:T(8,128)(2,1)} %get-tuple-element.14), channel_id=1, source_target_pairs={{0,8},{8,16},{16,24},{24,0},{1,9},{9,17},{17,25},{25,1},{2,10},{10... | collective-permute-start | bytes 1327112 | tf_op jit(solution)/shard_map/ppermute | solution.py:188
  69.9 2.0 collective-permute-start.5
  72.9 60.3 %all-gather.3.cloned.1.call-done = bf16[192,9472]{1,0:T(8,128)(2,1)} async-done(((bf16[24,9472]{1,0:T(8,128)(2,1)}), bf16[192,9472]{1,0:T(8,128)(2,1)}) %all-gather.3.cloned.1.call-update) | async-done | bytes 3637264 | tf_op jit(solution)/shard_map/all_gather | solution.py:166
  134.1 4.0 %slice.83 = bf16[8,24,9216]{2,1,0:T(8,128)(2,1)} slice(bf16[8,24,9472]{2,1,0:T(8,128)(2,1)} %bitcast.28), slice={[0:8], [0:24], [0:9216]} | slice | bytes 7077888 | tf_op jit(solution)/shard_map/slice | solution.py:167
  140.7 1.7 reduce-window.9
  148.5 4.5 %fusion = f32[5,768]{1,0:T(8,128)S(1)} fusion(bf16[5,8192]{1,0:T(8,128)(2,1)S(1)} %bitcast.35, s32[8192]{0:T(1024)S(1)} %get-tuple-element.12), kind=kOutput, calls=%fused_computation.2 | convolution fusion | flops 69206016 | bytes 130048 | tf_op jit(solution)/shard_map/dot_general | solution.py:216
  154.4 2.7 %fusion.49 = (f32[768,128]{1,0:T(8,128)}, f32[768,128]{1,0:T(8,128)}) fusion(f32[128]{0:T(128)S(1)} %copy-done.6, f32[768]{0:T(1024)S(1)} %select_multiply_fusion), kind=kLoop, calls=%fused_computation.81 | loop fusion | flops 196608 | bytes 790016 | tf_op jit(solution)/shard_map/sin | solution.py:38
  157.1 1.8 reduce-precision_convert_fusion.5
  159.0 7.0 %fusion.3 = f32[1024,192]{0,1:T(8,128)S(1)} fusion(bf16[1024,4608]{1,0:T(8,128)(2,1)} %get-tuple-element.7, bf16[192,9216]{1,0:T(8,128)(2,1)S(1)} %bitcast.29), kind=kOutput, calls=%fused_computation.7 | convolution fusion | flops 1818132480 | bytes 13762560 | tf_op jit(solution)/shard_map/dot_general | solution.py:197
  165.9 10.2 %fusion.8 = f32[1024]{0:T(1024)S(1)} fusion(f32[1024,192]{0,1:T(8,128)S(1)} %fusion.3, bf16[1024,9216]{1,0:T(8,128)(2,1)} %get-tuple-element.6, bf16[192,9216]{1,0:T(8,128)(2,1)S(1)} %bitcast.30, f32[192]{0:T(256)S(1)} %and_select_fusion.1), kind=kOutput, calls=%fused_computation.12 | convolution fusion | flops 3624467456 | bytes 23204608 | tf_op jit(solution)/shard_map/dot_general | solution.py:195
  176.2 1.5 collective-permute-start
  179.1 9.6 %shard_map.87 = bf16[768,4608]{1,0:T(8,128)(2,1)} custom-call(bf16[768,256]{1,0:T(8,128)(2,1)} %get-tuple-element.44.row_sin_ref, bf16[768,256]{1,0:T(8,128)(2,1)} %get-tuple-element.45.row_cos_ref, bf16[256,4608]{1,0:T(8,128)(2,1)} %and_convert_fusion.expand_ref, f32[768,128]{1,0:T(8,128)} %get-tuple-element.20.col_cos_ref, ...), custom_call_target="tpu_custom_call" | custom-call | tf_op jit(solution)/shard_map/pallas_call | solution.py:131
  188.7 4.0 %fusion.51 = f32[24,4608]{1,0:T(8,128)S(1)} fusion(bf16[768,4608]{1,0:T(8,128)(2,1)} %shard_map.87, s32[768]{0:T(1024)S(1)} %fusion.73), kind=kOutput, calls=%fused_computation.85 | convolution fusion | flops 169887744 | bytes 7523328 | tf_op jit(solution)/shard_map/dot_general | solution.py:226
  192.7 1.5 collective-permute-start.1
  194.3 2.5 %fusion.18 = f32[3,8,9216]{2,1,0:T(8,128)} fusion(f32[96,9216]{1,0:T(8,128)S(1)} %get-tuple-element.11, f32[24,4608]{1,0:T(8,128)S(1)} %fusion.51, bf16[24,9216]{1,0:T(8,128)(2,1)} %collective-permute-done.5, bf16[24,9216]{1,0:T(8,128)(2,1)} %collective-permute-done.4, bf16[24,9216]{1,0:T(8,128)(2,1)} %collective-permute-done.3), kind=kLoop, calls=%fused_computation.24 | loop fusion | flops 1990656 | bytes 3538944 | tf_op jit(solution)/shard_map/reshape | solution.py:229
  (66 shorter events, 27.8 us)
Async XLA Ops:
  7.2 126.0 %all-gather.3.cloned.1.call-start = ((), (), s32[]{:S(2)}) async-start(), calls=%async_computation | async-start | bytes 4091904 | tf_op jit(solution)/shard_map/all_gather | solution.py:166
  7.2 14.3 %copy-start.3 = (f32[72]{0:T(128)}, f32[72]{0:T(128)S(1)}, u32[]{:S(2)}) copy-start(f32[72]{0:T(128)S(1)} %multiply_multiply_fusion) | copy-start | bytes 868
  7.2 14.2 %copy-start.5 = (f32[128]{0:T(128)}, f32[128]{0:T(128)S(1)}, u32[]{:S(2)}) copy-start(f32[128]{0:T(128)S(1)} %fusion.82) | copy-start | bytes 1540
  48.7 11.9 %collective-permute-start.2 = (f32[96,9216]{1,0:T(8,128)}, f32[96,9216]{1,0:T(8,128)S(1)}, u32[]{:S(2)}, u32[]{:S(2)}) collective-permute-start(f32[96,9216]{1,0:T(8,128)} %get-tuple-element.9), channel_id=1, source_target_pairs={{0,4},{4,0},{1,5},{5,1},{2,6},{6,2},{3,7},{7,3},{8,12},{12,8},{9,1... | collective-permute-start | bytes 10616840 | tf_op jit(solution)/shard_map/ppermute | solution.py:184
  60.6 1.8 copy-start
  67.1 127.2 %collective-permute-start.3 = (bf16[24,9216]{1,0:T(8,128)(2,1)}, bf16[24,9216]{1,0:T(8,128)(2,1)}, u32[]{:S(2)}, u32[]{:S(2)}) collective-permute-start(bf16[24,9216]{1,0:T(8,128)(2,1)} %get-tuple-element.14), channel_id=1, source_target_pairs={{0,8},{8,16},{16,24},{24,0},{1,9},{9,17},{17,25},{25,1},{2,10},{10... | collective-permute-start | bytes 1327112 | tf_op jit(solution)/shard_map/ppermute | solution.py:188
  69.9 124.4 %collective-permute-start.5 = (bf16[24,9216]{1,0:T(8,128)(2,1)}, bf16[24,9216]{1,0:T(8,128)(2,1)}, u32[]{:S(2)}, u32[]{:S(2)}) collective-permute-start(bf16[24,9216]{1,0:T(8,128)(2,1)} %get-tuple-element.15), channel_id=1, source_target_pairs={{0,24},{8,0},{16,8},{24,16},{1,25},{9,1},{17,9},{25,17},{2,26},{10... | collective-permute-start | bytes 1327112 | tf_op jit(solution)/shard_map/ppermute | solution.py:188
  71.9 122.4 %collective-permute-start.4 = (bf16[24,9216]{1,0:T(8,128)(2,1)}, bf16[24,9216]{1,0:T(8,128)(2,1)}, u32[]{:S(2)}, u32[]{:S(2)}) collective-permute-start(bf16[24,9216]{1,0:T(8,128)(2,1)} %get-tuple-element.16), channel_id=1, source_target_pairs={{0,16},{8,24},{16,0},{24,8},{1,17},{9,25},{17,1},{25,9},{2,18},{10... | collective-permute-start | bytes 1327112 | tf_op jit(solution)/shard_map/ppermute | solution.py:188
  138.1 0.6 copy-start.2
  139.4 15.0 %copy-start.6 = (f32[128]{0:T(128)S(1)}, f32[128]{0:T(128)}, u32[]{:S(2)}) copy-start(f32[128]{0:T(128)} %copy-done.5) | copy-start | bytes 1540
  148.5 8.6 %copy-start.4 = (f32[72]{0:T(128)S(1)}, f32[72]{0:T(128)}, u32[]{:S(2)}) copy-start(f32[72]{0:T(128)} %copy-done.3) | copy-start | bytes 868
  148.5 10.4 %copy-start.1 = (bf16[8,24,9216]{2,1,0:T(8,128)(2,1)S(1)}, bf16[8,24,9216]{2,1,0:T(8,128)(2,1)}, u32[]{:S(2)}) copy-start(bf16[8,24,9216]{2,1,0:T(8,128)(2,1)} %slice.83) | copy-start | bytes 10616836
  176.2 16.5 %collective-permute-start = (f32[1024]{0:T(1024)S(1)}, f32[1024]{0:T(1024)S(1)}, u32[]{:S(2)}, u32[]{:S(2)}) collective-permute-start(f32[1024]{0:T(1024)S(1)} %fusion.8), channel_id=1, source_target_pairs={{0,1},{1,0},{2,3},{3,2},{4,5},{5,4},{6,7},{7,6},{8,9},{9,8},{10,11... | collective-permute-start | bytes 12296 | tf_op jit(solution)/shard_map/ppermute | solution.py:205
  192.7 4.0 %collective-permute-start.1 = (f32[1024]{0:T(1024)S(1)}, f32[1024]{0:T(1024)S(1)}, u32[]{:S(2)}, u32[]{:S(2)}) collective-permute-start(f32[1024]{0:T(1024)S(1)} %max.10), channel_id=1, source_target_pairs={{0,2},{1,3},{2,0},{3,1},{4,6},{5,7},{6,4},{7,5},{8,10},{9,11},{10,... | collective-permute-start | bytes 12296 | tf_op jit(solution)/shard_map/ppermute | solution.py:205
Sparse Core Ops, SparseCore 0:
  56.5 76.6 all-gather.2

commit v14 on v12

--- a/solution.py
+++ b/solution.py
@@ -43,32 +43,38 @@
     return row_sin[:, lanes] * col_cos + row_cos[:, lanes] * col_sin
 
 
-def weights_kernel(
-    row_sin_ref, row_cos_ref, expand_ref, col_cos_ref, col_sin_ref, noise_ref, particles_ref, selector_ref,
-    out_ref, power_ref, sums_ref, mine_ref,
-):
-    pixels = noise_ref.shape[1]
-    row_sin = jnp.dot(row_sin_ref[...], expand_ref[...], preferred_element_type=jnp.float32)
-    row_cos = jnp.dot(row_cos_ref[...], expand_ref[...], preferred_element_type=jnp.float32)
-    col_cos = col_cos_ref[...]
-    col_sin = col_sin_ref[...]
-    for tile in range(pixels // 128):
-        lanes = slice(tile * 128, (tile + 1) * 128)
-        imag = slice(pixels + tile * 128, pixels + (tile + 1) * 128)
-        contrast_rows = contrast_tile(row_sin, row_cos, col_cos, col_sin, tile)
-        factor = noise_ref[:, lanes] * contrast_rows
-        out_ref[:, lanes] = (particles_ref[:, lanes].astype(jnp.float32) * factor).astype(jnp.bfloat16)
-        out_ref[:, imag] = (particles_ref[:, imag].astype(jnp.float32) * factor).astype(jnp.bfloat16)
-        power_ref[:, lanes] = (factor * contrast_rows).astype(jnp.bfloat16)
-
-    @pl.when(pl.program_id(0) == 0)
-    def _():
-        sums_ref[...] = jnp.zeros_like(sums_ref)
-        mine_ref[...] = jnp.zeros_like(mine_ref)
-
-    half = sums_ref.shape[0]
-    sums_ref[...] += jnp.dot(selector_ref[:half, :], out_ref[...], preferred_element_type=jnp.float32)
-    mine_ref[...] += jnp.dot(selector_ref[half:, :], out_ref[...], preferred_element_type=jnp.float32)
+def make_weights_kernel(with_power):
+    def weights_kernel(
+        row_sin_ref, row_cos_ref, expand_ref, col_cos_ref, col_sin_ref, noise_ref, particles_ref, selector_ref,
+        out_ref, *rest,
+    ):
+        if with_power:
+            power_ref, other_ref, mine_ref = rest
+        else:
+            other_ref, mine_ref = rest
+        pixels = noise_ref.shape[1]
+        row_sin = jnp.dot(row_sin_ref[...], expand_ref[...], preferred_element_type=jnp.float32)
+        row_cos = jnp.dot(row_cos_ref[...], expand_ref[...], preferred_element_type=jnp.float32)
+        col_cos = col_cos_ref[...]
+        col_sin = col_sin_ref[...]
+        for tile in range(pixels // 128):
+            lanes = slice(tile * 128, (tile + 1) * 128)
+            contrast_rows = contrast_tile(row_sin, row_cos, col_cos, col_sin, tile)
+            factor = noise_ref[:, lanes] * contrast_rows
+            out_ref[:, lanes] = (particles_ref[:, lanes].astype(jnp.float32) * factor).astype(jnp.bfloat16)
+            if with_power:
+                power_ref[:, lanes] = (factor * contrast_rows).astype(jnp.bfloat16)
+
+        @pl.when(pl.program_id(0) == 0)
+        def _():
+            other_ref[...] = jnp.zeros_like(other_ref)
+            mine_ref[...] = jnp.zeros_like(mine_ref)
+
+        half = other_ref.shape[0]
+        other_ref[...] += jnp.dot(selector_ref[:half, :], out_ref[...], preferred_element_type=jnp.float32)
+        mine_ref[...] += jnp.dot(selector_ref[half:, :], out_ref[...], preferred_element_type=jnp.float32)
+
+    return weights_kernel
 
 
 def power_kernel(row_sin_ref, row_cos_ref, expand_ref, col_cos_ref, col_sin_ref, noise_ref, power_ref):
@@ -95,30 +101,28 @@
     ]
 
 
-def weighted_rows(particles, defocus, inv_noise, selector):
+def weighted_half(particles, tables, inv_noise, selector, part):
     rows = particles.shape[0]
+    pixels = inv_noise.shape[0]
     poses = selector.shape[0]
-    pixels = inv_noise.shape[0]
     block = min(ROW_BLOCK, rows)
-    tables = contrast_tables(defocus, pixels)
     width = tables[0].shape[1]
+    with_power = part == 0
+    outs = [pl.BlockSpec((block, pixels), lambda i: (i, 0))]
+    shapes = [jax.ShapeDtypeStruct((rows, pixels), jnp.bfloat16)]
+    if with_power:
+        outs.append(pl.BlockSpec((block, pixels), lambda i: (i, 0)))
+        shapes.append(jax.ShapeDtypeStruct((rows, pixels), jnp.bfloat16))
+    for _ in range(2):
+        outs.append(pl.BlockSpec((poses // 2, pixels), lambda i: (0, 0)))
+        shapes.append(jax.ShapeDtypeStruct((poses // 2, pixels), jnp.float32))
     return pl.pallas_call(
-        weights_kernel,
+        make_weights_kernel(with_power),
         grid=(rows // block,),
         in_specs=table_specs(block, width, pixels)
-        + [pl.BlockSpec((block, 2 * pixels), lambda i: (i, 0)), pl.BlockSpec((poses, block), lambda i: (0, i))],
-        out_specs=[
-            pl.BlockSpec((block, 2 * pixels), lambda i: (i, 0)),
-            pl.BlockSpec((block, pixels), lambda i: (i, 0)),
-            pl.BlockSpec((poses // 2, 2 * pixels), lambda i: (0, 0)),
-            pl.BlockSpec((poses // 2, 2 * pixels), lambda i: (0, 0)),
-        ],
-        out_shape=[
-            jax.ShapeDtypeStruct((rows, 2 * pixels), jnp.bfloat16),
-            jax.ShapeDtypeStruct((rows, pixels), jnp.bfloat16),
-            jax.ShapeDtypeStruct((poses // 2, 2 * pixels), jnp.float32),
-            jax.ShapeDtypeStruct((poses // 2, 2 * pixels), jnp.float32),
-        ],
+        + [pl.BlockSpec((block, pixels), lambda i: (i, part)), pl.BlockSpec((poses, block), lambda i: (0, i))],
+        out_specs=outs,
+        out_shape=shapes,
     )(*tables, inv_noise[None, :], particles, selector)
 
 
@@ -179,16 +183,26 @@
     pose = jnp.where(in_block, pose, -1)
     poses = jnp.arange(block_classes * rotations, dtype=jnp.int32)
     selector = (poses[:, None] == pose[None, :]).astype(jnp.bfloat16)
-    weighted, power_weight, for_other, for_me = weighted_rows(particles, defocus, inv_noise, selector)
-    chip_sums = for_me + lax.ppermute(for_other, "core", swap)
-    numerator = lax.psum_scatter(chip_sums, "chip", scatter_dimension=0, tiled=True)
+    tables = contrast_tables(defocus, pixels)
+    halves = []
+    weighted_parts = []
+    for part in range(2):
+        made = weighted_half(particles, tables, inv_noise, selector, part)
+        if part == 0:
+            power_weight = made[1]
+        weighted_parts.append(made[0])
+        chip_sums = made[-1] + lax.ppermute(made[-2], "core", swap)
+        halves.append(lax.psum_scatter(chip_sums, "chip", scatter_dimension=0, tiled=True))
+    numerator = jnp.concatenate(halves, axis=1)
 
     class_total = counts.shape[0]
     log_prior = jnp.log(
         (counts + 1).astype(jnp.float32) / (jnp.sum(counts) + class_total).astype(jnp.float32)
     )
     score = lax.dot_general(
-        weighted, flat_images, (((1,), (1,)), ((), ())), preferred_element_type=jnp.float32
+        weighted_parts[0], flat_images[:, :pixels], (((1,), (1,)), ((), ())), preferred_element_type=jnp.float32
+    ) + lax.dot_general(
+        weighted_parts[1], flat_images[:, pixels:], (((1,), (1,)), ((), ())), preferred_element_type=jnp.float32
     ) + lax.dot_general(
         power_weight, power * jnp.bfloat16(-0.5), (((1,), (1,)), ((), ())), preferred_element_type=jnp.float32
     )

time: 141 us -> 146 us (1.035)
  Pallas kernels: 36.9 us -> 47.5 us
  waiting for transfers between devices: 11.1 us -> 3.77 us
  matrix products: 22 us -> 26.1 us
  local copies, waits for them, and re-layouts: 14.9 us -> 11.3 us
    pallas_call x1 -> x2, Pallas kernels: 27.3 us -> 37.9 us  [weighted_half(): pl.pallas_call(make_weights_kernel(with_power), grid=(rows // block,), in...]
    reduce_scatter x1 -> x2, waiting for transfers between devices: 4.96 us -> 0.01 us  [on_device(): lax.psum_scatter(chip_sums, 'chip', scatter_dimension=0, tiled=True)]
    dot_general x1 -> x2, matrix products: 6.3 us -> 10.3 us  [the longest x1 7.07 us: on_device(): lax.dot_general(weighted_parts[1], flat_images[:, pixels:], (((1,), (1,))...]
    unnamed x11 -> x19, local copies, waits for them, and re-layouts: 5.24 us -> 1.64 us
    ppermute x1 -> x2, waiting for transfers between devices: 6.14 us -> 3.69 us  [on_device(): chip_sums = made[-1] + lax.ppermute(made[-2], 'core', swap)]
    reshape x1 -> x0, other arithmetic: 2.2 us -> none  [on_device(): return (best_score, class_images.reshape(owned, rotations, 2 * pixels))]
    div x0 -> x1, other arithmetic: none -> 2.18 us  [on_device(): numerator / (jnp.concatenate([denominator, denominator], axis=1) + 1.0)]
    add x1 -> x2, other arithmetic: 4.21 us -> 5.87 us  [on_device(): chip_sums = made[-1] + lax.ppermute(made[-2], 'core', swap)]
  transfers between devices with their start and end apart: 5 -> 7, of which waited for: 2 -> 1; matrix products, arithmetic and copies ran while one was open for 44% -> 46% of each run, Pallas kernels for 26% -> 33%
where the time goes in v14:
time: 146 us; the launch traced here: 145 us
  Pallas kernels  47.5 us (33%)
  other arithmetic  34.7 us (24%)
  matrix products  26.1 us (18%)
  between operations  16.5 us (11%)
  local copies, waits for them, and re-layouts  11.3 us (8%)
  starting transfers between devices  5.31 us (4%)
  waiting for transfers between devices  3.77 us (3%)
    pallas_call x2, Pallas kernels, weighted_half(): pl.pallas_call(make_weights_kernel(with_power), grid=(rows // block,), in...  37.9 us
    pallas_call x1, Pallas kernels, power_rows(): pl.pallas_call(power_kernel, grid=(rows // block,), in_specs=table_specs(...  9.61 us
    dot_general x1, matrix products, on_device(): lax.dot_general(power_weight, power * jnp.bfloat16(-0.5), (((1,), (1,)),...  7.33 us
    dot_general x1, matrix products, on_device(): lax.dot_general(weighted_parts[1], flat_images[:, pixels:], (((1,), (1,))...  7.07 us
    add x2, other arithmetic, on_device(): chip_sums = made[-1] + lax.ppermute(made[-2], 'core', swap)  5.87 us
    sin x2, other arithmetic, contrast_tables(): jnp.sin(column_angle)  5.55 us
    convert_element_type x3, other arithmetic, split_pieces(): pieces.append(piece.astype(jnp.bfloat16))  5.27 us
    dot_general x1, matrix products, on_device(): lax.dot_general(every_fact, picker, (((1,), (1,)), ((), ())), preferred_e...  4.46 us
  transfers between devices with their start and end apart: 7, of which 1 were waited for; matrix products, arithmetic and copies ran while one was open for 46% of the time, Pallas kernels for 33%

profile of v14, /device:TPU:0, one launch (start us, length us, event | category | flops | bytes accessed | tf_op | source)
XLA Modules:
  0.0 145.1 jit_solution(14289160578383903894)
XLA Ops:
  9.8 1.8 %pad_maximum_fusion = bf16[24,9472]{1,0:T(8,128)(2,1)} fusion(bf16[24,256]{1,0:T(8,128)(2,1)S(1)} %reshape.256, bf16[24,9216]{1,0:T(8,128)(2,1)} %bitcast.34), kind=kLoop, calls=%fused_computation.71 | loop fusion | flops 909312 | bytes 909312 | tf_op jit(solution)/shard_map/concatenate | solution.py:167
  13.0 2.5 %reduce-precision_convert_fusion.1 = (bf16[1024,72]{1,0:T(8,128)(2,1)S(1)}, bf16[1024,72]{1,0:T(8,128)(2,1)S(1)}, bf16[1024,72]{1,0:T(8,128)(2,1)S(1)}, bf16[102...) fusion(f32[1024]{0:T(1024)S(1)} %get-tuple-element.38, ...), kind=kLoop, calls=%fused_computation.41 | loop fusion | flops 1400832 | bytes 889120 | tf_op jit(solution)/shard_map/convert_element_type | solution.py:19
  15.5 1.6 %fusion.44 = (bf16[1024,256]{1,0:T(8,128)(2,1)}, bf16[1024,256]{1,0:T(8,128)(2,1)}) fusion(bf16[1024,72]{1,0:T(8,128)(2,1)S(1)} %get-tuple-element.32, bf16[1024,72]{1,0:T(8,128)(2,1)S(1)} %get-tuple-element.31, bf16[1024,72]{1,0:T(8,128)(2,1)S(1)} %get-tuple-element.35, bf16[1024,72]{1,0:T(8,128)(2,1)S(1)} %get-tuple-element.34, ...), kind=kLoop, calls=%fused_computation.65 | loop fusion | flops 4980736 | bytes 1933312 | tf_op jit(solution)/shard_map/concatenate | solution.py:21
  18.0 3.1 %fusion.47 = (f32[1024,128]{1,0:T(8,128)}, f32[1024,128]{1,0:T(8,128)}) fusion(f32[128]{0:T(128)S(1)} %fusion.89, f32[1024]{0:T(1024)S(1)} %get-tuple-element.38), kind=kLoop, calls=%fused_computation.69 | loop fusion | flops 262144 | bytes 1053184 | tf_op jit(solution)/shard_map/sin | solution.py:38
  21.1 2.2 %and_convert_fusion.expand_ref = bf16[256,4608]{1,0:T(8,128)(2,1)} fusion(s32[4608]{0:T(1024)S(1)} %add_select_fusion.1, s32[256]{0:T(256)S(1)} %and_select_fusion.4, pred[256]{0:T(512)(128)(4,1)S(1)} %iota_compare_fusion.8), kind=kLoop, calls=%fused_computation.5 | loop fusion | flops 3538944 | bytes 2379008 | tf_op jit(solution)/shard_map/convert_element_type | solution.py:37
  23.3 18.0 %shard_map.87 = (bf16[1024,4608]{1,0:T(8,128)(2,1)}, f32[96,4608]{1,0:T(8,128)}, f32[96,4608]{1,0:T(8,128)}) custom-call(bf16[1024,256]{1,0:T(8,128)(2,1)} %get-tuple-element.43.row_sin_ref, bf16[1024,256]{1,0:T(8,128)(2,1)} %get-tuple-element.44.row_cos_ref, bf16[256,4608]{1,0:T(8,128)(2,1)} %and_convert_fusion.expand_ref, ...), custom_call_target="tpu_custom_call" | custom-call | tf_op jit(solution)/shard_map/pallas_call | solution.py:119
  41.9 3.7 %collective-permute-done.3 = f32[96,4608]{1,0:T(8,128)S(1)} collective-permute-done((f32[96,4608]{1,0:T(8,128)}, f32[96,4608]{1,0:T(8,128)S(1)}, u32[]{:S(2)}, u32[]{:S(2)}) %collective-permute-start.3) | collective-permute-done | bytes 1769504 | tf_op jit(solution)/shard_map/ppermute | solution.py:194
  45.6 2.9 %add.245 = f32[96,4608]{1,0:T(8,128)} add(f32[96,4608]{1,0:T(8,128)} %get-tuple-element.14, f32[96,4608]{1,0:T(8,128)S(1)} %collective-permute-done.3) | non-fusion elementwise | flops 442368 | bytes 5308416 | tf_op jit(solution)/shard_map/add | solution.py:194
  48.6 19.8 %shard_map.86 = (bf16[1024,4608]{1,0:T(8,128)(2,1)}, bf16[1024,4608]{1,0:T(8,128)(2,1)}, f32[96,4608]{1,0:T(8,128)}, f32[96,4608]{1,0:T(8,128)}) custom-call(bf16[1024,256]{1,0:T(8,128)(2,1)} %get-tuple-element.43.row_sin_ref, bf16[1024,256]{1,0:T(8,128)(2,1)} %get-tuple-element.44.row_cos_ref, bf16[256,4608]{1,0:T(8,128)(2,1)} %and_convert_fusion.expand_ref, ...), custom_call_target="tpu_custom_call" | custom-call | tf_op jit(solution)/shard_map/pallas_call | solution.py:119
  70.2 1.7 %gather_fusion = f32[192]{0:T(256)S(1)} fusion(f32[96]{0:T(128)S(1)} %divide_log_fusion, s32[1024]{0:T(1024)S(1)} %pad_clamp_fusion), kind=kCustom, calls=%fused_computation | custom fusion | bytes 2304 | tf_op jit(solution)/shard_map/jit(_take)/gather | solution.py:209
  72.5 3.0 %add.244 = f32[96,4608]{1,0:T(8,128)} add(f32[96,4608]{1,0:T(8,128)} %get-tuple-element.12, f32[96,4608]{1,0:T(8,128)S(1)} %collective-permute-done.2) | non-fusion elementwise | flops 442368 | bytes 5308416 | tf_op jit(solution)/shard_map/add | solution.py:194
  76.4 2.3 %slice.62 = bf16[8,24,9216]{2,1,0:T(8,128)(2,1)S(1)} slice(bf16[8,24,9472]{2,1,0:T(8,128)(2,1)} %bitcast.30), slice={[0:8], [0:24], [0:9216]} | slice | bytes 7077888 | tf_op jit(solution)/shard_map/slice | solution.py:171
  81.4 1.7 %reduce-window.9 = s32[64,128]{1,0:T(8,128)} reduce-window(s32[64,128]{1,0:T(8,128)} %reshape.264, s32[]{:T(128)} %constant.156.clone.1), window={size=1x128 pad=0_0x127_0}, to_apply=%region_4.5 | reduce-window | flops 1040384 | bytes 65540 | tf_op jit(solution)/shard_map/reduce-window
  86.8 7.1 %fusion.6 = f32[1024,192]{0,1:T(8,128)S(1)} fusion(bf16[1024,4608]{1,0:T(8,128)(2,1)} %get-tuple-element.10, bf16[192,9216]{1,0:T(8,128)(2,1)S(1)} %bitcast.31), kind=kOutput, calls=%fused_computation.10 | convolution fusion | flops 1811939328 | bytes 11993088 | tf_op jit(solution)/shard_map/dot_general | solution.py:204
  94.7 7.3 %fusion.3 = f32[1024,192]{0,1:T(8,128)S(1)} fusion(bf16[1024,4608]{1,0:T(8,128)(2,1)} %get-tuple-element.11, bf16[192,9216]{1,0:T(8,128)(2,1)S(1)} %bitcast.32), kind=kOutput, calls=%fused_computation.8 | convolution fusion | flops 1818132480 | bytes 13762560 | tf_op jit(solution)/shard_map/dot_general | solution.py:206
  102.1 3.2 %fusion.20 = f32[1024]{0:T(1024)S(1)} fusion(f32[1024,192]{0,1:T(8,128)S(1)} %fusion.3, f32[1024,192]{0,1:T(8,128)S(1)} %fusion.6, bf16[1024,4608]{1,0:T(8,128)(2,1)S(1)} %bitcast.43, bf16[192,9216]{1,0:T(8,128)(2,1)S(1)} %bitcast.33, f32[192]{0:T(256)S(1)} %copy-done.3), kind=kOutput, calls=%fused_computation.18 | convolution fusion | flops 1812724736 | bytes 12784640 | tf_op jit(solution)/shard_map/dot_general | solution.py:202
  105.3 2.7 %collective-permute-start = (f32[1024]{0:T(1024)S(1)}, f32[1024]{0:T(1024)S(1)}, u32[]{:S(2)}, u32[]{:S(2)}) collective-permute-start(f32[1024]{0:T(1024)S(1)} %fusion.20), channel_id=1, source_target_pairs={{0,1},{1,0},{2,3},{3,2},{4,5},{5,4},{6,7},{7,6},{8,9},{9,8},{10,11... | collective-permute-start | bytes 12296 | tf_op jit(solution)/shard_map/ppermute | solution.py:214
  107.9 4.5 %fusion = f32[5,768]{1,0:T(8,128)S(1)} fusion(bf16[5,8192]{1,0:T(8,128)(2,1)S(1)} %bitcast.40, s32[8192]{0:T(1024)S(1)} %get-tuple-element.16), kind=kOutput, calls=%fused_computation.2 | convolution fusion | flops 69206016 | bytes 130048 | tf_op jit(solution)/shard_map/dot_general | solution.py:225
  113.1 2.1 %reduce-precision_convert_fusion.5 = (bf16[768,72]{1,0:T(8,128)(2,1)S(1)}, bf16[768,72]{1,0:T(8,128)(2,1)S(1)}, bf16[768,72]{1,0:T(8,128)(2,1)S(1)}, bf16[768,72...) fusion(f32[768]{0:T(1024)S(1)} %select_multiply_fusion, f32[72]{0:T(128)S(1)} %multiply_multiply_fusion), kind=kLoop, calls=%fused_computation.51 | loop fusion | flops 1050624 | bytes 666912 | tf_op jit(solution)/shard_map/convert_element_type | solution.py:19
  116.6 2.5 %fusion.59 = (f32[768,128]{1,0:T(8,128)}, f32[768,128]{1,0:T(8,128)}) fusion(f32[128]{0:T(128)S(1)} %fusion.89, f32[768]{0:T(1024)S(1)} %select_multiply_fusion), kind=kLoop, calls=%fused_computation.83 | loop fusion | flops 196608 | bytes 790016 | tf_op jit(solution)/shard_map/sin | solution.py:38
  119.1 9.6 %shard_map.88 = bf16[768,4608]{1,0:T(8,128)(2,1)} custom-call(bf16[768,256]{1,0:T(8,128)(2,1)} %get-tuple-element.45.row_sin_ref, bf16[768,256]{1,0:T(8,128)(2,1)} %get-tuple-element.46.row_cos_ref, bf16[256,4608]{1,0:T(8,128)(2,1)} %and_convert_fusion.expand_ref, f32[768,128]{1,0:T(8,128)} %get-tuple-element.21.col_cos_ref, ...), custom_call_target="tpu_custom_call" | custom-call | tf_op jit(solution)/shard_map/pallas_call | solution.py:135
  129.3 4.0 %convolution_bitcast_fusion = f32[3,8,4608]{2,1,0:T(8,128)S(1)} fusion(bf16[768,4608]{1,0:T(8,128)(2,1)} %shard_map.88, s32[768]{0:T(1024)S(1)} %fusion.80), kind=kOutput, calls=%fused_computation.4 | convolution fusion | flops 169887744 | bytes 7523328 | tf_op jit(solution)/shard_map/dot_general | solution.py:235
  133.4 1.5 %collective-permute-start.1 = (f32[1024]{0:T(1024)S(1)}, f32[1024]{0:T(1024)S(1)}, u32[]{:S(2)}, u32[]{:S(2)}) collective-permute-start(f32[1024]{0:T(1024)S(1)} %max.10), channel_id=1, source_target_pairs={{0,2},{1,3},{2,0},{3,1},{4,6},{5,7},{6,4},{7,5},{8,10},{9,11},{10,... | collective-permute-start | bytes 12296 | tf_op jit(solution)/shard_map/ppermute | solution.py:214
  134.9 2.2 %maximum_divide_fusion = f32[3,8,9216]{2,1,0:T(8,128)} fusion(f32[3,8,4608]{2,1,0:T(8,128)} %bitcast.35, f32[3,8,4608]{2,1,0:T(8,128)} %bitcast.36, f32[3,8,4608]{2,1,0:T(8,128)S(1)} %convolution_bitcast_fusion), kind=kLoop, calls=%fused_computation.26 | loop fusion | flops 884736 | bytes 2211840 | tf_op jit(solution)/shard_map/div | solution.py:237
  (73 shorter events, 17.7 us)
Async XLA Ops:
  8.0 67.5 %all-gather.3.cloned.1.call-start = ((), (), s32[]{:S(2)}) async-start(), calls=%async_computation.4 | async-start | bytes 4091904 | tf_op jit(solution)/shard_map/all_gather | solution.py:170
  11.6 123.3 %reduce-scatter.5.cloned.1.call-start = ((), (), s32[]{:S(2)}) async-start(), calls=%async_computation.3 | async-start | bytes 2211840 | tf_op jit(solution)/shard_map/reduce_scatter | solution.py:195
  41.4 4.3 %collective-permute-start.3 = (f32[96,4608]{1,0:T(8,128)}, f32[96,4608]{1,0:T(8,128)S(1)}, u32[]{:S(2)}, u32[]{:S(2)}) collective-permute-start(f32[96,4608]{1,0:T(8,128)} %get-tuple-element.15), channel_id=1, source_target_pairs={{0,4},{4,0},{1,5},{5,1},{2,6},{6,2},{3,7},{7,3},{8,12},{12,8},{9,1... | collective-permute-start | bytes 5308424 | tf_op jit(solution)/shard_map/ppermute | solution.py:194
  48.6 20.3 %copy-start.4 = (s32[96]{0:T(128)S(1)}, s32[96]{0:T(128)}, u32[]{:S(2)}) copy-start(s32[96]{0:T(128)} %param.13) | copy-start | bytes 1156
  48.6 86.4 %reduce-scatter.3.cloned.1.call-start = ((), (), s32[]{:S(2)}) async-start(), calls=%async_computation.2 | async-start | bytes 2211840 | tf_op jit(solution)/shard_map/reduce_scatter | solution.py:195
  68.5 4.1 %collective-permute-start.2 = (f32[96,4608]{1,0:T(8,128)}, f32[96,4608]{1,0:T(8,128)S(1)}, u32[]{:S(2)}, u32[]{:S(2)}) collective-permute-start(f32[96,4608]{1,0:T(8,128)} %get-tuple-element.13), channel_id=1, source_target_pairs={{0,4},{4,0},{1,5},{5,1},{2,6},{6,2},{3,7},{7,3},{8,12},{12,8},{9,1... | collective-permute-start | bytes 5308424 | tf_op jit(solution)/shard_map/ppermute | solution.py:194
  78.7 0.6 copy-start
  86.8 7.1 %copy-start.2 = (s32[64,128]{1,0:T(8,128)S(1)}, s32[64,128]{1,0:T(8,128)}, u32[]{:S(2)}) copy-start(s32[64,128]{1,0:T(8,128)} %reduce-window.9) | copy-start | bytes 98308
  86.8 7.8 %copy-start.1 = (bf16[8,5120]{1,0:T(8,128)(2,1)S(1)}, bf16[8,5120]{1,0:T(8,128)(2,1)}, u32[]{:S(2)}) copy-start(bf16[8,5120]{1,0:T(8,128)(2,1)} %copy-done) | copy-start | bytes 245764
  86.8 15.2 %slice-start = ((s8[9437184]{0:T(1024)(128)(4,1)}), s8[4194304]{0:T(1024)(128)(4,1)S(1)}, s32[]{:S(2)}) async-start(s8[9437184]{0:T(1024)(128)(4,1)} %bitcast.42), calls=%async_computation.5 | async-start | bytes 8388608
  86.8 15.2 %slice-start.1 = ((s8[9437184]{0:T(1024)(128)(4,1)}), s8[4194304]{0:T(1024)(128)(4,1)S(1)}, s32[]{:S(2)}) async-start(s8[9437184]{0:T(1024)(128)(4,1)} %bitcast.42), calls=%async_computation.6 | async-start | bytes 8388608
  94.7 7.4 %copy-start.3 = (f32[192]{0:T(256)S(1)}, f32[192]{0:T(256)}, u32[]{:S(2)}) copy-start(f32[192]{0:T(256)} %and_select_fusion.1) | copy-start | bytes 2308
  94.7 7.4 %slice-start.2 = ((s8[9437184]{0:T(1024)(128)(4,1)}), s8[1048576]{0:T(1024)(128)(4,1)S(1)}, s32[]{:S(2)}) async-start(s8[9437184]{0:T(1024)(128)(4,1)} %bitcast.42), calls=%async_computation.7 | async-start | bytes 2097152
  105.3 28.1 %collective-permute-start = (f32[1024]{0:T(1024)S(1)}, f32[1024]{0:T(1024)S(1)}, u32[]{:S(2)}, u32[]{:S(2)}) collective-permute-start(f32[1024]{0:T(1024)S(1)} %fusion.20), channel_id=1, source_target_pairs={{0,1},{1,0},{2,3},{3,2},{4,5},{5,4},{6,7},{7,6},{8,9},{9,8},{10,11... | collective-permute-start | bytes 12296 | tf_op jit(solution)/shard_map/ppermute | solution.py:214
  133.4 3.7 %collective-permute-start.1 = (f32[1024]{0:T(1024)S(1)}, f32[1024]{0:T(1024)S(1)}, u32[]{:S(2)}, u32[]{:S(2)}) collective-permute-start(f32[1024]{0:T(1024)S(1)} %max.10), channel_id=1, source_target_pairs={{0,2},{1,3},{2,0},{3,1},{4,6},{5,7},{6,4},{7,5},{8,10},{9,11},{10,... | collective-permute-start | bytes 12296 | tf_op jit(solution)/shard_map/ppermute | solution.py:214
Sparse Core Ops, SparseCore 0:
  11.7 45.0 all-gather.2
Sparse Core Ops, SparseCore 1:
  48.6 40.8 reduce-scatter.4
  91.8 37.3 reduce-scatter.2

commit v15 on v12

--- a/solution.py
+++ b/solution.py
@@ -48,14 +48,17 @@
     out_ref, power_ref, sums_ref, mine_ref,
 ):
     pixels = noise_ref.shape[1]
-    row_sin = jnp.dot(row_sin_ref[...], expand_ref[...], preferred_element_type=jnp.float32)
-    row_cos = jnp.dot(row_cos_ref[...], expand_ref[...], preferred_element_type=jnp.float32)
+    row_sin_pieces = row_sin_ref[...]
+    row_cos_pieces = row_cos_ref[...]
     col_cos = col_cos_ref[...]
     col_sin = col_sin_ref[...]
     for tile in range(pixels // 128):
         lanes = slice(tile * 128, (tile + 1) * 128)
         imag = slice(pixels + tile * 128, pixels + (tile + 1) * 128)
-        contrast_rows = contrast_tile(row_sin, row_cos, col_cos, col_sin, tile)
+        expand = expand_ref[:, lanes]
+        row_sin = jnp.dot(row_sin_pieces, expand, preferred_element_type=jnp.float32)
+        row_cos = jnp.dot(row_cos_pieces, expand, preferred_element_type=jnp.float32)
+        contrast_rows = row_sin * col_cos + row_cos * col_sin
         factor = noise_ref[:, lanes] * contrast_rows
         out_ref[:, lanes] = (particles_ref[:, lanes].astype(jnp.float32) * factor).astype(jnp.bfloat16)
         out_ref[:, imag] = (particles_ref[:, imag].astype(jnp.float32) * factor).astype(jnp.bfloat16)

time: 141 us -> 141 us (level)
  no operation moved by 1% of the time
where the time goes in v15:
time: 141 us; the launch traced here: 139 us
  Pallas kernels  36.1 us (26%)
  other arithmetic  33.5 us (24%)
  matrix products  22.1 us (16%)
  between operations  16.4 us (12%)
  local copies, waits for them, and re-layouts  14.9 us (11%)
  waiting for transfers between devices  11.6 us (8%)
  starting transfers between devices  4.91 us (3%)
    pallas_call x1, Pallas kernels, weighted_rows(): pl.pallas_call(weights_kernel, grid=(rows // block,), in_specs=table_spec...  26.5 us
    pallas_call x1, Pallas kernels, power_rows(): pl.pallas_call(power_kernel, grid=(rows // block,), in_specs=table_specs(...  9.65 us
    dot_general x1, matrix products, on_device(): lax.dot_general(power_weight, power * jnp.bfloat16(-0.5), (((1,), (1,)),...  7.06 us
    ppermute x1, waiting for transfers between devices, on_device(): chip_sums = for_me + lax.ppermute(for_other, 'core', swap)  6.31 us
    dot_general x1, matrix products, on_device(): lax.dot_general(weighted, flat_images, (((1,), (1,)), ((), ())), preferre...  6.29 us
    sin x2, other arithmetic, contrast_tables(): jnp.sin(column_angle)  5.53 us
    reduce_scatter x1, waiting for transfers between devices, on_device(): lax.psum_scatter(chip_sums, 'chip', scatter_dimension=0, tiled=True)  5.27 us
    unnamed x11, local copies, waits for them, and re-layouts  5.21 us
  transfers between devices with their start and end apart: 5, of which 2 were waited for; matrix products, arithmetic and copies ran while one was open for 44% of the time, Pallas kernels for 26%

profile of v15, /device:TPU:0, one launch (start us, length us, event | category | flops | bytes accessed | tf_op | source)
XLA Modules:
  0.0 139.5 jit_solution(47819066044955893)
XLA Ops:
  9.8 1.8 %pad_maximum_fusion = bf16[24,9472]{1,0:T(8,128)(2,1)} fusion(bf16[24,256]{1,0:T(8,128)(2,1)S(1)} %reshape.254, bf16[24,9216]{1,0:T(8,128)(2,1)} %bitcast.31), kind=kLoop, calls=%fused_computation.66 | loop fusion | flops 909312 | bytes 909312 | tf_op jit(solution)/shard_map/concatenate | solution.py:166
  13.0 2.5 %reduce-precision_convert_fusion.1 = (bf16[1024,72]{1,0:T(8,128)(2,1)S(1)}, bf16[1024,72]{1,0:T(8,128)(2,1)S(1)}, bf16[1024,72]{1,0:T(8,128)(2,1)S(1)}, bf16[102...) fusion(f32[1024]{0:T(1024)S(1)} %get-tuple-element.32, ...), kind=kLoop, calls=%fused_computation.36 | loop fusion | flops 1400832 | bytes 889120 | tf_op jit(solution)/shard_map/convert_element_type | solution.py:19
  15.5 1.6 %fusion.32 = (bf16[1024,256]{1,0:T(8,128)(2,1)}, bf16[1024,256]{1,0:T(8,128)(2,1)}) fusion(bf16[1024,72]{1,0:T(8,128)(2,1)S(1)} %get-tuple-element.26, bf16[1024,72]{1,0:T(8,128)(2,1)S(1)} %get-tuple-element.25, bf16[1024,72]{1,0:T(8,128)(2,1)S(1)} %get-tuple-element.29, bf16[1024,72]{1,0:T(8,128)(2,1)S(1)} %get-tuple-element.28, ...), kind=kLoop, calls=%fused_computation.60 | loop fusion | flops 4980736 | bytes 1933312 | tf_op jit(solution)/shard_map/concatenate | solution.py:21
  18.0 3.0 %fusion.35 = (f32[1024,128]{1,0:T(8,128)}, f32[1024,128]{1,0:T(8,128)}) fusion(f32[128]{0:T(128)S(1)} %fusion.78, f32[1024]{0:T(1024)S(1)} %get-tuple-element.32), kind=kLoop, calls=%fused_computation.64 | loop fusion | flops 262144 | bytes 1053184 | tf_op jit(solution)/shard_map/sin | solution.py:38
  21.1 2.2 %and_convert_fusion.expand_ref = bf16[256,4608]{1,0:T(8,128)(2,1)} fusion(s32[4608]{0:T(1024)S(1)} %add_select_fusion.1, s32[256]{0:T(256)S(1)} %and_select_fusion.4, pred[256]{0:T(512)(128)(4,1)S(1)} %iota_compare_fusion.8), kind=kLoop, calls=%fused_computation.4 | loop fusion | flops 3538944 | bytes 2379008 | tf_op jit(solution)/shard_map/convert_element_type | solution.py:37
  23.3 26.5 %shard_map.86 = (bf16[1024,9216]{1,0:T(8,128)(2,1)}, bf16[1024,4608]{1,0:T(8,128)(2,1)}, f32[96,9216]{1,0:T(8,128)}, f32[96,9216]{1,0:T(8,128)}) custom-call(bf16[1024,256]{1,0:T(8,128)(2,1)} %get-tuple-element.37.row_sin_ref, bf16[1024,256]{1,0:T(8,128)(2,1)} %get-tuple-element.38.row_cos_ref, bf16[256,4608]{1,0:T(8,128)(2,1)} %and_convert_fusion.expand_ref, ...), custom_call_target="tpu_custom_call" | custom-call | tf_op jit(solution)/shard_map/pallas_call | solution.py:108
  50.3 6.3 %collective-permute-done.2 = f32[96,9216]{1,0:T(8,128)S(1)} collective-permute-done((f32[96,9216]{1,0:T(8,128)}, f32[96,9216]{1,0:T(8,128)S(1)}, u32[]{:S(2)}, u32[]{:S(2)}) %collective-permute-start.2) | collective-permute-done | bytes 3538976 | tf_op jit(solution)/shard_map/ppermute | solution.py:186
  56.6 4.2 %add.232 = f32[96,9216]{1,0:T(8,128)} add(f32[96,9216]{1,0:T(8,128)} %get-tuple-element.8, f32[96,9216]{1,0:T(8,128)S(1)} %collective-permute-done.2) | non-fusion elementwise | flops 884736 | bytes 10616832 | tf_op jit(solution)/shard_map/add | solution.py:186
  62.8 1.7 %gather_fusion = f32[192]{0:T(256)S(1)} fusion(f32[96]{0:T(128)S(1)} %divide_log_fusion, s32[1024]{0:T(1024)S(1)} %pad_clamp_fusion), kind=kCustom, calls=%fused_computation | custom fusion | bytes 2304 | tf_op jit(solution)/shard_map/jit(_take)/gather | solution.py:198
  65.1 2.2 %slice.60 = bf16[8,24,9216]{2,1,0:T(8,128)(2,1)S(1)} slice(bf16[8,24,9472]{2,1,0:T(8,128)(2,1)} %bitcast.27), slice={[0:8], [0:24], [0:9216]} | slice | bytes 7077888 | tf_op jit(solution)/shard_map/slice | solution.py:170
  70.9 1.6 %reduce-window.9 = s32[64,128]{1,0:T(8,128)} reduce-window(s32[64,128]{1,0:T(8,128)} %reshape.263, s32[]{:T(128)} %constant.156.clone.1), window={size=1x128 pad=0_0x127_0}, to_apply=%region_3.4 | reduce-window | flops 1040384 | bytes 65540 | tf_op jit(solution)/shard_map/reduce-window
  72.6 1.4 %slice.66 = s32[64,1]{1,0:T(8,128)} slice(s32[64,128]{1,0:T(8,128)} %reduce-window.9), slice={[0:64], [127:128]} | slice | bytes 512 | tf_op jit(solution)/shard_map/slice
  78.7 7.1 %fusion.3 = f32[1024,192]{0,1:T(8,128)S(1)} fusion(bf16[1024,4608]{1,0:T(8,128)(2,1)} %get-tuple-element.7, bf16[192,9216]{1,0:T(8,128)(2,1)S(1)} %bitcast.29), kind=kOutput, calls=%fused_computation.7 | convolution fusion | flops 1818132480 | bytes 13762560 | tf_op jit(solution)/shard_map/dot_general | solution.py:195
  85.8 2.1 %copy-done.2 = bf16[1024,9216]{1,0:T(8,128)(2,1)S(1)} copy-done((bf16[1024,9216]{1,0:T(8,128)(2,1)S(1)}, bf16[1024,9216]{1,0:T(8,128)(2,1)}, u32[]{:S(2)}) %copy-start.2) | copy-done | bytes 18874392
  87.9 6.3 %fusion.8 = f32[1024]{0:T(1024)S(1)} fusion(f32[1024,192]{0,1:T(8,128)S(1)} %fusion.3, bf16[1024,9216]{1,0:T(8,128)(2,1)S(1)} %copy-done.2, bf16[192,9216]{1,0:T(8,128)(2,1)S(1)} %bitcast.30, f32[192]{0:T(256)S(1)} %copy-done.1), kind=kOutput, calls=%fused_computation.12 | convolution fusion | flops 3624467456 | bytes 23204608 | tf_op jit(solution)/shard_map/dot_general | solution.py:193
  94.2 2.7 %collective-permute-start = (f32[1024]{0:T(1024)S(1)}, f32[1024]{0:T(1024)S(1)}, u32[]{:S(2)}, u32[]{:S(2)}) collective-permute-start(f32[1024]{0:T(1024)S(1)} %fusion.8), channel_id=1, source_target_pairs={{0,1},{1,0},{2,3},{3,2},{4,5},{5,4},{6,7},{7,6},{8,9},{9,8},{10,11... | collective-permute-start | bytes 12296 | tf_op jit(solution)/shard_map/ppermute | solution.py:203
  96.9 4.7 %fusion = f32[5,768]{1,0:T(8,128)S(1)} fusion(bf16[5,8192]{1,0:T(8,128)(2,1)S(1)} %bitcast.35, s32[8192]{0:T(1024)S(1)} %get-tuple-element.10), kind=kOutput, calls=%fused_computation.2 | convolution fusion | flops 69206016 | bytes 130048 | tf_op jit(solution)/shard_map/dot_general | solution.py:214
  102.2 1.9 %reduce-precision_convert_fusion.5 = (bf16[768,72]{1,0:T(8,128)(2,1)S(1)}, bf16[768,72]{1,0:T(8,128)(2,1)S(1)}, bf16[768,72]{1,0:T(8,128)(2,1)S(1)}, bf16[768,72...) fusion(f32[768]{0:T(1024)S(1)} %select_multiply_fusion, f32[72]{0:T(128)S(1)} %multiply_multiply_fusion), kind=kLoop, calls=%fused_computation.46 | loop fusion | flops 1050624 | bytes 666912 | tf_op jit(solution)/shard_map/convert_element_type | solution.py:19
  105.5 2.5 %fusion.47 = (f32[768,128]{1,0:T(8,128)}, f32[768,128]{1,0:T(8,128)}) fusion(f32[128]{0:T(128)S(1)} %fusion.78, f32[768]{0:T(1024)S(1)} %select_multiply_fusion), kind=kLoop, calls=%fused_computation.78 | loop fusion | flops 196608 | bytes 790016 | tf_op jit(solution)/shard_map/sin | solution.py:38
  108.6 9.6 %shard_map.87 = bf16[768,4608]{1,0:T(8,128)(2,1)} custom-call(bf16[768,256]{1,0:T(8,128)(2,1)} %get-tuple-element.39.row_sin_ref, bf16[768,256]{1,0:T(8,128)(2,1)} %get-tuple-element.40.row_cos_ref, bf16[256,4608]{1,0:T(8,128)(2,1)} %and_convert_fusion.expand_ref, f32[768,128]{1,0:T(8,128)} %get-tuple-element.15.col_cos_ref, ...), custom_call_target="tpu_custom_call" | custom-call | tf_op jit(solution)/shard_map/pallas_call | solution.py:134
  118.3 1.6 %collective-permute-start.1 = (f32[1024]{0:T(1024)S(1)}, f32[1024]{0:T(1024)S(1)}, u32[]{:S(2)}, u32[]{:S(2)}) collective-permute-start(f32[1024]{0:T(1024)S(1)} %max.10), channel_id=1, source_target_pairs={{0,2},{1,3},{2,0},{3,1},{4,6},{5,7},{6,4},{7,5},{8,10},{9,11},{10,... | collective-permute-start | bytes 12296 | tf_op jit(solution)/shard_map/ppermute | solution.py:203
  119.9 4.1 %fusion.49 = f32[24,4608]{1,0:T(8,128)S(1)} fusion(bf16[768,4608]{1,0:T(8,128)(2,1)} %shard_map.87, s32[768]{0:T(1024)S(1)} %fusion.69), kind=kOutput, calls=%fused_computation.82 | convolution fusion | flops 169887744 | bytes 7523328 | tf_op jit(solution)/shard_map/dot_general | solution.py:224
  124.6 5.3 %reduce-scatter.2.cloned.1.call-done = f32[24,9216]{1,0:T(8,128)} async-done(((f32[96,9216]{1,0:T(8,128)}), f32[24,9216]{1,0:T(8,128)}) %reduce-scatter.2.cloned.1.call-update) | async-done | bytes 884752 | tf_op jit(solution)/shard_map/reduce_scatter | solution.py:187
  129.8 2.2 %fusion.16 = f32[3,8,9216]{2,1,0:T(8,128)} fusion(f32[24,9216]{1,0:T(8,128)} %reduce-scatter.2.cloned.1.call-done, f32[24,4608]{1,0:T(8,128)S(1)} %fusion.49), kind=kLoop, calls=%fused_computation.22 | loop fusion | flops 663552 | bytes 2211840 | tf_op jit(solution)/shard_map/reshape | solution.py:227
  (56 shorter events, 17.9 us)
Async XLA Ops:
  8.0 57.1 %all-gather.3.cloned.1.call-start = ((), (), s32[]{:S(2)}) async-start(), calls=%async_computation.2 | async-start | bytes 4091904 | tf_op jit(solution)/shard_map/all_gather | solution.py:169
  11.6 118.2 %reduce-scatter.2.cloned.1.call-start = ((), (), s32[]{:S(2)}) async-start(), calls=%async_computation.1 | async-start | bytes 4423680 | tf_op jit(solution)/shard_map/reduce_scatter | solution.py:187
  49.8 6.8 %collective-permute-start.2 = (f32[96,9216]{1,0:T(8,128)}, f32[96,9216]{1,0:T(8,128)S(1)}, u32[]{:S(2)}, u32[]{:S(2)}) collective-permute-start(f32[96,9216]{1,0:T(8,128)} %get-tuple-element.9), channel_id=1, source_target_pairs={{0,4},{4,0},{1,5},{5,1},{2,6},{6,2},{3,7},{7,3},{8,12},{12,8},{9,1... | collective-permute-start | bytes 10616840 | tf_op jit(solution)/shard_map/ppermute | solution.py:186
  60.8 0.7 copy-start.3
  68.3 0.6 copy-start
  78.7 7.1 %copy-start.1 = (f32[192]{0:T(256)S(1)}, f32[192]{0:T(256)}, u32[]{:S(2)}) copy-start(f32[192]{0:T(256)} %and_select_fusion.1) | copy-start | bytes 2308
  78.7 9.2 %copy-start.2 = (bf16[1024,9216]{1,0:T(8,128)(2,1)S(1)}, bf16[1024,9216]{1,0:T(8,128)(2,1)}, u32[]{:S(2)}) copy-start(bf16[1024,9216]{1,0:T(8,128)(2,1)} %get-tuple-element.6) | copy-start | bytes 56623108
  94.2 24.1 %collective-permute-start = (f32[1024]{0:T(1024)S(1)}, f32[1024]{0:T(1024)S(1)}, u32[]{:S(2)}, u32[]{:S(2)}) collective-permute-start(f32[1024]{0:T(1024)S(1)} %fusion.8), channel_id=1, source_target_pairs={{0,1},{1,0},{2,3},{3,2},{4,5},{5,4},{6,7},{7,6},{8,9},{9,8},{10,11... | collective-permute-start | bytes 12296 | tf_op jit(solution)/shard_map/ppermute | solution.py:203
  118.3 5.7 %collective-permute-start.1 = (f32[1024]{0:T(1024)S(1)}, f32[1024]{0:T(1024)S(1)}, u32[]{:S(2)}, u32[]{:S(2)}) collective-permute-start(f32[1024]{0:T(1024)S(1)} %max.10), channel_id=1, source_target_pairs={{0,2},{1,3},{2,0},{3,1},{4,6},{5,7},{6,4},{7,5},{8,10},{9,11},{10,... | collective-permute-start | bytes 12296 | tf_op jit(solution)/shard_map/ppermute | solution.py:203
Sparse Core Ops, SparseCore 0:
  11.7 45.0 all-gather.2
Sparse Core Ops, SparseCore 1:
  60.9 68.9 reduce-scatter.1

commit v16 on v15

--- a/solution.py
+++ b/solution.py
@@ -27,7 +27,7 @@
     scaled = 12.0 * defocus
     row_offset = (jnp.arange(groups, dtype=jnp.int32) - pixels // 128).astype(jnp.float32)
     row_angle = scaled[:, None] * (row_offset * row_offset / 4096.0)[None, :]
-    column = (jnp.arange(128, dtype=jnp.int32) % 64).astype(jnp.float32)
+    column = jnp.arange(64, dtype=jnp.int32).astype(jnp.float32)
     column_angle = scaled[:, None] * (column * column / 4096.0)[None, :] + PHASE
     width = -(-3 * groups // 128) * 128
     row_sin = split_pieces(-AMPLITUDE * jnp.sin(row_angle), width)
@@ -35,7 +35,9 @@
     slot = jnp.arange(width, dtype=jnp.int32)[:, None]
     group_of = (jnp.arange(pixels, dtype=jnp.int32) // 64)[None, :]
     expand = ((slot < 3 * groups) & (slot % groups == group_of)).astype(jnp.bfloat16)
-    return row_sin, row_cos, expand, jnp.cos(column_angle), jnp.sin(column_angle)
+    col_cos = jnp.cos(column_angle)
+    col_sin = jnp.sin(column_angle)
+    return row_sin, row_cos, expand, jnp.concatenate([col_cos, col_cos], 1), jnp.concatenate([col_sin, col_sin], 1)
 
 
 def contrast_tile(row_sin, row_cos, col_cos, col_sin, tile):
@@ -102,7 +104,7 @@
     rows = particles.shape[0]
     poses = selector.shape[0]
     pixels = inv_noise.shape[0]
-    block = min(ROW_BLOCK, rows)
+    block = min(2 * ROW_BLOCK if poses * pixels * 8 <= 16 * 2**20 else ROW_BLOCK, rows)
     tables = contrast_tables(defocus, pixels)
     width = tables[0].shape[1]
     return pl.pallas_call(

time: 141 us -> 139 us (0.986)
  Pallas kernels: 36.1 us -> 34.3 us
    concatenate x0 -> x2, other arithmetic: none -> 2.52 us  [contrast_tables(): jnp.concatenate([col_cos, col_cos], 1)]
    sin x2, other arithmetic: 5.53 us -> 3.34 us  [contrast_tables(): col_sin = jnp.sin(column_angle)]
    pallas_call x1, Pallas kernels: 26.5 us -> 24.7 us  [weighted_rows(): pl.pallas_call(weights_kernel, grid=(rows // block,), in_specs=table_spec...]
  transfers between devices with their start and end apart: 5 -> 5, of which waited for: 2 -> 2; matrix products, arithmetic and copies ran while one was open for 44% -> 45% of each run, Pallas kernels for 26% -> 25%
where the time goes in v16:
time: 139 us; the launch traced here: 138 us
  Pallas kernels  34.3 us (25%)
  other arithmetic  33.8 us (24%)
  matrix products  22 us (16%)
  between operations  16.4 us (12%)
  local copies, waits for them, and re-layouts  14.9 us (11%)
  waiting for transfers between devices  11 us (8%)
  starting transfers between devices  5.42 us (4%)
    pallas_call x1, Pallas kernels, weighted_rows(): pl.pallas_call(weights_kernel, grid=(rows // block,), in_specs=table_spec...  24.7 us
    pallas_call x1, Pallas kernels, power_rows(): pl.pallas_call(power_kernel, grid=(rows // block,), in_specs=table_specs(...  9.62 us
    dot_general x1, matrix products, on_device(): lax.dot_general(power_weight, power * jnp.bfloat16(-0.5), (((1,), (1,)),...  7.05 us
    dot_general x1, matrix products, on_device(): lax.dot_general(weighted, flat_images, (((1,), (1,)), ((), ())), preferre...  6.29 us
    ppermute x1, waiting for transfers between devices, on_device(): chip_sums = for_me + lax.ppermute(for_other, 'core', swap)  6.11 us
    unnamed x11, local copies, waits for them, and re-layouts  5.21 us
    convert_element_type x3, other arithmetic, split_pieces(): pieces.append(piece.astype(jnp.bfloat16))  5 us
    reduce_scatter x1, waiting for transfers between devices, on_device(): lax.psum_scatter(chip_sums, 'chip', scatter_dimension=0, tiled=True)  4.82 us
  transfers between devices with their start and end apart: 5, of which 2 were waited for; matrix products, arithmetic and copies ran while one was open for 45% of the time, Pallas kernels for 25%

profile of v16, /device:TPU:0, one launch (start us, length us, event | category | flops | bytes accessed | tf_op | source)
XLA Modules:
  0.0 137.8 jit_solution(13677728264515478633)
XLA Ops:
  9.8 1.8 %pad_maximum_fusion.2 = bf16[24,9472]{1,0:T(8,128)(2,1)} fusion(bf16[24,256]{1,0:T(8,128)(2,1)S(1)} %reshape.248, bf16[24,9216]{1,0:T(8,128)(2,1)} %bitcast.31), kind=kLoop, calls=%fused_computation.68 | loop fusion | flops 909312 | bytes 909312 | tf_op jit(solution)/shard_map/concatenate | solution.py:168
  13.0 1.9 %fusion.35 = (f32[1024,64]{1,0:T(8,128)S(1)}, f32[1024,64]{1,0:T(8,128)S(1)}) fusion(f32[64]{0:T(128)S(1)} %multiply_multiply_fusion, f32[1024]{0:T(1024)S(1)} %get-tuple-element.32), kind=kLoop, calls=%fused_computation.66 | loop fusion | flops 131072 | bytes 528640 | tf_op jit(solution)/shard_map/sin | solution.py:39
  16.3 2.5 %reduce-precision_convert_fusion.1 = (bf16[1024,72]{1,0:T(8,128)(2,1)S(1)}, bf16[1024,72]{1,0:T(8,128)(2,1)S(1)}, bf16[1024,72]{1,0:T(8,128)(2,1)S(1)}, bf16[102...) fusion(f32[1024]{0:T(1024)S(1)} %get-tuple-element.32, ...), kind=kLoop, calls=%fused_computation.36 | loop fusion | flops 1400832 | bytes 889120 | tf_op jit(solution)/shard_map/convert_element_type | solution.py:19
  18.7 1.6 %fusion.32 = (bf16[1024,256]{1,0:T(8,128)(2,1)}, bf16[1024,256]{1,0:T(8,128)(2,1)}) fusion(bf16[1024,72]{1,0:T(8,128)(2,1)S(1)} %get-tuple-element.26, bf16[1024,72]{1,0:T(8,128)(2,1)S(1)} %get-tuple-element.25, bf16[1024,72]{1,0:T(8,128)(2,1)S(1)} %get-tuple-element.29, bf16[1024,72]{1,0:T(8,128)(2,1)S(1)} %get-tuple-element.28, ...), kind=kLoop, calls=%fused_computation.60 | loop fusion | flops 4980736 | bytes 1933312 | tf_op jit(solution)/shard_map/concatenate | solution.py:21
  21.2 2.2 %and_convert_fusion.expand_ref = bf16[256,4608]{1,0:T(8,128)(2,1)} fusion(s32[4608]{0:T(1024)S(1)} %add_select_fusion.1, s32[256]{0:T(256)S(1)} %and_select_fusion.3, pred[256]{0:T(512)(128)(4,1)S(1)} %iota_compare_fusion.8), kind=kLoop, calls=%fused_computation.4 | loop fusion | flops 3538944 | bytes 2379008 | tf_op jit(solution)/shard_map/convert_element_type | solution.py:37
  23.4 24.7 %shard_map.86 = (bf16[1024,9216]{1,0:T(8,128)(2,1)}, bf16[1024,4608]{1,0:T(8,128)(2,1)}, f32[96,9216]{1,0:T(8,128)}, f32[96,9216]{1,0:T(8,128)}) custom-call(bf16[1024,256]{1,0:T(8,128)(2,1)} %get-tuple-element.37.row_sin_ref, bf16[1024,256]{1,0:T(8,128)(2,1)} %get-tuple-element.38.row_cos_ref, bf16[256,4608]{1,0:T(8,128)(2,1)} %and_convert_fusion.expand_ref, ...), custom_call_target="tpu_custom_call" | custom-call | tf_op jit(solution)/shard_map/pallas_call | solution.py:110
  48.7 6.1 %collective-permute-done.2 = f32[96,9216]{1,0:T(8,128)S(1)} collective-permute-done((f32[96,9216]{1,0:T(8,128)}, f32[96,9216]{1,0:T(8,128)S(1)}, u32[]{:S(2)}, u32[]{:S(2)}) %collective-permute-start.2) | collective-permute-done | bytes 3538976 | tf_op jit(solution)/shard_map/ppermute | solution.py:188
  54.8 4.2 %add.217 = f32[96,9216]{1,0:T(8,128)} add(f32[96,9216]{1,0:T(8,128)} %get-tuple-element.8, f32[96,9216]{1,0:T(8,128)S(1)} %collective-permute-done.2) | non-fusion elementwise | flops 884736 | bytes 10616832 | tf_op jit(solution)/shard_map/add | solution.py:188
  61.0 1.7 %gather_fusion = f32[192]{0:T(256)S(1)} fusion(f32[96]{0:T(128)S(1)} %divide_log_fusion, s32[1024]{0:T(1024)S(1)} %pad_clamp_fusion), kind=kCustom, calls=%fused_computation | custom fusion | bytes 2304 | tf_op jit(solution)/shard_map/jit(_take)/gather | solution.py:200
  63.3 2.2 %slice.60 = bf16[8,24,9216]{2,1,0:T(8,128)(2,1)S(1)} slice(bf16[8,24,9472]{2,1,0:T(8,128)(2,1)} %bitcast.27), slice={[0:8], [0:24], [0:9216]} | slice | bytes 7077888 | tf_op jit(solution)/shard_map/slice | solution.py:172
  69.1 1.6 %reduce-window.9 = s32[64,128]{1,0:T(8,128)} reduce-window(s32[64,128]{1,0:T(8,128)} %reshape.257, s32[]{:T(128)} %constant.141.clone.1), window={size=1x128 pad=0_0x127_0}, to_apply=%region_3.4 | reduce-window | flops 1040384 | bytes 65540 | tf_op jit(solution)/shard_map/reduce-window
  70.8 1.4 %slice.66 = s32[64,1]{1,0:T(8,128)} slice(s32[64,128]{1,0:T(8,128)} %reduce-window.9), slice={[0:64], [127:128]} | slice | bytes 512 | tf_op jit(solution)/shard_map/slice
  76.9 7.1 %fusion.3 = f32[1024,192]{0,1:T(8,128)S(1)} fusion(bf16[1024,4608]{1,0:T(8,128)(2,1)} %get-tuple-element.7, bf16[192,9216]{1,0:T(8,128)(2,1)S(1)} %bitcast.29), kind=kOutput, calls=%fused_computation.7 | convolution fusion | flops 1818132480 | bytes 13762560 | tf_op jit(solution)/shard_map/dot_general | solution.py:197
  84.0 2.1 %copy-done.2 = bf16[1024,9216]{1,0:T(8,128)(2,1)S(1)} copy-done((bf16[1024,9216]{1,0:T(8,128)(2,1)S(1)}, bf16[1024,9216]{1,0:T(8,128)(2,1)}, u32[]{:S(2)}) %copy-start.2) | copy-done | bytes 18874392
  86.1 6.3 %fusion.8 = f32[1024]{0:T(1024)S(1)} fusion(f32[1024,192]{0,1:T(8,128)S(1)} %fusion.3, bf16[1024,9216]{1,0:T(8,128)(2,1)S(1)} %copy-done.2, bf16[192,9216]{1,0:T(8,128)(2,1)S(1)} %bitcast.30, f32[192]{0:T(256)S(1)} %copy-done.1), kind=kOutput, calls=%fused_computation.12 | convolution fusion | flops 3624467456 | bytes 23204608 | tf_op jit(solution)/shard_map/dot_general | solution.py:195
  92.4 3.2 %collective-permute-start = (f32[1024]{0:T(1024)S(1)}, f32[1024]{0:T(1024)S(1)}, u32[]{:S(2)}, u32[]{:S(2)}) collective-permute-start(f32[1024]{0:T(1024)S(1)} %fusion.8), channel_id=1, source_target_pairs={{0,1},{1,0},{2,3},{3,2},{4,5},{5,4},{6,7},{7,6},{8,9},{9,8},{10,11... | collective-permute-start | bytes 12296 | tf_op jit(solution)/shard_map/ppermute | solution.py:205
  95.6 4.7 %fusion = f32[5,768]{1,0:T(8,128)S(1)} fusion(bf16[5,8192]{1,0:T(8,128)(2,1)S(1)} %bitcast.35, s32[8192]{0:T(1024)S(1)} %get-tuple-element.10), kind=kOutput, calls=%fused_computation.2 | convolution fusion | flops 69206016 | bytes 130048 | tf_op jit(solution)/shard_map/dot_general | solution.py:216
  100.9 1.4 %fusion.47 = (f32[768,64]{1,0:T(8,128)S(1)}, f32[768,64]{1,0:T(8,128)S(1)}) fusion(f32[64]{0:T(128)S(1)} %multiply_multiply_fusion, f32[768]{0:T(1024)S(1)} %select_multiply_fusion), kind=kLoop, calls=%fused_computation.82 | loop fusion | flops 98304 | bytes 396544 | tf_op jit(solution)/shard_map/sin | solution.py:39
  103.6 1.8 %reduce-precision_convert_fusion.5 = (bf16[768,72]{1,0:T(8,128)(2,1)S(1)}, bf16[768,72]{1,0:T(8,128)(2,1)S(1)}, bf16[768,72]{1,0:T(8,128)(2,1)S(1)}, bf16[768,72...) fusion(f32[768]{0:T(1024)S(1)} %select_multiply_fusion, f32[72]{0:T(128)S(1)} %multiply_multiply_fusion.1), kind=kLoop, calls=%fused_computation.46 | loop fusion | flops 1050624 | bytes 666912 | tf_op jit(solution)/shard_map/convert_element_type | solution.py:19
  107.5 9.6 %shard_map.87 = bf16[768,4608]{1,0:T(8,128)(2,1)} custom-call(bf16[768,256]{1,0:T(8,128)(2,1)} %get-tuple-element.41.row_sin_ref, bf16[768,256]{1,0:T(8,128)(2,1)} %get-tuple-element.42.row_cos_ref, bf16[256,4608]{1,0:T(8,128)(2,1)} %and_convert_fusion.expand_ref, f32[768,128]{1,0:T(8,128)} %get-tuple-element.43.col_cos_ref, ...), custom_call_target="tpu_custom_call" | custom-call | tf_op jit(solution)/shard_map/pallas_call | solution.py:136
  117.1 1.6 %collective-permute-start.1 = (f32[1024]{0:T(1024)S(1)}, f32[1024]{0:T(1024)S(1)}, u32[]{:S(2)}, u32[]{:S(2)}) collective-permute-start(f32[1024]{0:T(1024)S(1)} %max.10), channel_id=1, source_target_pairs={{0,2},{1,3},{2,0},{3,1},{4,6},{5,7},{6,4},{7,5},{8,10},{9,11},{10,... | collective-permute-start | bytes 12296 | tf_op jit(solution)/shard_map/ppermute | solution.py:205
  118.7 4.0 %fusion.49 = f32[24,4608]{1,0:T(8,128)S(1)} fusion(bf16[768,4608]{1,0:T(8,128)(2,1)} %shard_map.87, s32[768]{0:T(1024)S(1)} %fusion.69), kind=kOutput, calls=%fused_computation.86 | convolution fusion | flops 169887744 | bytes 7523328 | tf_op jit(solution)/shard_map/dot_general | solution.py:226
  123.3 4.8 %reduce-scatter.2.cloned.1.call-done = f32[24,9216]{1,0:T(8,128)} async-done(((f32[96,9216]{1,0:T(8,128)}), f32[24,9216]{1,0:T(8,128)}) %reduce-scatter.2.cloned.1.call-update) | async-done | bytes 884752 | tf_op jit(solution)/shard_map/reduce_scatter | solution.py:189
  128.1 2.2 %fusion.16 = f32[3,8,9216]{2,1,0:T(8,128)} fusion(f32[24,9216]{1,0:T(8,128)} %reduce-scatter.2.cloned.1.call-done, f32[24,4608]{1,0:T(8,128)S(1)} %fusion.49), kind=kLoop, calls=%fused_computation.22 | loop fusion | flops 663552 | bytes 2211840 | tf_op jit(solution)/shard_map/reshape | solution.py:229
  (58 shorter events, 20.4 us)
Async XLA Ops:
  8.0 55.3 %all-gather.3.cloned.1.call-start = ((), (), s32[]{:S(2)}) async-start(), calls=%async_computation.2 | async-start | bytes 4091904 | tf_op jit(solution)/shard_map/all_gather | solution.py:171
  11.6 116.5 %reduce-scatter.2.cloned.1.call-start = ((), (), s32[]{:S(2)}) async-start(), calls=%async_computation.1 | async-start | bytes 4423680 | tf_op jit(solution)/shard_map/reduce_scatter | solution.py:189
  48.1 6.7 %collective-permute-start.2 = (f32[96,9216]{1,0:T(8,128)}, f32[96,9216]{1,0:T(8,128)S(1)}, u32[]{:S(2)}, u32[]{:S(2)}) collective-permute-start(f32[96,9216]{1,0:T(8,128)} %get-tuple-element.9), channel_id=1, source_target_pairs={{0,4},{4,0},{1,5},{5,1},{2,6},{6,2},{3,7},{7,3},{8,12},{12,8},{9,1... | collective-permute-start | bytes 10616840 | tf_op jit(solution)/shard_map/ppermute | solution.py:188
  59.0 0.7 copy-start.3
  66.5 0.6 copy-start
  76.9 7.1 %copy-start.1 = (f32[192]{0:T(256)S(1)}, f32[192]{0:T(256)}, u32[]{:S(2)}) copy-start(f32[192]{0:T(256)} %and_select_fusion.1) | copy-start | bytes 2308
  76.9 9.2 %copy-start.2 = (bf16[1024,9216]{1,0:T(8,128)(2,1)S(1)}, bf16[1024,9216]{1,0:T(8,128)(2,1)}, u32[]{:S(2)}) copy-start(bf16[1024,9216]{1,0:T(8,128)(2,1)} %get-tuple-element.6) | copy-start | bytes 56623108
  92.4 24.7 %collective-permute-start = (f32[1024]{0:T(1024)S(1)}, f32[1024]{0:T(1024)S(1)}, u32[]{:S(2)}, u32[]{:S(2)}) collective-permute-start(f32[1024]{0:T(1024)S(1)} %fusion.8), channel_id=1, source_target_pairs={{0,1},{1,0},{2,3},{3,2},{4,5},{5,4},{6,7},{7,6},{8,9},{9,8},{10,11... | collective-permute-start | bytes 12296 | tf_op jit(solution)/shard_map/ppermute | solution.py:205
  117.1 5.6 %collective-permute-start.1 = (f32[1024]{0:T(1024)S(1)}, f32[1024]{0:T(1024)S(1)}, u32[]{:S(2)}, u32[]{:S(2)}) collective-permute-start(f32[1024]{0:T(1024)S(1)} %max.10), channel_id=1, source_target_pairs={{0,2},{1,3},{2,0},{3,1},{4,6},{5,7},{6,4},{7,5},{8,10},{9,11},{10,... | collective-permute-start | bytes 12296 | tf_op jit(solution)/shard_map/ppermute | solution.py:205
Sparse Core Ops, SparseCore 0:
  11.7 45.0 all-gather.2
Sparse Core Ops, SparseCore 1:
  59.1 68.9 reduce-scatter.1

commit v17 on v16

--- a/solution.py
+++ b/solution.py
@@ -47,7 +47,7 @@
 
 def weights_kernel(
     row_sin_ref, row_cos_ref, expand_ref, col_cos_ref, col_sin_ref, noise_ref, particles_ref, selector_ref,
-    out_ref, power_ref, sums_ref, mine_ref,
+    out_ref, power_ref, sums_ref,
 ):
     pixels = noise_ref.shape[1]
     row_sin_pieces = row_sin_ref[...]
@@ -69,11 +69,8 @@
     @pl.when(pl.program_id(0) == 0)
     def _():
         sums_ref[...] = jnp.zeros_like(sums_ref)
-        mine_ref[...] = jnp.zeros_like(mine_ref)
-
-    half = sums_ref.shape[0]
-    sums_ref[...] += jnp.dot(selector_ref[:half, :], out_ref[...], preferred_element_type=jnp.float32)
-    mine_ref[...] += jnp.dot(selector_ref[half:, :], out_ref[...], preferred_element_type=jnp.float32)
+
+    sums_ref[...] += jnp.dot(selector_ref[...], out_ref[...], preferred_element_type=jnp.float32)
 
 
 def power_kernel(row_sin_ref, row_cos_ref, expand_ref, col_cos_ref, col_sin_ref, noise_ref, power_ref):
@@ -115,14 +112,12 @@
         out_specs=[
             pl.BlockSpec((block, 2 * pixels), lambda i: (i, 0)),
             pl.BlockSpec((block, pixels), lambda i: (i, 0)),
-            pl.BlockSpec((poses // 2, 2 * pixels), lambda i: (0, 0)),
-            pl.BlockSpec((poses // 2, 2 * pixels), lambda i: (0, 0)),
+            pl.BlockSpec((poses, 2 * pixels), lambda i: (0, 0)),
         ],
         out_shape=[
             jax.ShapeDtypeStruct((rows, 2 * pixels), jnp.bfloat16),
             jax.ShapeDtypeStruct((rows, pixels), jnp.bfloat16),
-            jax.ShapeDtypeStruct((poses // 2, 2 * pixels), jnp.float32),
-            jax.ShapeDtypeStruct((poses // 2, 2 * pixels), jnp.float32),
+            jax.ShapeDtypeStruct((poses, 2 * pixels), jnp.float32),
         ],
     )(*tables, inv_noise[None, :], particles, selector)
 
@@ -178,15 +173,11 @@
     power = (real_part * real_part + imag_part * imag_part).astype(jnp.bfloat16)
 
     in_block = (local_class >= 0) & (local_class < block_classes)
-    owner = local_class // owned
-    mine = (owner % 2 == core).astype(jnp.int32)
-    pose = ((mine * chips + owner // 2) * owned + local_class % owned) * rotations + part_rot
-    pose = jnp.where(in_block, pose, -1)
+    pose = jnp.where(in_block, local_class * rotations + part_rot, -1)
     poses = jnp.arange(block_classes * rotations, dtype=jnp.int32)
     selector = (poses[:, None] == pose[None, :]).astype(jnp.bfloat16)
-    weighted, power_weight, for_other, for_me = weighted_rows(particles, defocus, inv_noise, selector)
-    chip_sums = for_me + lax.ppermute(for_other, "core", swap)
-    numerator = lax.psum_scatter(chip_sums, "chip", scatter_dimension=0, tiled=True)
+    weighted, power_weight, partial = weighted_rows(particles, defocus, inv_noise, selector)
+    numerator = lax.psum_scatter(partial, ("chip", "core"), scatter_dimension=0, tiled=True)
 
     class_total = counts.shape[0]
     log_prior = jnp.log(

time: 139 us -> 145 us (1.043)
  waiting for transfers between devices: 11 us -> 24.9 us
  other arithmetic: 33.8 us -> 29.7 us
  starting transfers between devices: 5.42 us -> 3.18 us
  between operations: 16.4 us -> 14.9 us
    reduce_scatter x1, waiting for transfers between devices: 4.82 us -> 19.7 us  [on_device(): lax.psum_scatter(partial, ('chip', 'core'), scatter_dimension=0, tiled=True)]
    ppermute x1 -> x0, waiting for transfers between devices: 6.11 us -> none  [on_device(): chip_sums = for_me + lax.ppermute(for_other, 'core', swap)]
    all_gather x1, waiting for transfers between devices: 0.01 us -> 5.15 us  [on_device(): gathered = lax.all_gather(sending, ('chip', 'core'), axis=0, tiled=False)]
    add x1 -> x0, other arithmetic: 4.23 us -> none  [on_device(): chip_sums = for_me + lax.ppermute(for_other, 'core', swap)]
    ppermute x2, starting transfers between devices: 4.79 us -> 3.1 us  [on_device(): best_score = jnp.maximum(best_score, lax.ppermute(best_score, 'cls', pairs))]
  transfers between devices with their start and end apart: 5 -> 4, of which waited for: 2 -> 2; matrix products, arithmetic and copies ran while one was open for 45% -> 40% of each run, Pallas kernels for 25% -> 23%
where the time goes in v17:
time: 145 us; the launch traced here: 144 us
  Pallas kernels  33.5 us (23%)
  other arithmetic  29.7 us (20%)
  waiting for transfers between devices  24.9 us (17%)
  matrix products  22.2 us (15%)
  local copies, waits for them, and re-layouts  15.1 us (10%)
  between operations  14.9 us (10%)
  starting transfers between devices  3.18 us (2%)
    pallas_call x1, Pallas kernels, weighted_rows(): pl.pallas_call(weights_kernel, grid=(rows // block,), in_specs=table_spec...  23.9 us
    reduce_scatter x1, waiting for transfers between devices, on_device(): lax.psum_scatter(partial, ('chip', 'core'), scatter_dimension=0, tiled=True)  19.7 us
    pallas_call x1, Pallas kernels, power_rows(): pl.pallas_call(power_kernel, grid=(rows // block,), in_specs=table_specs(...  9.66 us
    dot_general x1, matrix products, on_device(): lax.dot_general(power_weight, power * jnp.bfloat16(-0.5), (((1,), (1,)),...  7.18 us
    dot_general x1, matrix products, on_device(): lax.dot_general(weighted, flat_images, (((1,), (1,)), ((), ())), preferre...  6.29 us
    unnamed x11, local copies, waits for them, and re-layouts  5.31 us
    all_gather x1, waiting for transfers between devices, on_device(): gathered = lax.all_gather(sending, ('chip', 'core'), axis=0, tiled=False)  5.15 us
    convert_element_type x3, other arithmetic, split_pieces(): pieces.append(piece.astype(jnp.bfloat16))  5 us
  transfers between devices with their start and end apart: 4, of which 2 were waited for; matrix products, arithmetic and copies ran while one was open for 40% of the time, Pallas kernels for 23%

profile of v17, /device:TPU:0, one launch (start us, length us, event | category | flops | bytes accessed | tf_op | source)
XLA Modules:
  0.0 143.5 jit_solution(6921357708114006525)
XLA Ops:
  8.9 1.8 %pad_maximum_fusion.2 = bf16[24,9472]{1,0:T(8,128)(2,1)} fusion(bf16[24,256]{1,0:T(8,128)(2,1)S(1)} %reshape.248, bf16[24,9216]{1,0:T(8,128)(2,1)} %bitcast.31), kind=kLoop, calls=%fused_computation.68 | loop fusion | flops 909312 | bytes 909312 | tf_op jit(solution)/shard_map/concatenate | solution.py:163
  12.2 1.9 %fusion.35 = (f32[1024,64]{1,0:T(8,128)S(1)}, f32[1024,64]{1,0:T(8,128)S(1)}) fusion(f32[64]{0:T(128)S(1)} %multiply_multiply_fusion, f32[1024]{0:T(1024)S(1)} %get-tuple-element.30), kind=kLoop, calls=%fused_computation.66 | loop fusion | flops 131072 | bytes 528640 | tf_op jit(solution)/shard_map/sin | solution.py:39
  15.4 2.5 %reduce-precision_convert_fusion.1 = (bf16[1024,72]{1,0:T(8,128)(2,1)S(1)}, bf16[1024,72]{1,0:T(8,128)(2,1)S(1)}, bf16[1024,72]{1,0:T(8,128)(2,1)S(1)}, bf16[102...) fusion(f32[1024]{0:T(1024)S(1)} %get-tuple-element.30, ...), kind=kLoop, calls=%fused_computation.36 | loop fusion | flops 1400832 | bytes 889120 | tf_op jit(solution)/shard_map/convert_element_type | solution.py:19
  17.9 1.6 %fusion.32 = (bf16[1024,256]{1,0:T(8,128)(2,1)}, bf16[1024,256]{1,0:T(8,128)(2,1)}) fusion(bf16[1024,72]{1,0:T(8,128)(2,1)S(1)} %get-tuple-element.24, bf16[1024,72]{1,0:T(8,128)(2,1)S(1)} %get-tuple-element.23, bf16[1024,72]{1,0:T(8,128)(2,1)S(1)} %get-tuple-element.27, bf16[1024,72]{1,0:T(8,128)(2,1)S(1)} %get-tuple-element.26, ...), kind=kLoop, calls=%fused_computation.60 | loop fusion | flops 4980736 | bytes 1933312 | tf_op jit(solution)/shard_map/concatenate | solution.py:21
  20.4 2.2 %and_convert_fusion.expand_ref = bf16[256,4608]{1,0:T(8,128)(2,1)} fusion(s32[4608]{0:T(1024)S(1)} %add_select_fusion.1, s32[256]{0:T(256)S(1)} %and_select_fusion.3, pred[256]{0:T(512)(128)(4,1)S(1)} %iota_compare_fusion.8), kind=kLoop, calls=%fused_computation.4 | loop fusion | flops 3538944 | bytes 2379008 | tf_op jit(solution)/shard_map/convert_element_type | solution.py:37
  22.6 23.9 %shard_map.86 = (bf16[1024,9216]{1,0:T(8,128)(2,1)}, bf16[1024,4608]{1,0:T(8,128)(2,1)}, f32[192,9216]{1,0:T(8,128)}) custom-call(bf16[1024,256]{1,0:T(8,128)(2,1)} %get-tuple-element.35.row_sin_ref, bf16[1024,256]{1,0:T(8,128)(2,1)} %get-tuple-element.36.row_cos_ref, bf16[256,4608]{1,0:T(8,128)(2,1)} %and_convert_fusion.expand_ref, ...), custom_call_target="tpu_custom_call" | custom-call | tf_op jit(solution)/shard_map/pallas_call | solution.py:107
  48.5 1.7 %gather_fusion = f32[192]{0:T(256)S(1)} fusion(f32[96]{0:T(128)S(1)} %divide_log_fusion, s32[1024]{0:T(1024)S(1)} %pad_clamp_fusion), kind=kCustom, calls=%fused_computation | custom fusion | bytes 2304 | tf_op jit(solution)/shard_map/jit(_take)/gather | solution.py:191
  50.8 5.2 %all-gather.3.cloned.1.call-done = bf16[192,9472]{1,0:T(8,128)(2,1)} async-done(((bf16[24,9472]{1,0:T(8,128)(2,1)}), bf16[192,9472]{1,0:T(8,128)(2,1)}) %all-gather.3.cloned.1.call-update) | async-done | bytes 3637264 | tf_op jit(solution)/shard_map/all_gather | solution.py:166
  55.9 2.2 %slice.60 = bf16[8,24,9216]{2,1,0:T(8,128)(2,1)S(1)} slice(bf16[8,24,9472]{2,1,0:T(8,128)(2,1)} %bitcast.27), slice={[0:8], [0:24], [0:9216]} | slice | bytes 7077888 | tf_op jit(solution)/shard_map/slice | solution.py:167
  61.7 1.7 %reduce-window.9 = s32[64,128]{1,0:T(8,128)} reduce-window(s32[64,128]{1,0:T(8,128)} %reshape.257, s32[]{:T(128)} %constant.107.clone.1), window={size=1x128 pad=0_0x127_0}, to_apply=%region_3.4 | reduce-window | flops 1040384 | bytes 65540 | tf_op jit(solution)/shard_map/reduce-window
  63.4 1.4 %slice.66 = s32[64,1]{1,0:T(8,128)} slice(s32[64,128]{1,0:T(8,128)} %reduce-window.9), slice={[0:64], [127:128]} | slice | bytes 512 | tf_op jit(solution)/shard_map/slice
  64.8 1.4 %reduce-window.12 = s32[65,1]{1,0:T(8,128)} reduce-window(s32[64,1]{1,0:T(8,128)} %slice.66, s32[]{:T(128)} %constant.107.clone.1), window={size=64x1 pad=64_0x0_0}, to_apply=%region_4.5 | reduce-window | flops 4095 | bytes 520 | tf_op jit(solution)/shard_map/reduce-window.2
  69.6 7.2 %fusion.3 = f32[1024,192]{0,1:T(8,128)S(1)} fusion(bf16[1024,4608]{1,0:T(8,128)(2,1)} %get-tuple-element.6, bf16[192,9216]{1,0:T(8,128)(2,1)S(1)} %bitcast.29), kind=kOutput, calls=%fused_computation.7 | convolution fusion | flops 1818132480 | bytes 13762560 | tf_op jit(solution)/shard_map/dot_general | solution.py:188
  76.8 2.2 %copy-done.2 = bf16[1024,9216]{1,0:T(8,128)(2,1)S(1)} copy-done((bf16[1024,9216]{1,0:T(8,128)(2,1)S(1)}, bf16[1024,9216]{1,0:T(8,128)(2,1)}, u32[]{:S(2)}) %copy-start.2) | copy-done | bytes 18874392
  79.0 6.3 %fusion.8 = f32[1024]{0:T(1024)S(1)} fusion(f32[1024,192]{0,1:T(8,128)S(1)} %fusion.3, bf16[1024,9216]{1,0:T(8,128)(2,1)S(1)} %copy-done.2, bf16[192,9216]{1,0:T(8,128)(2,1)S(1)} %bitcast.30, f32[192]{0:T(256)S(1)} %copy-done.1), kind=kOutput, calls=%fused_computation.12 | convolution fusion | flops 3624467456 | bytes 23204608 | tf_op jit(solution)/shard_map/dot_general | solution.py:186
  85.3 1.5 %collective-permute-start = (f32[1024]{0:T(1024)S(1)}, f32[1024]{0:T(1024)S(1)}, u32[]{:S(2)}, u32[]{:S(2)}) collective-permute-start(f32[1024]{0:T(1024)S(1)} %fusion.8), channel_id=1, source_target_pairs={{0,1},{1,0},{2,3},{3,2},{4,5},{5,4},{6,7},{7,6},{8,9},{9,8},{10,11... | collective-permute-start | bytes 12296 | tf_op jit(solution)/shard_map/ppermute | solution.py:196
  86.8 4.7 %fusion = f32[5,768]{1,0:T(8,128)S(1)} fusion(bf16[5,8192]{1,0:T(8,128)(2,1)S(1)} %bitcast.35, s32[8192]{0:T(1024)S(1)} %get-tuple-element.8), kind=kOutput, calls=%fused_computation.2 | convolution fusion | flops 69206016 | bytes 130048 | tf_op jit(solution)/shard_map/dot_general | solution.py:207
  92.2 1.4 %fusion.47 = (f32[768,64]{1,0:T(8,128)S(1)}, f32[768,64]{1,0:T(8,128)S(1)}) fusion(f32[64]{0:T(128)S(1)} %multiply_multiply_fusion, f32[768]{0:T(1024)S(1)} %select_multiply_fusion), kind=kLoop, calls=%fused_computation.82 | loop fusion | flops 98304 | bytes 396544 | tf_op jit(solution)/shard_map/sin | solution.py:39
  94.9 1.8 %reduce-precision_convert_fusion.5 = (bf16[768,72]{1,0:T(8,128)(2,1)S(1)}, bf16[768,72]{1,0:T(8,128)(2,1)S(1)}, bf16[768,72]{1,0:T(8,128)(2,1)S(1)}, bf16[768,72...) fusion(f32[768]{0:T(1024)S(1)} %select_multiply_fusion, f32[72]{0:T(128)S(1)} %multiply_multiply_fusion.1), kind=kLoop, calls=%fused_computation.46 | loop fusion | flops 1050624 | bytes 666912 | tf_op jit(solution)/shard_map/convert_element_type | solution.py:19
  98.8 9.7 %shard_map.87 = bf16[768,4608]{1,0:T(8,128)(2,1)} custom-call(bf16[768,256]{1,0:T(8,128)(2,1)} %get-tuple-element.39.row_sin_ref, bf16[768,256]{1,0:T(8,128)(2,1)} %get-tuple-element.40.row_cos_ref, bf16[256,4608]{1,0:T(8,128)(2,1)} %and_convert_fusion.expand_ref, f32[768,128]{1,0:T(8,128)} %get-tuple-element.41.col_cos_ref, ...), custom_call_target="tpu_custom_call" | custom-call | tf_op jit(solution)/shard_map/pallas_call | solution.py:131
  108.5 1.6 %collective-permute-start.1 = (f32[1024]{0:T(1024)S(1)}, f32[1024]{0:T(1024)S(1)}, u32[]{:S(2)}, u32[]{:S(2)}) collective-permute-start(f32[1024]{0:T(1024)S(1)} %max.10), channel_id=1, source_target_pairs={{0,2},{1,3},{2,0},{3,1},{4,6},{5,7},{6,4},{7,5},{8,10},{9,11},{10,... | collective-permute-start | bytes 12296 | tf_op jit(solution)/shard_map/ppermute | solution.py:196
  110.0 4.1 %fusion.49 = f32[24,4608]{1,0:T(8,128)S(1)} fusion(bf16[768,4608]{1,0:T(8,128)(2,1)} %shard_map.87, s32[768]{0:T(1024)S(1)} %fusion.59), kind=kOutput, calls=%fused_computation.86 | convolution fusion | flops 169887744 | bytes 7523328 | tf_op jit(solution)/shard_map/dot_general | solution.py:217
  114.8 19.7 %reduce-scatter.2.cloned.1.call-done = f32[24,9216]{1,0:T(8,128)} async-done(((f32[192,9216]{1,0:T(8,128)}), f32[24,9216]{1,0:T(8,128)}) %reduce-scatter.2.cloned.1.call-update) | async-done | bytes 884752 | tf_op jit(solution)/shard_map/reduce_scatter | solution.py:180
  134.5 2.2 %fusion.16 = f32[3,8,9216]{2,1,0:T(8,128)} fusion(f32[24,9216]{1,0:T(8,128)} %reduce-scatter.2.cloned.1.call-done, f32[24,4608]{1,0:T(8,128)S(1)} %fusion.49), kind=kLoop, calls=%fused_computation.22 | loop fusion | flops 663552 | bytes 2211840 | tf_op jit(solution)/shard_map/reshape | solution.py:220
  (55 shorter events, 18.6 us)
Async XLA Ops:
  7.2 48.8 %all-gather.3.cloned.1.call-start = ((), (), s32[]{:S(2)}) async-start(), calls=%async_computation.2 | async-start | bytes 4091904 | tf_op jit(solution)/shard_map/all_gather | solution.py:166
  10.7 123.7 %reduce-scatter.2.cloned.1.call-start = ((), (), s32[]{:S(2)}) async-start(), calls=%async_computation.1 | async-start | bytes 7962624 | tf_op jit(solution)/shard_map/reduce_scatter | solution.py:180
  46.5 0.7 copy-start.3
  59.1 0.6 copy-start
  69.6 7.2 %copy-start.1 = (f32[192]{0:T(256)S(1)}, f32[192]{0:T(256)}, u32[]{:S(2)}) copy-start(f32[192]{0:T(256)} %and_select_fusion.1) | copy-start | bytes 2308
  69.6 9.4 %copy-start.2 = (bf16[1024,9216]{1,0:T(8,128)(2,1)S(1)}, bf16[1024,9216]{1,0:T(8,128)(2,1)}, u32[]{:S(2)}) copy-start(bf16[1024,9216]{1,0:T(8,128)(2,1)} %get-tuple-element.5) | copy-start | bytes 56623108
  85.3 23.2 %collective-permute-start = (f32[1024]{0:T(1024)S(1)}, f32[1024]{0:T(1024)S(1)}, u32[]{:S(2)}, u32[]{:S(2)}) collective-permute-start(f32[1024]{0:T(1024)S(1)} %fusion.8), channel_id=1, source_target_pairs={{0,1},{1,0},{2,3},{3,2},{4,5},{5,4},{6,7},{7,6},{8,9},{9,8},{10,11... | collective-permute-start | bytes 12296 | tf_op jit(solution)/shard_map/ppermute | solution.py:196
  108.5 5.7 %collective-permute-start.1 = (f32[1024]{0:T(1024)S(1)}, f32[1024]{0:T(1024)S(1)}, u32[]{:S(2)}, u32[]{:S(2)}) collective-permute-start(f32[1024]{0:T(1024)S(1)} %max.10), channel_id=1, source_target_pairs={{0,2},{1,3},{2,0},{3,1},{4,6},{5,7},{6,4},{7,5},{8,10},{9,11},{10,... | collective-permute-start | bytes 12296 | tf_op jit(solution)/shard_map/ppermute | solution.py:196
Sparse Core Ops, SparseCore 0:
  10.9 45.0 all-gather.2
  58.2 76.1 reduce-scatter.1

commit v18 on v16

--- a/solution.py
+++ b/solution.py
@@ -23,6 +23,65 @@
 
 
 def contrast_tables(defocus, pixels):
+    groups = pixels // 64
+    scaled = 12.0 * defocus
+    row_offset = (jnp.arange(groups, dtype=jnp.int32) - pixels // 128).astype(jnp.float32)
+    row_angle = scaled[:, None] * (row_offset * row_offset / 4096.0)[None, :]
+    column = jnp.arange(64, dtype=jnp.int32).astype(jnp.float32)
+    column_angle = scaled[:, None] * (column * column / 4096.0)[None, :] + PHASE
+    width = -(-groups // 128) * 128
+    pad = ((0, 0), (0, width - groups))
+    row_sin = jnp.pad(-AMPLITUDE * jnp.sin(row_angle), pad)
+    row_cos = jnp.pad(-AMPLITUDE * jnp.cos(row_angle), pad)
+    col_cos = jnp.cos(column_angle)
+    col_sin = jnp.sin(column_angle)
+    return row_sin, row_cos, jnp.concatenate([col_cos, col_cos], 1), jnp.concatenate([col_sin, col_sin], 1)
+
+
+def contrast_tile(row_sin_ref, row_cos_ref, col_cos, col_sin, tile):
+    first_half = lax.broadcasted_iota(jnp.int32, col_cos.shape, 1) < 64
+    row_sin = jnp.where(first_half, row_sin_ref[:, 2 * tile : 2 * tile + 1], row_sin_ref[:, 2 * tile + 1 : 2 * tile + 2])
+    row_cos = jnp.where(first_half, row_cos_ref[:, 2 * tile : 2 * tile + 1], row_cos_ref[:, 2 * tile + 1 : 2 * tile + 2])
+    return row_sin * col_cos + row_cos * col_sin
+
+
+def weights_kernel(
+    row_sin_ref, row_cos_ref, col_cos_ref, col_sin_ref, noise_ref, particles_ref, selector_ref,
+    out_ref, power_ref, sums_ref, mine_ref,
+):
+    pixels = noise_ref.shape[1]
+    col_cos = col_cos_ref[...]
+    col_sin = col_sin_ref[...]
+    for tile in range(pixels // 128):
+        lanes = slice(tile * 128, (tile + 1) * 128)
+        imag = slice(pixels + tile * 128, pixels + (tile + 1) * 128)
+        contrast_rows = contrast_tile(row_sin_ref, row_cos_ref, col_cos, col_sin, tile)
+        factor = noise_ref[:, lanes] * contrast_rows
+        out_ref[:, lanes] = (particles_ref[:, lanes].astype(jnp.float32) * factor).astype(jnp.bfloat16)
+        out_ref[:, imag] = (particles_ref[:, imag].astype(jnp.float32) * factor).astype(jnp.bfloat16)
+        power_ref[:, lanes] = (factor * contrast_rows).astype(jnp.bfloat16)
+
+    @pl.when(pl.program_id(0) == 0)
+    def _():
+        sums_ref[...] = jnp.zeros_like(sums_ref)
+        mine_ref[...] = jnp.zeros_like(mine_ref)
+
+    half = sums_ref.shape[0]
+    sums_ref[...] += jnp.dot(selector_ref[:half, :], out_ref[...], preferred_element_type=jnp.float32)
+    mine_ref[...] += jnp.dot(selector_ref[half:, :], out_ref[...], preferred_element_type=jnp.float32)
+
+
+def table_specs(block, width, pixels):
+    return [
+        pl.BlockSpec((block, width), lambda i: (i, 0)),
+        pl.BlockSpec((block, width), lambda i: (i, 0)),
+        pl.BlockSpec((block, 128), lambda i: (i, 0)),
+        pl.BlockSpec((block, 128), lambda i: (i, 0)),
+        pl.BlockSpec((1, pixels), lambda i: (0, 0)),
+    ]
+
+
+def expanded_tables(defocus, pixels):
     groups = pixels // 64
     scaled = 12.0 * defocus
     row_offset = (jnp.arange(groups, dtype=jnp.int32) - pixels // 128).astype(jnp.float32)
@@ -40,43 +99,7 @@
     return row_sin, row_cos, expand, jnp.concatenate([col_cos, col_cos], 1), jnp.concatenate([col_sin, col_sin], 1)
 
 
-def contrast_tile(row_sin, row_cos, col_cos, col_sin, tile):
-    lanes = slice(tile * 128, (tile + 1) * 128)
-    return row_sin[:, lanes] * col_cos + row_cos[:, lanes] * col_sin
-
-
-def weights_kernel(
-    row_sin_ref, row_cos_ref, expand_ref, col_cos_ref, col_sin_ref, noise_ref, particles_ref, selector_ref,
-    out_ref, power_ref, sums_ref, mine_ref,
-):
-    pixels = noise_ref.shape[1]
-    row_sin_pieces = row_sin_ref[...]
-    row_cos_pieces = row_cos_ref[...]
-    col_cos = col_cos_ref[...]
-    col_sin = col_sin_ref[...]
-    for tile in range(pixels // 128):
-        lanes = slice(tile * 128, (tile + 1) * 128)
-        imag = slice(pixels + tile * 128, pixels + (tile + 1) * 128)
-        expand = expand_ref[:, lanes]
-        row_sin = jnp.dot(row_sin_pieces, expand, preferred_element_type=jnp.float32)
-        row_cos = jnp.dot(row_cos_pieces, expand, preferred_element_type=jnp.float32)
-        contrast_rows = row_sin * col_cos + row_cos * col_sin
-        factor = noise_ref[:, lanes] * contrast_rows
-        out_ref[:, lanes] = (particles_ref[:, lanes].astype(jnp.float32) * factor).astype(jnp.bfloat16)
-        out_ref[:, imag] = (particles_ref[:, imag].astype(jnp.float32) * factor).astype(jnp.bfloat16)
-        power_ref[:, lanes] = (factor * contrast_rows).astype(jnp.bfloat16)
-
-    @pl.when(pl.program_id(0) == 0)
-    def _():
-        sums_ref[...] = jnp.zeros_like(sums_ref)
-        mine_ref[...] = jnp.zeros_like(mine_ref)
-
-    half = sums_ref.shape[0]
-    sums_ref[...] += jnp.dot(selector_ref[:half, :], out_ref[...], preferred_element_type=jnp.float32)
-    mine_ref[...] += jnp.dot(selector_ref[half:, :], out_ref[...], preferred_element_type=jnp.float32)
-
-
-def power_kernel(row_sin_ref, row_cos_ref, expand_ref, col_cos_ref, col_sin_ref, noise_ref, power_ref):
+def expanded_power_kernel(row_sin_ref, row_cos_ref, expand_ref, col_cos_ref, col_sin_ref, noise_ref, power_ref):
     pixels = noise_ref.shape[1]
     row_sin = jnp.dot(row_sin_ref[...], expand_ref[...], preferred_element_type=jnp.float32)
     row_cos = jnp.dot(row_cos_ref[...], expand_ref[...], preferred_element_type=jnp.float32)
@@ -84,12 +107,12 @@
     col_sin = col_sin_ref[...]
     for tile in range(pixels // 128):
         lanes = slice(tile * 128, (tile + 1) * 128)
-        contrast_rows = contrast_tile(row_sin, row_cos, col_cos, col_sin, tile)
+        contrast_rows = row_sin[:, lanes] * col_cos + row_cos[:, lanes] * col_sin
         factor = noise_ref[:, lanes] * contrast_rows
         power_ref[:, lanes] = (factor * contrast_rows).astype(jnp.bfloat16)
 
 
-def table_specs(block, width, pixels):
+def expanded_specs(block, width, pixels):
     return [
         pl.BlockSpec((block, width), lambda i: (i, 0)),
         pl.BlockSpec((block, width), lambda i: (i, 0)),
@@ -131,12 +154,12 @@
     rows = defocus.shape[0]
     pixels = inv_noise.shape[0]
     block = min(ROW_BLOCK, rows)
-    tables = contrast_tables(defocus, pixels)
+    tables = expanded_tables(defocus, pixels)
     width = tables[0].shape[1]
     return pl.pallas_call(
-        power_kernel,
+        expanded_power_kernel,
         grid=(rows // block,),
-        in_specs=table_specs(block, width, pixels),
+        in_specs=expanded_specs(block, width, pixels),
         out_specs=pl.BlockSpec((block, pixels), lambda i: (i, 0)),
         out_shape=jax.ShapeDtypeStruct((rows, pixels), jnp.bfloat16),
     )(*tables, inv_noise[None, :])

time: 139 us -> 146 us (1.050)
  Pallas kernels: 34.3 us -> 44.3 us
  other arithmetic: 33.8 us -> 31.6 us
  waiting for transfers between devices: 11 us -> 9.04 us
    pallas_call x1, Pallas kernels: 24.7 us -> 34.7 us  [weighted_rows(): pl.pallas_call(weights_kernel, grid=(rows // block,), in_specs=table_spec...]
    convert_element_type x3 -> x2, other arithmetic: 5 us -> 2.54 us  [split_pieces(): pieces.append(piece.astype(jnp.bfloat16))]
    mul x1 -> x2, other arithmetic: 0.62 us -> 2.6 us  [the longest x1 1.92 us: contrast_tables(): row_cos = jnp.pad(-AMPLITUDE * jnp.cos(row_angle), pad)]
    pad x0 -> x2, local copies, waits for them, and re-layouts: none -> 1.65 us  [the longest x1 0.83 us: contrast_tables(): row_sin = jnp.pad(-AMPLITUDE * jnp.sin(row_angle), pad)]
    concatenate x3 -> x2, other arithmetic: 3.09 us -> 1.44 us  [split_pieces(): joined = jnp.concatenate(pieces, axis=1)]
    sin x2 -> x1, other arithmetic: 3.34 us -> 1.9 us  [contrast_tables(): col_sin = jnp.sin(column_angle)]
  transfers between devices with their start and end apart: 5 -> 5, of which waited for: 2 -> 2; matrix products, arithmetic and copies ran while one was open for 45% -> 42% of each run, Pallas kernels for 25% -> 31%
where the time goes in v18:
time: 146 us; the launch traced here: 144 us
  Pallas kernels  44.3 us (30%)
  other arithmetic  31.6 us (22%)
  matrix products  22.1 us (15%)
  between operations  16.4 us (11%)
  local copies, waits for them, and re-layouts  16 us (11%)
  waiting for transfers between devices  9.04 us (6%)
  starting transfers between devices  4.99 us (3%)
    pallas_call x1, Pallas kernels, weighted_rows(): pl.pallas_call(weights_kernel, grid=(rows // block,), in_specs=table_spec...  34.7 us
    pallas_call x1, Pallas kernels, power_rows(): pl.pallas_call(expanded_power_kernel, grid=(rows // block,), in_specs=exp...  9.62 us
    dot_general x1, matrix products, on_device(): lax.dot_general(power_weight, power * jnp.bfloat16(-0.5), (((1,), (1,)),...  7.08 us
    dot_general x1, matrix products, on_device(): lax.dot_general(weighted, flat_images, (((1,), (1,)), ((), ())), preferre...  6.29 us
    ppermute x1, waiting for transfers between devices, on_device(): chip_sums = for_me + lax.ppermute(for_other, 'core', swap)  4.77 us
    dot_general x1, matrix products, on_device(): lax.dot_general(every_fact, picker, (((1,), (1,)), ((), ())), preferred_e...  4.71 us
    unnamed x11, local copies, waits for them, and re-layouts  4.61 us
    ppermute x2, starting transfers between devices, on_device(): best_score = jnp.maximum(best_score, lax.ppermute(best_score, 'cls', pairs))  4.41 us
  transfers between devices with their start and end apart: 5, of which 2 were waited for; matrix products, arithmetic and copies ran while one was open for 42% of the time, Pallas kernels for 31%

profile of v18, /device:TPU:0, one launch (start us, length us, event | category | flops | bytes accessed | tf_op | source)
XLA Modules:
  0.0 144.5 jit_solution(6919676695988685773)
XLA Ops:
  9.8 1.8 %pad_maximum_fusion.2 = bf16[24,9472]{1,0:T(8,128)(2,1)} fusion(bf16[24,256]{1,0:T(8,128)(2,1)S(1)} %reshape.248, bf16[24,9216]{1,0:T(8,128)(2,1)} %bitcast.31), kind=kLoop, calls=%fused_computation.45 | loop fusion | flops 909312 | bytes 909312 | tf_op jit(solution)/shard_map/concatenate | solution.py:191
  13.0 1.9 %fusion.20 = (f32[1024,72]{1,0:T(8,128)S(1)}, f32[1024,72]{1,0:T(8,128)S(1)}) fusion(f32[72]{0:T(128)S(1)} %multiply_multiply_fusion.1, f32[1024]{0:T(1024)S(1)} %get-tuple-element.28), kind=kLoop, calls=%fused_computation.39 | loop fusion | flops 221184 | bytes 594208 | tf_op jit(solution)/shard_map/mul | solution.py:35
  16.6 1.9 %fusion.21 = (f32[1024,64]{1,0:T(8,128)S(1)}, f32[1024,64]{1,0:T(8,128)S(1)}) fusion(f32[64]{0:T(128)S(1)} %multiply_multiply_fusion, f32[1024]{0:T(1024)S(1)} %get-tuple-element.28), kind=kLoop, calls=%fused_computation.43 | loop fusion | flops 131072 | bytes 528640 | tf_op jit(solution)/shard_map/sin | solution.py:37
  20.7 34.7 %shard_map.86 = (bf16[1024,9216]{1,0:T(8,128)(2,1)}, bf16[1024,4608]{1,0:T(8,128)(2,1)}, f32[96,9216]{1,0:T(8,128)}, f32[96,9216]{1,0:T(8,128)}) custom-call(f32[1024,128]{1,0:T(8,128)} %pad.18.row_sin_ref, f32[1024,128]{1,0:T(8,128)} %pad.19.row_cos_ref, f32[1024,128]{1,0:T(8,128)} %get-tuple-element.33.col_cos_ref, ...), custom_call_target="tpu_custom_call" | custom-call | tf_op jit(solution)/shard_map/pallas_call | solution.py:133
  57.1 4.8 %collective-permute-done.2 = f32[96,9216]{1,0:T(8,128)S(1)} collective-permute-done((f32[96,9216]{1,0:T(8,128)}, f32[96,9216]{1,0:T(8,128)S(1)}, u32[]{:S(2)}, u32[]{:S(2)}) %collective-permute-start.2) | collective-permute-done | bytes 3538976 | tf_op jit(solution)/shard_map/ppermute | solution.py:211
  61.9 4.1 %add.212 = f32[96,9216]{1,0:T(8,128)} add(f32[96,9216]{1,0:T(8,128)} %get-tuple-element.8, f32[96,9216]{1,0:T(8,128)S(1)} %collective-permute-done.2) | non-fusion elementwise | flops 884736 | bytes 10616832 | tf_op jit(solution)/shard_map/add | solution.py:211
  66.1 1.8 %gather_fusion = f32[192]{0:T(256)S(1)} fusion(f32[96]{0:T(128)S(1)} %divide_log_fusion, s32[1024]{0:T(1024)S(1)} %pad_clamp_fusion), kind=kCustom, calls=%fused_computation | custom fusion | bytes 2304 | tf_op jit(solution)/shard_map/jit(_take)/gather | solution.py:223
  68.5 2.3 %and_convert_fusion.expand_ref = bf16[256,4608]{1,0:T(8,128)(2,1)} fusion(s32[4608]{0:T(1024)S(1)} %add_select_fusion.1, s32[256]{0:T(256)S(1)} %and_select_fusion.1, pred[256]{0:T(512)(128)(4,1)S(1)} %iota_compare_fusion.7), kind=kLoop, calls=%fused_computation.4 | loop fusion | flops 3538944 | bytes 2379008 | tf_op jit(solution)/shard_map/convert_element_type | solution.py:96
  70.7 2.2 %slice.60 = bf16[8,24,9216]{2,1,0:T(8,128)(2,1)S(1)} slice(bf16[8,24,9472]{2,1,0:T(8,128)(2,1)} %bitcast.27), slice={[0:8], [0:24], [0:9216]} | slice | bytes 7077888 | tf_op jit(solution)/shard_map/slice | solution.py:195
  76.5 1.7 %reduce-window.9 = s32[64,128]{1,0:T(8,128)} reduce-window(s32[64,128]{1,0:T(8,128)} %reshape.257, s32[]{:T(128)} %constant.138.clone.1), window={size=1x128 pad=0_0x127_0}, to_apply=%region_3.4 | reduce-window | flops 1040384 | bytes 65540 | tf_op jit(solution)/shard_map/reduce-window
  78.2 1.4 slice.66
  79.7 1.4 reduce-window.12
  84.4 7.1 %fusion.3 = f32[1024,192]{0,1:T(8,128)S(1)} fusion(bf16[1024,4608]{1,0:T(8,128)(2,1)} %get-tuple-element.7, bf16[192,9216]{1,0:T(8,128)(2,1)S(1)} %bitcast.29), kind=kOutput, calls=%fused_computation.7 | convolution fusion | flops 1818132480 | bytes 13762560 | tf_op jit(solution)/shard_map/dot_general | solution.py:220
  91.5 2.1 %copy-done.2 = bf16[1024,9216]{1,0:T(8,128)(2,1)S(1)} copy-done((bf16[1024,9216]{1,0:T(8,128)(2,1)S(1)}, bf16[1024,9216]{1,0:T(8,128)(2,1)}, u32[]{:S(2)}) %copy-start.2) | copy-done | bytes 18874392
  93.6 6.3 %fusion.8 = f32[1024]{0:T(1024)S(1)} fusion(f32[1024,192]{0,1:T(8,128)S(1)} %fusion.3, bf16[1024,9216]{1,0:T(8,128)(2,1)S(1)} %copy-done.2, bf16[192,9216]{1,0:T(8,128)(2,1)S(1)} %bitcast.30, f32[192]{0:T(256)S(1)} %copy-done.1), kind=kOutput, calls=%fused_computation.12 | convolution fusion | flops 3624467456 | bytes 23204608 | tf_op jit(solution)/shard_map/dot_general | solution.py:218
  99.9 2.8 %collective-permute-start = (f32[1024]{0:T(1024)S(1)}, f32[1024]{0:T(1024)S(1)}, u32[]{:S(2)}, u32[]{:S(2)}) collective-permute-start(f32[1024]{0:T(1024)S(1)} %fusion.8), channel_id=1, source_target_pairs={{0,1},{1,0},{2,3},{3,2},{4,5},{5,4},{6,7},{7,6},{8,9},{9,8},{10,11... | collective-permute-start | bytes 12296 | tf_op jit(solution)/shard_map/ppermute | solution.py:228
  102.8 4.7 %fusion = f32[5,768]{1,0:T(8,128)S(1)} fusion(bf16[5,8192]{1,0:T(8,128)(2,1)S(1)} %bitcast.35, s32[8192]{0:T(1024)S(1)} %get-tuple-element.10), kind=kOutput, calls=%fused_computation.2 | convolution fusion | flops 69206016 | bytes 130048 | tf_op jit(solution)/shard_map/dot_general | solution.py:239
  108.2 1.4 fusion.33
  110.8 1.8 %reduce-precision_convert_fusion.1 = (bf16[768,72]{1,0:T(8,128)(2,1)S(1)}, bf16[768,72]{1,0:T(8,128)(2,1)S(1)}, bf16[768,72]{1,0:T(8,128)(2,1)S(1)}, bf16[768,72...) fusion(f32[768]{0:T(1024)S(1)} %select_multiply_fusion, f32[72]{0:T(128)S(1)} %multiply_multiply_fusion.1), kind=kLoop, calls=%fused_computation.31 | loop fusion | flops 1050624 | bytes 666912 | tf_op jit(solution)/shard_map/convert_element_type | solution.py:19
  114.8 9.6 %shard_map.87 = bf16[768,4608]{1,0:T(8,128)(2,1)} custom-call(bf16[768,256]{1,0:T(8,128)(2,1)} %get-tuple-element.35.row_sin_ref, bf16[768,256]{1,0:T(8,128)(2,1)} %get-tuple-element.36.row_cos_ref, bf16[256,4608]{1,0:T(8,128)(2,1)} %and_convert_fusion.expand_ref, f32[768,128]{1,0:T(8,128)} %get-tuple-element.37.col_cos_ref, ...), custom_call_target="tpu_custom_call" | custom-call | tf_op jit(solution)/shard_map/pallas_call | solution.py:159
  124.4 1.6 %collective-permute-start.1 = (f32[1024]{0:T(1024)S(1)}, f32[1024]{0:T(1024)S(1)}, u32[]{:S(2)}, u32[]{:S(2)}) collective-permute-start(f32[1024]{0:T(1024)S(1)} %max.10), channel_id=1, source_target_pairs={{0,2},{1,3},{2,0},{3,1},{4,6},{5,7},{6,4},{7,5},{8,10},{9,11},{10,... | collective-permute-start | bytes 12296 | tf_op jit(solution)/shard_map/ppermute | solution.py:228
  126.0 4.0 %fusion.35 = f32[24,4608]{1,0:T(8,128)S(1)} fusion(bf16[768,4608]{1,0:T(8,128)(2,1)} %shard_map.87, s32[768]{0:T(1024)S(1)} %fusion.55), kind=kOutput, calls=%fused_computation.63 | convolution fusion | flops 169887744 | bytes 7523328 | tf_op jit(solution)/shard_map/dot_general | solution.py:249
  130.6 4.2 %reduce-scatter.2.cloned.1.call-done = f32[24,9216]{1,0:T(8,128)} async-done(((f32[96,9216]{1,0:T(8,128)}), f32[24,9216]{1,0:T(8,128)}) %reduce-scatter.2.cloned.1.call-update) | async-done | bytes 884752 | tf_op jit(solution)/shard_map/reduce_scatter | solution.py:212
  134.8 2.2 %fusion.10 = f32[3,8,9216]{2,1,0:T(8,128)} fusion(f32[24,9216]{1,0:T(8,128)} %reduce-scatter.2.cloned.1.call-done, f32[24,4608]{1,0:T(8,128)S(1)} %fusion.35), kind=kLoop, calls=%fused_computation.15 | loop fusion | flops 663552 | bytes 2211840 | tf_op jit(solution)/shard_map/reshape | solution.py:252
  (59 shorter events, 20.1 us)
Async XLA Ops:
  8.0 62.7 %all-gather.3.cloned.1.call-start = ((), (), s32[]{:S(2)}) async-start(), calls=%async_computation.2 | async-start | bytes 4091904 | tf_op jit(solution)/shard_map/all_gather | solution.py:194
  11.6 123.2 %reduce-scatter.2.cloned.1.call-start = ((), (), s32[]{:S(2)}) async-start(), calls=%async_computation.1 | async-start | bytes 4423680 | tf_op jit(solution)/shard_map/reduce_scatter | solution.py:212
  20.7 35.2 %copy-start.3 = (s32[96]{0:T(128)S(1)}, s32[96]{0:T(128)}, u32[]{:S(2)}) copy-start(s32[96]{0:T(128)} %param.13) | copy-start | bytes 1156
  55.3 6.6 %collective-permute-start.2 = (f32[96,9216]{1,0:T(8,128)}, f32[96,9216]{1,0:T(8,128)S(1)}, u32[]{:S(2)}, u32[]{:S(2)}) collective-permute-start(f32[96,9216]{1,0:T(8,128)} %get-tuple-element.9), channel_id=1, source_target_pairs={{0,4},{4,0},{1,5},{5,1},{2,6},{6,2},{3,7},{7,3},{8,12},{12,8},{9,1... | collective-permute-start | bytes 10616840 | tf_op jit(solution)/shard_map/ppermute | solution.py:211
  73.9 0.6 copy-start
  84.4 7.1 %copy-start.1 = (f32[192]{0:T(256)S(1)}, f32[192]{0:T(256)}, u32[]{:S(2)}) copy-start(f32[192]{0:T(256)} %and_select_fusion.2) | copy-start | bytes 2308
  84.4 9.2 %copy-start.2 = (bf16[1024,9216]{1,0:T(8,128)(2,1)S(1)}, bf16[1024,9216]{1,0:T(8,128)(2,1)}, u32[]{:S(2)}) copy-start(bf16[1024,9216]{1,0:T(8,128)(2,1)} %get-tuple-element.6) | copy-start | bytes 56623108
  99.9 24.4 %collective-permute-start = (f32[1024]{0:T(1024)S(1)}, f32[1024]{0:T(1024)S(1)}, u32[]{:S(2)}, u32[]{:S(2)}) collective-permute-start(f32[1024]{0:T(1024)S(1)} %fusion.8), channel_id=1, source_target_pairs={{0,1},{1,0},{2,3},{3,2},{4,5},{5,4},{6,7},{7,6},{8,9},{9,8},{10,11... | collective-permute-start | bytes 12296 | tf_op jit(solution)/shard_map/ppermute | solution.py:228
  124.4 5.6 %collective-permute-start.1 = (f32[1024]{0:T(1024)S(1)}, f32[1024]{0:T(1024)S(1)}, u32[]{:S(2)}, u32[]{:S(2)}) collective-permute-start(f32[1024]{0:T(1024)S(1)} %max.10), channel_id=1, source_target_pairs={{0,2},{1,3},{2,0},{3,1},{4,6},{5,7},{6,4},{7,5},{8,10},{9,11},{10,... | collective-permute-start | bytes 12296 | tf_op jit(solution)/shard_map/ppermute | solution.py:228
Sparse Core Ops, SparseCore 0:
  11.7 45.0 all-gather.2
Sparse Core Ops, SparseCore 1:
  66.1 68.7 reduce-scatter.1
